TPU v7x, 128 devices: a whole 4x4x4 slice. The times are simulated.
128 devices in a mesh: seq: 16 (over z, y), tp: 8 (over x, core).
Axes of the slice: x: 4, y: 4, z: 4, core: 2. Of those that a mesh axis runs over, the one named last changes fastest.
Arguments:
- hidden: bfloat16 [128, 64, 2560], P(None, 'seq'), may hold values from -6 to 6
- gain_attn: bfloat16 [2560], replicated, may hold values from 0.099609375 to 1.8984375
- w_query: bfloat16 [2560, 2560], P(None, 'tp'), may hold values from -0.125 to 0.125
- w_key: bfloat16 [2560, 640], P(None, 'tp'), may hold values from -0.375 to 0.375
- w_value: bfloat16 [2560, 640], P(None, 'tp'), may hold values from -0.25 to 0.25
- w_out: bfloat16 [2560, 2560], P('tp'), may hold values from -0.125 to 0.125
- gain_ffn: bfloat16 [2560], replicated, may hold values from 0.099609375 to 1.8984375
- w_gate: bfloat16 [2560, 6912], P(None, 'tp'), may hold values from -0.125 to 0.125
- w_up: bfloat16 [2560, 6912], P(None, 'tp'), may hold values from -0.125 to 0.125
- w_down: bfloat16 [6912, 2560], P('tp'), may hold values from -0.078125 to 0.078125
- shared_pages: bfloat16 [320, 8, 2, 80, 128], P('seq', 'tp'), may hold values from -270 to 270
- leaf_pages: bfloat16 [512, 8, 2, 80, 128], P('seq', 'tp'), may hold values from -270 to 270
- root_table: int32 [4, 16], replicated, may hold values from 0 to 319, as said below
- mid_table: int32 [16, 16], replicated, may hold values from 0 to 319, as said below
- leaf_table: int32 [64, 8], replicated, may hold values from 0 to 511, as said below
- root_len: int32 [4], replicated, may hold values from 1024 to 2048, as said below
- mid_len: int32 [16], replicated, may hold values from 1 to 2048, as said below
- leaf_len: int32 [64], replicated, may hold values from 1 to 1024, as said below
- mid_parent: int32 [16], replicated, may hold values from 0 to 3
- leaf_parent: int32 [64], replicated, may hold values from 0 to 15
- slot_request: int32 [64], replicated, may hold values from 0 to 63, as said below
Outputs:
- layer_out: float32 [128, 64, 2560], P('tp', 'seq')
Inputs may be any that keep to these rules, and one draw needn't show every extreme that they name: `slot_request`: A permutation of the requests. The 4 requests of slots 4 * s to 4 * s + 3 have their leaves with 4 distinct owners (see leaf_table). `leaf_table`: all pages of one request's leaf lie with one owner, the index of seq equal to page // 32; each owner holds the leaves of exactly 4 requests, and every leaf page is named once. `root_table`: with mid_table, names every shared page exactly once. Shared page g is held by the index of seq g // 20; each index holds exactly 1 page of every root. `mid_table`: with root_table, names every shared page exactly once. Each index of seq holds exactly 1 page of every middle node. `root_len`: some root reaches the largest value. `mid_len`: some middle node reaches the largest value. `leaf_len`: some leaf reaches the largest value.
All inputs are finite; a program needn't handle non-finite values.
Results may differ from a plain program's by a relative error of at most 0.009.
The roundings to bfloat16 on the way count: a program that leaves them out, or rounds other values in their place, can miss the bound.
Values may be sent and summed in bfloat16 or wider, within the bound.
No kernel may reach another device: no remote copies, remote signals or barrier semaphores. Data moves between devices by JAX's collectives and lax.ppermute only.
A program may use at most 192 MiB of HBM per device.

v0:
```python
import jax
import jax.numpy as jnp
from jax import lax
from jax.sharding import PartitionSpec as P

QH = 32
KVH = 8
HD = 80
WINDOW = 4096


masked_score = -1e30
rope_base = 10000.0


def rms_norm(row_data, gain_vector):
    values = row_data.astype(jnp.float32)
    inverse_rms = lax.rsqrt(jnp.mean(values * values, -1, keepdims=True) + 1e-05)
    return (values * inverse_rms * gain_vector.astype(jnp.float32)).astype(jnp.bfloat16)


def rotate(vector, position):
    half_size = vector.shape[-1] // 2
    frequency = rope_base ** (-2.0 * jnp.arange(half_size, dtype=jnp.float32) / vector.shape[-1])
    angles = position.astype(jnp.float32)[..., None] * frequency
    cos_part = jnp.cos(angles)
    sin_part = jnp.sin(angles)
    first_half = vector[..., :half_size]
    second_half = vector[..., half_size:]
    return jnp.concatenate(
        [
            first_half * cos_part - second_half * sin_part,
            second_half * cos_part + first_half * sin_part,
        ],
        -1,
    )


def page_columns(pages):
    moved = jnp.moveaxis(pages, -5, -2)
    return moved.reshape(moved.shape[:-2] + (moved.shape[-2] * moved.shape[-1],))


def attend(queries, key_pack, key_pos, present, query_pos):
    scores = jnp.einsum(
        "nbkge,bket->nbkgt", queries, key_pack[:, :, 0], preferred_element_type=jnp.float32
    ) * queries.shape[-1] ** (-0.5)
    distance = query_pos[:, :, None] - key_pos[None, :, :]
    allowed = (present[None, :, :] & (distance >= 0) & (distance < WINDOW))[:, :, None, None, :]
    scores = jnp.where(allowed, scores, masked_score)
    maximum = jnp.max(scores, -1)
    weights = jnp.where(allowed, jnp.exp(scores - maximum[..., None]), 0.0)
    totals = jnp.sum(weights, -1)
    weighted = jnp.einsum(
        "nbkgt,bket->nbkge",
        weights.astype(jnp.bfloat16),
        key_pack[:, :, 1],
        preferred_element_type=jnp.float32,
    )
    return (weighted, maximum, totals)


def merge_parts(first, second):
    maximum = jnp.maximum(first[1], second[1])
    first_scale = jnp.exp(first[1] - maximum)
    second_scale = jnp.exp(second[1] - maximum)
    return (
        first[0] * first_scale[..., None] + second[0] * second_scale[..., None],
        maximum,
        first[2] * first_scale + second[2] * second_scale,
    )


def spans(request_ids, root_len, mid_len, leaf_len, mid_parent, leaf_parent):
    mid_nodes = leaf_parent[request_ids]
    root_nodes = mid_parent[mid_nodes]
    return (root_nodes, mid_nodes, root_len[root_nodes], mid_len[mid_nodes], leaf_len[request_ids])


def shards(
    hidden,
    gain_attn,
    w_query,
    w_key,
    w_value,
    w_out,
    gain_ffn,
    w_gate,
    w_up,
    w_down,
    shared_pages,
    leaf_pages,
    root_table,
    mid_table,
    leaf_table,
    root_len,
    mid_len,
    leaf_len,
    mid_parent,
    leaf_parent,
    slot_request,
):
    new_rows, local_reqs, model_width = hidden.shape
    seq_count = lax.axis_size("seq")
    seq_index = lax.axis_index("seq")
    kv_local = leaf_pages.shape[1]
    group_size = QH // KVH
    pages_here = leaf_pages.shape[0]
    slot_ids = seq_index * local_reqs + jnp.arange(local_reqs, dtype=jnp.int32)
    requests = slot_request[slot_ids]
    root_nodes, mid_nodes, root_span, mid_span, leaf_span = spans(
        requests, root_len, mid_len, leaf_len, mid_parent, leaf_parent
    )
    context = root_span + mid_span + leaf_span
    new_index = jnp.arange(new_rows, dtype=jnp.int32)
    query_pos = context[None, :] + new_index[:, None]
    all_slots = slot_request.reshape(seq_count, local_reqs)
    page_store = lax.all_gather(shared_pages, "seq", axis=0, tiled=True)
    root_index = root_table[root_nodes]
    mid_index = mid_table[mid_nodes]
    normed = rms_norm(hidden, gain_attn).reshape(-1, model_width)
    query_proj = jnp.dot(normed, w_query, preferred_element_type=jnp.float32).reshape(
        new_rows, local_reqs, -1, HD
    )
    queries = (
        rotate(query_proj, query_pos[:, :, None])
        .astype(jnp.bfloat16)
        .reshape(new_rows, local_reqs, kv_local, group_size, HD)
    )
    key_proj = jnp.dot(normed, w_key, preferred_element_type=jnp.float32).reshape(
        new_rows, local_reqs, kv_local, HD
    )
    new_keys = rotate(key_proj, query_pos[:, :, None]).astype(jnp.bfloat16)
    new_values = (
        jnp.dot(normed, w_value, preferred_element_type=jnp.float32)
        .astype(jnp.bfloat16)
        .reshape(new_rows, local_reqs, kv_local, HD)
    )
    home_of = leaf_table[:, 0] // pages_here
    own_homes = home_of[requests]
    sender_match = home_of[all_slots] == seq_index
    sender_pick = jnp.argmax(sender_match, 1)
    sender_have = jnp.any(sender_match, 1)
    picked_request = jnp.take_along_axis(all_slots, sender_pick[:, None], 1)[:, 0]
    page_ids = jnp.where(
        sender_have[:, None], leaf_table[picked_request] - seq_index * pages_here, 0
    )
    leaf_steps = jnp.arange(leaf_table.shape[1] * leaf_pages.shape[-1], dtype=jnp.int32)
    fresh_pack = jnp.stack(
        [jnp.transpose(new_keys, (1, 2, 3, 0)), jnp.transpose(new_values, (1, 2, 3, 0))], 2
    )
    fresh_part = attend(
        queries,
        fresh_pack,
        context[:, None] + new_index[None, :],
        jnp.ones((local_reqs, new_rows), bool),
        query_pos,
    )
    outgoing = jnp.where(
        sender_have[:, None, None, None, None, None], jnp.take(leaf_pages, page_ids, axis=0), 0
    )
    arrived = lax.all_to_all(outgoing, "seq", split_axis=0, concat_axis=0, tiled=True)
    leaf_pack = page_columns(jnp.take(arrived, own_homes, axis=0))
    leaf_pos = (root_span + mid_span)[:, None] + leaf_steps[None, :]
    leaf_part = attend(
        queries, leaf_pack, leaf_pos, leaf_steps[None, :] < leaf_span[:, None], query_pos
    )
    root_pack = page_columns(jnp.take(page_store, root_index, axis=0))
    root_steps = jnp.arange(root_pack.shape[-1], dtype=jnp.int32)
    root_part = attend(
        queries,
        root_pack,
        root_steps[None, :] + 0 * root_span[:, None],
        root_steps[None, :] < root_span[:, None],
        query_pos,
    )
    mid_pack = page_columns(jnp.take(page_store, mid_index, axis=0))
    mid_steps = jnp.arange(mid_pack.shape[-1], dtype=jnp.int32)
    mid_part = attend(
        queries,
        mid_pack,
        root_span[:, None] + mid_steps[None, :],
        mid_steps[None, :] < mid_span[:, None],
        query_pos,
    )
    combined = merge_parts(merge_parts(root_part, mid_part), merge_parts(leaf_part, fresh_part))
    attended = (
        (combined[0] / combined[2][..., None])
        .astype(jnp.bfloat16)
        .reshape(new_rows * local_reqs, -1)
    )
    attn_proj = lax.psum(jnp.dot(attended, w_out, preferred_element_type=jnp.float32), "tp")
    resid = hidden.astype(jnp.float32) + attn_proj.reshape(new_rows, local_reqs, model_width)
    normed_ffn = rms_norm(resid, gain_ffn).reshape(-1, model_width)
    gate_rows = jnp.dot(normed_ffn, w_gate, preferred_element_type=jnp.float32)
    up_rows = jnp.dot(normed_ffn, w_up, preferred_element_type=jnp.float32)
    activated = (
        (jax.nn.silu(gate_rows) * up_rows).astype(jnp.bfloat16).reshape(new_rows, local_reqs, -1)
    )
    own_count = new_rows // lax.axis_size("tp")
    ffn_proj = lax.psum_scatter(
        jnp.dot(
            activated.reshape(-1, activated.shape[-1]), w_down, preferred_element_type=jnp.float32
        ).reshape(own_count * lax.axis_size("tp"), local_reqs, model_width),
        "tp",
        scatter_dimension=0,
        tiled=True,
    )
    own_rows = lax.dynamic_slice_in_dim(resid, lax.axis_index("tp") * own_count, own_count, 0)
    return own_rows + ffn_proj


def solution(mesh):
    return jax.shard_map(
        shards,
        mesh=mesh,
        in_specs=(
            P(None, "seq", None),
            P(),
            P(None, "tp"),
            P(None, "tp"),
            P(None, "tp"),
            P("tp", None),
            P(),
            P(None, "tp"),
            P(None, "tp"),
            P("tp", None),
            P("seq", "tp", None, None, None),
            P("seq", "tp", None, None, None),
            P(),
            P(),
            P(),
            P(),
            P(),
            P(),
            P(),
            P(),
            P(),
        ),
        out_specs=P("tp", "seq", None),
        check_vma=False,
    )
```

profile of v0, /device:TPU:0, one launch (start us, length us, event | category | flops | bytes accessed | tf_op | source)
XLA Modules:
  0.0 450.8 jit_solution(16612270365806220123)
XLA Ops:
  13.6 3.6 gather_fusion.11
  17.2 5.5 %select_select_fusion = bf16[16,8,1,2,80,128]{5,4,3,1,2,0:T(8,128)(2,1)} fusion(bf16[16,8,1,2,80,128]{5,4,3,1,2,0:T(8,128)(2,1)} %bitcast.320, pred[16]{0:T(512)(128)(4,1)S(1)} %reduce_or.9, pred[16,8]{1,0:T(8,128)(4,1)S(1)} %get-tuple-element.17), kind=kLoop, calls=%fused_computation.47 | loop fusion | flops 5242880 | bytes 10485904 | tf_op jit(solution)/shard_map/jit(_where)/select_n | solution.py:159
  22.7 8.3 %all-to-all-start = ((bf16[16,8,1,2,80,128]{5,4,3,1,2,0:T(8,128)(2,1)}), bf16[16,8,1,2,80,128]{5,4,3,1,2,0:T(8,128)(2,1)}, u32[]{:S(2)}, u32[]{:S(2)}) async-start(bf16[16,8,1,2,80,128]{5,4,3,1,2,0:T(8,128)(2,1)} %select_select_fusion), calls=%async_computation | async-start | bytes 10485760 | tf_op jit(solution)/shard_map/all_to_all | solution.py:162
  37.0 3.3 fusion.17
  40.4 3.0 fusion.19
  43.4 5.8 %reshape.793 = bf16[512,2560]{1,0:T(8,128)(2,1)} reshape(bf16[128,4,2560]{2,1,0:T(4,128)(2,1)} %fusion.19) | data formatting | bytes 5242880 | tf_op jit(solution)/shard_map/reshape | solution.py:121
  55.0 2.8 fusion.73
  65.9 5.5 %fusion.26 = (pred[128,4,2048]{0,2,1:T(8,128)(4,1)}, pred[128,4,2048]{0,2,1:T(8,128)(4,1)}) fusion(s32[128,4]{0,1:T(4,128)S(1)} %get-tuple-element.29, pred[4,2048]{1,0:T(4,128)(4,1)S(1)} %iota_compare_fusion.1, s32[4,2048]{1,0:T(4,128)S(1)} %iota_add_fusion, pred[4,2048]{1,0:T(4,128)(4,1)S(1)} %iota_compare_fusion), kind=kLoop, calls=%fused_computation.54 | loop fusion | flops 10485760 | bytes 2148352 | tf_op jit(solution)/shard_map/and | solution.py:49
  71.4 56.5 %all-to-all-done = bf16[16,8,1,2,80,128]{5,4,3,1,2,0:T(8,128)(2,1)} async-done(((bf16[16,8,1,2,80,128]{5,4,3,1,2,0:T(8,128)(2,1)}), bf16[16,8,1,2,80,128]{5,4,3,1,2,0:T(8,128)(2,1)}, u32[]{:S(2)}, u32[]{:S(2)}) %all-to-all-start) | async-done | bytes 5242912 | tf_op jit(solution)/shard_map/all_to_all | solution.py:162
  127.9 3.4 gather_fusion.12
  136.7 3.2 copy-done.11
  142.7 15.5 %all-gather.2.cloned.1.call-done = bf16[320,1,2,80,128]{4,3,2,1,0:T(8,128)(2,1)} async-done(((bf16[20,1,2,80,128]{4,3,2,1,0:T(8,128)(2,1)}), bf16[320,1,2,80,128]{4,3,2,1,0:T(8,128)(2,1)}) %all-gather.2.cloned.1.call-update) | async-done | bytes 13107216 | tf_op jit(solution)/shard_map/all_gather | solution.py:118
  158.2 7.1 %gather_fusion.15 = bf16[64,2,80,128]{3,2,1,0:T(8,128)(2,1)} fusion(bf16[320,2,80,128]{3,2,1,0:T(8,128)(2,1)} %bitcast.326, s32[1024]{0:T(1024)S(1)} %copy-done.31), kind=kCustom, calls=%fused_computation.1.clone | custom fusion | bytes 5243136 | tf_op jit(solution)/shard_map/jit(_take)/gather | solution.py:177
  165.3 7.2 %gather_fusion.14 = bf16[64,2,80,128]{3,2,1,0:T(8,128)(2,1)} fusion(bf16[320,2,80,128]{3,2,1,0:T(8,128)(2,1)} %bitcast.327, s32[1024]{0:T(1024)S(1)} %copy-done.30), kind=kCustom, calls=%fused_computation.clone | custom fusion | bytes 5243136 | tf_op jit(solution)/shard_map/jit(_take)/gather | solution.py:168
  172.5 4.2 fusion.35
  176.6 5.2 %reshape.777 = bf16[4,1,2,80,2048]{4,3,0,2,1:T(8,128)(2,1)} reshape(bf16[4,1,2,80,16,128]{5,4,3,0,2,1:T(8,128)(2,1)} %fusion.35) | data formatting | bytes 5242880 | tf_op jit(solution)/shard_map/reshape | solution.py:41
  181.8 4.3 fusion.34
  186.1 5.2 %reshape.781 = bf16[4,1,2,80,2048]{4,3,0,2,1:T(8,128)(2,1)} reshape(bf16[4,1,2,80,16,128]{5,4,3,0,2,1:T(8,128)(2,1)} %fusion.34) | data formatting | bytes 5242880 | tf_op jit(solution)/shard_map/reshape | solution.py:41
  191.3 8.8 %fusion.1 = (f32[128,4,4]{0,2,1:T(4,128)S(1)}, f32[4,2048,128,4]{2,1,3,0:T(8,128)}) fusion(pred[128,4,2048]{0,2,1:T(8,128)(4,1)S(1)} %copy-done.13, bf16[128,4,4,40]{0,3,2,1:T(8,128)(2,1)S(1)} %copy-done.24, bf16[128,4,4,40]{0,3,2,1:T(8,128)(2,1)S(1)} %copy-done.22, bf16[4,1,2,80,2048]{4,3,0,2,1:T(8,128)(2,1)} %reshape.781), kind=kOutput, calls=%fused_computation.21 | convolution fusion | flops 684324864 | bytes 19472384 | tf_op jit(solution)/shard_map/nbkge,bket->nbkgt/dot_general | solution.py:45
  202.9 10.7 %fusion.2 = (f32[128,4,4]{0,2,1:T(4,128)S(1)}, f32[128,4,4]{0,2,1:T(4,128)S(1)}) fusion(f32[4,2048,128,4]{2,1,3,0:T(8,128)S(1)} %get-tuple-element.38, f32[128,4,4]{0,2,1:T(4,128)S(1)} %get-tuple-element.37, pred[128,4,2048]{0,2,1:T(8,128)(4,1)S(1)} %copy-done.12, f32[128,4,4]{0,2,1:T(4,128)S(1)} %get-tuple-element.31, ...), kind=kLoop, calls=%fused_computation.22 | loop fusion | flops 41938944 | bytes 35684352 | tf_op jit(solution)/shard_map/reduce_sum | solution.py:53
  213.8 3.0 fusion.56
  216.7 10.7 %fusion.68 = f32[128,4,1,4,80]{0,4,3,1,2:T(8,128)} fusion(f32[4,2048,128,4]{2,1,3,0:T(8,128)} %get-tuple-element.32, f32[128,4,4]{0,2,1:T(4,128)S(1)} %get-tuple-element.31, pred[128,4,2048]{0,2,1:T(8,128)(4,1)S(1)} %copy-done.13, bf16[4,1,2,80,2048]{4,3,0,2,1:T(8,128)(2,1)} %reshape.781, f32[128,4,4]{0,2,1:T(4,128)S(1)} %bitcast.342), kind=kOutput, calls=%fused_computation.94 | convolution fusion | flops 692224000 | bytes 19808256 | tf_op jit(solution)/shard_map/nbkgt,bket->nbkge/dot_general | solution.py:54
  227.4 5.8 %fusion.65 = f32[128,4,1,4,80]{0,4,3,1,2:T(8,128)} fusion(f32[128,4,1,4,80]{0,4,3,1,2:T(8,128)} %fusion.68, f32[4,2048,128,4]{2,1,3,0:T(8,128)S(1)} %get-tuple-element.38, f32[128,4,4]{0,2,1:T(4,128)S(1)} %get-tuple-element.37, pred[128,4,2048]{0,2,1:T(8,128)(4,1)S(1)} %copy-done.12, bf16[4,1,2,80,2048]{4,3,0,2,1:T(8,128)(2,1)} %reshape.777, ...), kind=kOutput, calls=%fused_computation.93 | convolution fusion | flops 692551680 | bytes 20471808 | tf_op jit(solution)/shard_map/nbkgt,bket->nbkge/dot_general | solution.py:54
  235.7 3.9 fusion.123
  239.6 7.1 %reshape.798 = f32[128,4,2560]{2,1,0:T(4,128)} reshape(f32[512,2560]{1,0:T(8,128)} %fusion.123) | data formatting | bytes 10485760 | tf_op jit(solution)/shard_map/reshape | solution.py:193
  247.4 77.0 %all-reduce.4.cloned.1.call-done = f32[128,4,2560]{2,1,0:T(4,128)} async-done(((f32[128,4,2560]{2,1,0:T(4,128)}), f32[128,4,2560]{2,1,0:T(4,128)}) %all-reduce.4.cloned.1.call-update) | async-done | bytes 5242896 | tf_op jit(solution)/shard_map/psum | solution.py:192
  324.4 5.1 %multiply_reduce_fusion = (f32[128,4]{1,0:T(8,128)S(1)}, f32[128,4,2560]{2,1,0:T(4,128)S(1)}) fusion(f32[128,4,2560]{2,1,0:T(4,128)} %all-reduce.4.cloned.1.call-done, bf16[128,4,2560]{2,1,0:T(4,128)(2,1)} %param.23), kind=kLoop, calls=%fused_computation.46 | loop fusion | flops 5242368 | bytes 13109248 | tf_op jit(solution)/shard_map/reduce_sum | solution.py:18
  334.6 5.6 %reshape.799 = bf16[512,2560]{1,0:T(8,128)(2,1)} reshape(bf16[128,4,2560]{2,1,0:T(4,128)(2,1)} %multiply_convert_fusion) | data formatting | bytes 5242880 | tf_op jit(solution)/shard_map/reshape | solution.py:194
  340.2 5.5 %fusion.124 = f32[512,864]{0,1:T(8,128)S(1)} fusion(bf16[512,2560]{1,0:T(8,128)(2,1)} %reshape.799, bf16[2560,864]{0,1:T(8,128)(2,1)} %param.30), kind=kOutput, calls=%fused_computation.214 | convolution fusion | flops 2264924160 | bytes 8814592 | tf_op jit(solution)/shard_map/dot_general | solution.py:195
  345.7 12.0 %fusion.78 = f32[512,2560]{1,0:T(8,128)} fusion(bf16[864,2560]{1,0:T(8,128)(2,1)} %param.32, f32[512,864]{0,1:T(8,128)S(1)} %fusion.124, bf16[512,2560]{1,0:T(8,128)(2,1)} %reshape.799, bf16[2560,864]{0,1:T(8,128)(2,1)} %param.31), kind=kOutput, calls=%fused_computation.102 | convolution fusion | flops 4532502528 | bytes 18481152 | tf_op jit(solution)/shard_map/dot_general | solution.py:202
  357.7 7.1 %reshape.800 = f32[128,4,2560]{2,1,0:T(4,128)} reshape(f32[512,2560]{1,0:T(8,128)} %fusion.78) | data formatting | bytes 10485760 | tf_op jit(solution)/shard_map/reshape | solution.py:204
  366.7 75.0 %all-reduce.6.cloned.1.call-done = f32[128,4,2560]{2,1,0:T(4,128)} async-done(((f32[128,4,2560]{2,1,0:T(4,128)}), f32[128,4,2560]{2,1,0:T(4,128)}) %all-reduce.6.cloned.1.call-update) | async-done | bytes 5242896
  (179 shorter events, 49.3 us)
Async XLA Ops:
  6.5 229.2 %copy-start = (bf16[320,2560]{1,0:T(8,128)(2,1)S(1)}, bf16[320,2560]{1,0:T(8,128)(2,1)}, u32[]{:S(2)}) copy-start(bf16[320,2560]{1,0:T(8,128)(2,1)} %param.28) | copy-start | bytes 4915204
  6.5 151.7 %all-gather.2.cloned.1.call-start = ((), (), s32[]{:S(2)}) async-start(), calls=%async_computation.1 | async-start | bytes 13926400 | tf_op jit(solution)/shard_map/all_gather | solution.py:118
  22.7 8.5 %copy-start.1 = (s32[64]{0:T(128)S(1)}, s32[64]{0:T(128)}, u32[]{:S(2)}) copy-start(s32[64]{0:T(128)} %param.43) | copy-start | bytes 772
  22.7 9.8 %copy-start.2 = (s32[64]{0:T(128)S(1)}, s32[64]{0:T(128)}, u32[]{:S(2)}) copy-start(s32[64]{0:T(128)} %param.40) | copy-start | bytes 772
  22.7 10.4 %copy-start.3 = (s32[64]{0:T(128)S(1)}, s32[64]{0:T(128)}, u32[]{:S(2)}) copy-start(s32[64]{0:T(128)} %param.42) | copy-start | bytes 772
  22.7 11.1 %copy-start.4 = (s32[16]{0:T(128)S(1)}, s32[16]{0:T(128)}, u32[]{:S(2)}) copy-start(s32[16]{0:T(128)} %param.39) | copy-start | bytes 196
  22.7 11.7 %copy-start.5 = (s32[16]{0:T(128)S(1)}, s32[16]{0:T(128)}, u32[]{:S(2)}) copy-start(s32[16]{0:T(128)} %param.41) | copy-start | bytes 196
  22.7 12.4 %copy-start.26 = (s32[16,16]{1,0:T(8,128)S(1)}, s32[16,16]{1,0:T(8,128)}, u32[]{:S(2)}) copy-start(s32[16,16]{1,0:T(8,128)} %param.36) | copy-start | bytes 3076
  22.7 13.0 %copy-start.6 = (s32[4]{0:T(128)S(1)}, s32[4]{0:T(128)}, u32[]{:S(2)}) copy-start(s32[4]{0:T(128)} %param.38) | copy-start | bytes 52
  22.7 13.7 %copy-start.25 = (s32[4,16]{1,0:T(4,128)S(1)}, s32[4,16]{1,0:T(4,128)}, u32[]{:S(2)}) copy-start(s32[4,16]{1,0:T(4,128)} %param.35) | copy-start | bytes 772
  22.7 14.3 %copy-start.32 = (bf16[2560]{0:T(1024)(128)(2,1)S(1)}, bf16[2560]{0:T(1024)(128)(2,1)}, u32[]{:S(2)}) copy-start(bf16[2560]{0:T(1024)(128)(2,1)} %param.24) | copy-start | bytes 15364
  22.7 105.2 %all-to-all-start = ((bf16[16,8,1,2,80,128]{5,4,3,1,2,0:T(8,128)(2,1)}), bf16[16,8,1,2,80,128]{5,4,3,1,2,0:T(8,128)(2,1)}, u32[]{:S(2)}, u32[]{:S(2)}) async-start(bf16[16,8,1,2,80,128]{5,4,3,1,2,0:T(8,128)(2,1)} %select_select_fusion), calls=%async_computation | async-start | bytes 10485760 | tf_op jit(solution)/shard_map/all_to_all | solution.py:162
  31.1 293.4 %all-reduce.4.cloned.1.call-start = ((), (), s32[]{:S(2)}) async-start(), calls=%async_computation.2 | async-start | bytes 10485760 | tf_op jit(solution)/shard_map/psum | solution.py:192
  40.4 8.9 %copy-start.20 = (bf16[2560,80]{0,1:T(8,128)(2,1)S(1)}, bf16[2560,80]{0,1:T(8,128)(2,1)}, u32[]{:S(2)}) copy-start(bf16[2560,80]{0,1:T(8,128)(2,1)} %param.27) | copy-start | bytes 1228804
  43.4 11.6 %copy-start.37 = (bf16[2560,80]{0,1:T(8,128)(2,1)S(1)}, bf16[2560,80]{0,1:T(8,128)(2,1)}, u32[]{:S(2)}) copy-start(bf16[2560,80]{0,1:T(8,128)(2,1)} %param.26) | copy-start | bytes 1228804
  65.7 71.0 %copy-start.15 = (pred[128,4,1024]{0,2,1:T(8,128)(4,1)}, pred[128,4,1024]{0,2,1:T(8,128)(4,1)S(1)}, u32[]{:S(2)}) copy-start(pred[128,4,1024]{0,2,1:T(8,128)(4,1)S(1)} %fusion.37) | copy-start | bytes 1572868
  140.0 18.2 %copy-start.31 = (s32[1024]{0:T(1024)S(1)}, s32[1024]{0:T(1024)}, u32[]{:S(2)}) copy-start(s32[1024]{0:T(1024)} %pad_clamp_fusion.4) | copy-start | bytes 12292
  142.7 22.6 %copy-start.30 = (s32[1024]{0:T(1024)S(1)}, s32[1024]{0:T(1024)}, u32[]{:S(2)}) copy-start(s32[1024]{0:T(1024)} %pad_clamp_fusion.5) | copy-start | bytes 12292
  158.2 14.3 %copy-start.35 = (pred[4,16]{1,0:T(4,128)(4,1)S(1)}, pred[4,16]{1,0:T(4,128)(4,1)}, u32[]{:S(2)}) copy-start(pred[4,16]{1,0:T(4,128)(4,1)} %compare_and_fusion.2) | copy-start | bytes 196
  172.5 9.4 %copy-start.34 = (pred[4,16]{1,0:T(4,128)(4,1)S(1)}, pred[4,16]{1,0:T(4,128)(4,1)}, u32[]{:S(2)}) copy-start(pred[4,16]{1,0:T(4,128)(4,1)} %compare_and_fusion.1) | copy-start | bytes 196
  181.8 9.5 %copy-start.13 = (pred[128,4,2048]{0,2,1:T(8,128)(4,1)S(1)}, pred[128,4,2048]{0,2,1:T(8,128)(4,1)}, u32[]{:S(2)}) copy-start(pred[128,4,2048]{0,2,1:T(8,128)(4,1)} %get-tuple-element.28) | copy-start | bytes 3145732
  181.8 9.5 %copy-start.22 = (bf16[128,4,4,40]{0,3,2,1:T(8,128)(2,1)S(1)}, bf16[128,4,4,40]{0,3,2,1:T(8,128)(2,1)}, u32[]{:S(2)}) copy-start(bf16[128,4,4,40]{0,3,2,1:T(8,128)(2,1)} %copy-done.21) | copy-start | bytes 491524
  181.8 9.5 %copy-start.24 = (bf16[128,4,4,40]{0,3,2,1:T(8,128)(2,1)S(1)}, bf16[128,4,4,40]{0,3,2,1:T(8,128)(2,1)}, u32[]{:S(2)}) copy-start(bf16[128,4,4,40]{0,3,2,1:T(8,128)(2,1)} %copy-done.23) | copy-start | bytes 491524
  191.3 8.8 %copy-start.12 = (pred[128,4,2048]{0,2,1:T(8,128)(4,1)S(1)}, pred[128,4,2048]{0,2,1:T(8,128)(4,1)}, u32[]{:S(2)}) copy-start(pred[128,4,2048]{0,2,1:T(8,128)(4,1)} %get-tuple-element.27) | copy-start | bytes 3145732
  191.3 8.8 %copy-start.14 = (bf16[4,1,2,80,2048]{4,3,0,2,1:T(8,128)(2,1)S(1)}, bf16[4,1,2,80,2048]{4,3,0,2,1:T(8,128)(2,1)}, u32[]{:S(2)}) copy-start(bf16[4,1,2,80,2048]{4,3,0,2,1:T(8,128)(2,1)} %reshape.777) | copy-start | bytes 7864324
  200.1 13.6 %slice-start = ((s8[8388608]{0:T(1024)(128)(4,1)}), s8[4194304]{0:T(1024)(128)(4,1)S(1)}, s32[]{:S(2)}) async-start(s8[8388608]{0:T(1024)(128)(4,1)} %bitcast.324), calls=%async_computation.4 | async-start | bytes 8388608
  202.9 10.8 %copy-start.28 = (f32[128,4,4]{0,2,1:T(4,128)S(1)}, f32[128,4,4]{0,2,1:T(4,128)}, u32[]{:S(2)}) copy-start(f32[128,4,4]{0,2,1:T(4,128)} %copy-done.27) | copy-start | bytes 24580
  202.9 10.8 %copy-start.29 = (f32[128,4,4]{0,2,1:T(4,128)S(1)}, f32[128,4,4]{0,2,1:T(4,128)}, u32[]{:S(2)}) copy-start(f32[128,4,4]{0,2,1:T(4,128)} %fusion.15) | copy-start | bytes 24580
  202.9 10.8 %slice-start.1 = ((s8[8388608]{0:T(1024)(128)(4,1)}), s8[4194304]{0:T(1024)(128)(4,1)S(1)}, s32[]{:S(2)}) async-start(s8[8388608]{0:T(1024)(128)(4,1)} %bitcast.324), calls=%async_computation.5 | async-start | bytes 8388608
  202.9 10.8 %copy-start.16 = (pred[128,4,1024]{0,2,1:T(8,128)(4,1)S(1)}, pred[128,4,1024]{0,2,1:T(8,128)(4,1)}, u32[]{:S(2)}) copy-start(pred[128,4,1024]{0,2,1:T(8,128)(4,1)} %copy-done.15) | copy-start | bytes 1572868
  202.9 10.8 %copy-start.17 = (bf16[4,1,2,80,1024]{4,3,0,2,1:T(8,128)(2,1)S(1)}, bf16[4,1,2,80,1024]{4,3,0,2,1:T(8,128)(2,1)}, u32[]{:S(2)}) copy-start(bf16[4,1,2,80,1024]{4,3,0,2,1:T(8,128)(2,1)} %reshape.788) | copy-start | bytes 3932164
  246.8 195.0 %all-reduce.6.cloned.1.call-start = ((), (), s32[]{:S(2)}) async-start(), calls=%async_computation.3 | async-start | bytes 10485760
  (13 other events, 36.5 us)
Sparse Core Ops, SparseCore 0:
  9.5 148.6 all-gather.1
  246.9 77.5 all-reduce.3
  365.0 76.6 all-reduce.5
where the time goes:
time: 457 us; the launch traced here: 451 us
  waiting for transfers between devices  225 us (49%)
  local copies, waits for them, and re-layouts  79.5 us (17%)
  matrix products  63.6 us (14%)
  other arithmetic  60 us (13%)
  between operations  14.6 us (3%)
  starting transfers between devices  8.4 us (2%)
    psum x1, waiting for transfers between devices, shards(): lax.psum(jnp.dot(attended, w_out, preferred_element_type=jnp.float32), 'tp')  77 us
    unnamed x4, waiting for transfers between devices  75.7 us
    all_to_all x1, waiting for transfers between devices, shards(): lax.all_to_all(outgoing, 'seq', split_axis=0, concat_axis=0, tiled=True)  56.5 us
    dot_general x4, matrix products, attend(): jnp.einsum('nbkgt,bket->nbkge', weights.astype(jnp.bfloat16), key_pack[:,...  21.1 us
    all_gather x1, waiting for transfers between devices, shards(): page_store = lax.all_gather(shared_pages, 'seq', axis=0, tiled=True)  15.5 us
    dot_general x4, matrix products, attend(): jnp.einsum('nbkge,bket->nbkgt', queries, key_pack[:, :, 0], preferred_ele...  14.4 us
    reduce_sum x3, other arithmetic, attend(): totals = jnp.sum(weights, -1)  13.6 us
    dot_general x1, matrix products, shards(): jnp.dot(activated.reshape(-1, activated.shape[-1]), w_down, preferred_ele...  12 us
  transfers between devices with their start and end apart: 4, of which 4 were waited for; matrix products, arithmetic and copies ran while one was open for 15% of the time, Pallas kernels for 0%

commit v1 on v0

--- a/solution.py
+++ b/solution.py
@@ -189,25 +189,28 @@
         .astype(jnp.bfloat16)
         .reshape(new_rows * local_reqs, -1)
     )
-    attn_proj = lax.psum(jnp.dot(attended, w_out, preferred_element_type=jnp.float32), "tp")
-    resid = hidden.astype(jnp.float32) + attn_proj.reshape(new_rows, local_reqs, model_width)
-    normed_ffn = rms_norm(resid, gain_ffn).reshape(-1, model_width)
-    gate_rows = jnp.dot(normed_ffn, w_gate, preferred_element_type=jnp.float32)
-    up_rows = jnp.dot(normed_ffn, w_up, preferred_element_type=jnp.float32)
-    activated = (
-        (jax.nn.silu(gate_rows) * up_rows).astype(jnp.bfloat16).reshape(new_rows, local_reqs, -1)
-    )
-    own_count = new_rows // lax.axis_size("tp")
-    ffn_proj = lax.psum_scatter(
-        jnp.dot(
-            activated.reshape(-1, activated.shape[-1]), w_down, preferred_element_type=jnp.float32
-        ).reshape(own_count * lax.axis_size("tp"), local_reqs, model_width),
+    tp_count = lax.axis_size("tp")
+    own_count = new_rows // tp_count
+    attn_proj = lax.psum_scatter(
+        jnp.dot(attended, w_out, preferred_element_type=jnp.float32),
         "tp",
         scatter_dimension=0,
         tiled=True,
-    )
-    own_rows = lax.dynamic_slice_in_dim(resid, lax.axis_index("tp") * own_count, own_count, 0)
-    return own_rows + ffn_proj
+    ).reshape(own_count, local_reqs, model_width)
+    own_hidden = lax.dynamic_slice_in_dim(hidden, lax.axis_index("tp") * own_count, own_count, 0)
+    resid = own_hidden.astype(jnp.float32) + attn_proj
+    normed_own = rms_norm(resid, gain_ffn).reshape(-1, model_width)
+    normed_ffn = lax.all_gather(normed_own, "tp", axis=0, tiled=True)
+    gate_rows = jnp.dot(normed_ffn, w_gate, preferred_element_type=jnp.float32)
+    up_rows = jnp.dot(normed_ffn, w_up, preferred_element_type=jnp.float32)
+    activated = (jax.nn.silu(gate_rows) * up_rows).astype(jnp.bfloat16)
+    ffn_proj = lax.psum_scatter(
+        jnp.dot(activated, w_down, preferred_element_type=jnp.float32),
+        "tp",
+        scatter_dimension=0,
+        tiled=True,
+    ).reshape(own_count, local_reqs, model_width)
+    return resid + ffn_proj
 
 
 def solution(mesh):

time: 457 us -> 387 us (0.85)
  waiting for transfers between devices: 225 us -> 179 us
  local copies, waits for them, and re-layouts: 79.5 us -> 59.5 us
  other arithmetic: 60 us -> 54.4 us
    reduce_scatter x0 -> x2, waiting for transfers between devices: none -> 81 us  [the longest x1 40.6 us: shards(): lax.psum_scatter(jnp.dot(activated, w_down, preferred_element_type=jnp.fl...]
    psum x1 -> x0, waiting for transfers between devices: 77 us -> none  [shards(): lax.psum(jnp.dot(attended, w_out, preferred_element_type=jnp.float32), 'tp')]
    unnamed x4, waiting for transfers between devices: 75.7 us -> 0.76 us
    all_gather x0 -> x1, waiting for transfers between devices: none -> 25.5 us  [shards(): normed_ffn = lax.all_gather(normed_own, 'tp', axis=0, tiled=True)]
    reshape x3, local copies, waits for them, and re-layouts: 19.8 us -> 3.35 us  [the longest x1 1.27 us: shards(): attn_proj = lax.psum_scatter(jnp.dot(attended, w_out, preferred_element_t...]
  transfers between devices with their start and end apart: 4 -> 5, of which waited for: 4 -> 5; matrix products, arithmetic and copies ran while one was open for 15% -> 17% of each run, Pallas kernels for 0% -> 0%
where the time goes in v1:
time: 387 us; the launch traced here: 381 us
  waiting for transfers between devices  179 us (46%)
  matrix products  65.3 us (17%)
  local copies, waits for them, and re-layouts  59.5 us (15%)
  other arithmetic  54.4 us (14%)
  between operations  14 us (4%)
  starting transfers between devices  8.7 us (2%)
    all_to_all x1, waiting for transfers between devices, shards(): lax.all_to_all(outgoing, 'seq', split_axis=0, concat_axis=0, tiled=True)  56.5 us
    reduce_scatter x1, waiting for transfers between devices, shards(): lax.psum_scatter(jnp.dot(activated, w_down, preferred_element_type=jnp.fl...  40.6 us
    reduce_scatter x1, waiting for transfers between devices, shards(): lax.psum_scatter(jnp.dot(attended, w_out, preferred_element_type=jnp.floa...  40.4 us
    all_gather x1, waiting for transfers between devices, shards(): normed_ffn = lax.all_gather(normed_own, 'tp', axis=0, tiled=True)  25.5 us
    dot_general x4, matrix products, attend(): jnp.einsum('nbkgt,bket->nbkge', weights.astype(jnp.bfloat16), key_pack[:,...  21.1 us
    all_gather x1, waiting for transfers between devices, shards(): page_store = lax.all_gather(shared_pages, 'seq', axis=0, tiled=True)  15.5 us
    dot_general x4, matrix products, attend(): jnp.einsum('nbkge,bket->nbkgt', queries, key_pack[:, :, 0], preferred_ele...  14.4 us
    reduce_sum x3, other arithmetic, attend(): totals = jnp.sum(weights, -1)  13.6 us
  transfers between devices with their start and end apart: 5, of which 5 were waited for; matrix products, arithmetic and copies ran while one was open for 17% of the time, Pallas kernels for 0%

profile of v1, /device:TPU:0, one launch (start us, length us, event | category | flops | bytes accessed | tf_op | source)
XLA Modules:
  0.0 381.1 jit_solution(9774462938295240041)
XLA Ops:
  13.6 3.6 gather_fusion.11
  17.2 5.5 %select_select_fusion = bf16[16,8,1,2,80,128]{5,4,3,1,2,0:T(8,128)(2,1)} fusion(bf16[16,8,1,2,80,128]{5,4,3,1,2,0:T(8,128)(2,1)} %bitcast.319, pred[16]{0:T(512)(128)(4,1)S(1)} %reduce_or.9, pred[16,8]{1,0:T(8,128)(4,1)S(1)} %get-tuple-element.15), kind=kLoop, calls=%fused_computation.44 | loop fusion | flops 5242880 | bytes 10485904 | tf_op jit(solution)/shard_map/jit(_where)/select_n | solution.py:159
  22.7 8.3 %all-to-all-start = ((bf16[16,8,1,2,80,128]{5,4,3,1,2,0:T(8,128)(2,1)}), bf16[16,8,1,2,80,128]{5,4,3,1,2,0:T(8,128)(2,1)}, u32[]{:S(2)}, u32[]{:S(2)}) async-start(bf16[16,8,1,2,80,128]{5,4,3,1,2,0:T(8,128)(2,1)} %select_select_fusion), calls=%async_computation | async-start | bytes 10485760 | tf_op jit(solution)/shard_map/all_to_all | solution.py:162
  37.0 3.3 fusion.17
  40.4 3.0 fusion.19
  43.4 5.8 %reshape.793 = bf16[512,2560]{1,0:T(8,128)(2,1)} reshape(bf16[128,4,2560]{2,1,0:T(4,128)(2,1)} %fusion.19) | data formatting | bytes 5242880 | tf_op jit(solution)/shard_map/reshape | solution.py:121
  49.3 2.6 convolution_convert_fusion
  55.0 2.8 fusion.73
  65.9 5.5 %fusion.26 = (pred[128,4,2048]{0,2,1:T(8,128)(4,1)}, pred[128,4,2048]{0,2,1:T(8,128)(4,1)}) fusion(s32[128,4]{0,1:T(4,128)S(1)} %get-tuple-element.27, pred[4,2048]{1,0:T(4,128)(4,1)S(1)} %iota_compare_fusion.1, s32[4,2048]{1,0:T(4,128)S(1)} %iota_add_fusion, pred[4,2048]{1,0:T(4,128)(4,1)S(1)} %iota_compare_fusion), kind=kLoop, calls=%fused_computation.51 | loop fusion | flops 10485760 | bytes 2148352 | tf_op jit(solution)/shard_map/and | solution.py:49
  71.4 56.5 %all-to-all-done = bf16[16,8,1,2,80,128]{5,4,3,1,2,0:T(8,128)(2,1)} async-done(((bf16[16,8,1,2,80,128]{5,4,3,1,2,0:T(8,128)(2,1)}), bf16[16,8,1,2,80,128]{5,4,3,1,2,0:T(8,128)(2,1)}, u32[]{:S(2)}, u32[]{:S(2)}) %all-to-all-start) | async-done | bytes 5242912 | tf_op jit(solution)/shard_map/all_to_all | solution.py:162
  127.9 3.4 gather_fusion.12
  136.7 3.2 copy-done.10
  140.0 2.7 fusion.15
  142.7 15.5 %all-gather.3.cloned.1.call-done = bf16[320,1,2,80,128]{4,3,2,1,0:T(8,128)(2,1)} async-done(((bf16[20,1,2,80,128]{4,3,2,1,0:T(8,128)(2,1)}), bf16[320,1,2,80,128]{4,3,2,1,0:T(8,128)(2,1)}) %all-gather.3.cloned.1.call-update) | async-done | bytes 13107216 | tf_op jit(solution)/shard_map/all_gather | solution.py:118
  158.2 7.1 %gather_fusion.15 = bf16[64,2,80,128]{3,2,1,0:T(8,128)(2,1)} fusion(bf16[320,2,80,128]{3,2,1,0:T(8,128)(2,1)} %bitcast.325, s32[1024]{0:T(1024)S(1)} %copy-done.30), kind=kCustom, calls=%fused_computation.1.clone | custom fusion | bytes 5243136 | tf_op jit(solution)/shard_map/jit(_take)/gather | solution.py:177
  165.3 7.2 %gather_fusion.14 = bf16[64,2,80,128]{3,2,1,0:T(8,128)(2,1)} fusion(bf16[320,2,80,128]{3,2,1,0:T(8,128)(2,1)} %bitcast.326, s32[1024]{0:T(1024)S(1)} %copy-done.29), kind=kCustom, calls=%fused_computation.clone | custom fusion | bytes 5243136 | tf_op jit(solution)/shard_map/jit(_take)/gather | solution.py:168
  172.5 4.2 %fusion.35 = bf16[4,1,2,80,16,128]{5,4,3,0,2,1:T(8,128)(2,1)} fusion(bf16[4,16,1,2,80,128]{5,4,3,1,0,2:T(8,128)(2,1)} %bitcast.322, pred[4,16]{1,0:T(4,128)(4,1)S(1)} %copy-done.34), kind=kLoop, calls=%fused_computation.64 | loop fusion | flops 1310720 | bytes 5242944 | tf_op jit(solution)/shard_map/transpose | solution.py:40
  176.6 5.2 %reshape.777 = bf16[4,1,2,80,2048]{4,3,0,2,1:T(8,128)(2,1)} reshape(bf16[4,1,2,80,16,128]{5,4,3,0,2,1:T(8,128)(2,1)} %fusion.35) | data formatting | bytes 5242880 | tf_op jit(solution)/shard_map/reshape | solution.py:41
  181.8 4.3 %fusion.34 = bf16[4,1,2,80,16,128]{5,4,3,0,2,1:T(8,128)(2,1)} fusion(bf16[4,16,1,2,80,128]{5,4,3,1,0,2:T(8,128)(2,1)} %bitcast.321, pred[4,16]{1,0:T(4,128)(4,1)S(1)} %copy-done.33), kind=kLoop, calls=%fused_computation.62 | loop fusion | flops 1310720 | bytes 5242944 | tf_op jit(solution)/shard_map/transpose | solution.py:40
  186.1 5.2 %reshape.781 = bf16[4,1,2,80,2048]{4,3,0,2,1:T(8,128)(2,1)} reshape(bf16[4,1,2,80,16,128]{5,4,3,0,2,1:T(8,128)(2,1)} %fusion.34) | data formatting | bytes 5242880 | tf_op jit(solution)/shard_map/reshape | solution.py:41
  191.3 8.8 %fusion.1 = (f32[128,4,4]{0,2,1:T(4,128)S(1)}, f32[4,2048,128,4]{2,1,3,0:T(8,128)}) fusion(pred[128,4,2048]{0,2,1:T(8,128)(4,1)S(1)} %copy-done.12, bf16[128,4,4,40]{0,3,2,1:T(8,128)(2,1)S(1)} %copy-done.23, bf16[128,4,4,40]{0,3,2,1:T(8,128)(2,1)S(1)} %copy-done.21, bf16[4,1,2,80,2048]{4,3,0,2,1:T(8,128)(2,1)} %reshape.781), kind=kOutput, calls=%fused_computation.21 | convolution fusion | flops 684324864 | bytes 19472384 | tf_op jit(solution)/shard_map/nbkge,bket->nbkgt/dot_general | solution.py:45
  200.1 2.7 fusion
  202.9 10.7 %fusion.2 = (f32[128,4,4]{0,2,1:T(4,128)S(1)}, f32[128,4,4]{0,2,1:T(4,128)S(1)}) fusion(f32[4,2048,128,4]{2,1,3,0:T(8,128)S(1)} %get-tuple-element.36, f32[128,4,4]{0,2,1:T(4,128)S(1)} %get-tuple-element.35, pred[128,4,2048]{0,2,1:T(8,128)(4,1)S(1)} %copy-done.11, f32[128,4,4]{0,2,1:T(4,128)S(1)} %get-tuple-element.29, ...), kind=kLoop, calls=%fused_computation.22 | loop fusion | flops 41938944 | bytes 35684352 | tf_op jit(solution)/shard_map/reduce_sum | solution.py:53
  213.8 3.0 fusion.56
  216.7 10.7 %fusion.68 = f32[128,4,1,4,80]{0,4,3,1,2:T(8,128)} fusion(f32[4,2048,128,4]{2,1,3,0:T(8,128)} %get-tuple-element.30, f32[128,4,4]{0,2,1:T(4,128)S(1)} %get-tuple-element.29, pred[128,4,2048]{0,2,1:T(8,128)(4,1)S(1)} %copy-done.12, bf16[4,1,2,80,2048]{4,3,0,2,1:T(8,128)(2,1)} %reshape.781, f32[128,4,4]{0,2,1:T(4,128)S(1)} %bitcast.341), kind=kOutput, calls=%fused_computation.91 | convolution fusion | flops 692224000 | bytes 19808256 | tf_op jit(solution)/shard_map/nbkgt,bket->nbkge/dot_general | solution.py:54
  227.4 5.8 %fusion.65 = f32[128,4,1,4,80]{0,4,3,1,2:T(8,128)} fusion(f32[128,4,1,4,80]{0,4,3,1,2:T(8,128)} %fusion.68, f32[4,2048,128,4]{2,1,3,0:T(8,128)S(1)} %get-tuple-element.36, f32[128,4,4]{0,2,1:T(4,128)S(1)} %get-tuple-element.35, pred[128,4,2048]{0,2,1:T(8,128)(4,1)S(1)} %copy-done.11, bf16[4,1,2,80,2048]{4,3,0,2,1:T(8,128)(2,1)} %reshape.777, ...), kind=kOutput, calls=%fused_computation.90 | convolution fusion | flops 692551680 | bytes 20471808 | tf_op jit(solution)/shard_map/nbkgt,bket->nbkge/dot_general | solution.py:54
  235.7 3.8 %fusion.124 = f32[512,2560]{1,0:T(8,128)} fusion(bf16[512,320]{1,0:T(8,128)(2,1)S(1)} %reshape.797, bf16[320,2560]{1,0:T(8,128)(2,1)S(1)} %copy-done), kind=kOutput, calls=%fused_computation.213 | convolution fusion | flops 838860800 | bytes 7208960 | tf_op jit(solution)/shard_map/dot_general | solution.py:195
  240.3 40.4 %reduce-scatter.3.cloned.1.call-done = f32[64,2560]{1,0:T(8,128)} async-done(((f32[512,2560]{1,0:T(8,128)}), f32[64,2560]{1,0:T(8,128)}) %reduce-scatter.3.cloned.1.call-update) | async-done | bytes 655376 | tf_op jit(solution)/shard_map/reduce_scatter | solution.py:194
  285.5 25.5 %all-gather.5.cloned.1.call-done = bf16[512,2560]{1,0:T(8,128)(2,1)} async-done(((bf16[64,2560]{1,0:T(8,128)(2,1)}), bf16[512,2560]{1,0:T(8,128)(2,1)}) %all-gather.5.cloned.1.call-update) | async-done | bytes 2621456 | tf_op jit(solution)/shard_map/all_gather | solution.py:203
  311.0 6.8 %fusion.125 = f32[512,864]{0,1:T(8,128)} fusion(bf16[512,2560]{1,0:T(8,128)(2,1)} %all-gather.5.cloned.1.call-done, bf16[2560,864]{0,1:T(8,128)(2,1)} %param.30), kind=kOutput, calls=%fused_computation.214 | convolution fusion | flops 2264924160 | bytes 8814592 | tf_op jit(solution)/shard_map/dot_general | solution.py:204
  317.8 12.5 %fusion.78 = f32[512,2560]{1,0:T(8,128)} fusion(bf16[864,2560]{1,0:T(8,128)(2,1)} %param.32, f32[512,864]{0,1:T(8,128)} %fusion.125, bf16[512,2560]{1,0:T(8,128)(2,1)} %all-gather.5.cloned.1.call-done, bf16[2560,864]{0,1:T(8,128)(2,1)} %param.31), kind=kOutput, calls=%fused_computation.99 | convolution fusion | flops 4532502528 | bytes 18481152 | tf_op jit(solution)/shard_map/dot_general | solution.py:208
  330.4 40.6 %reduce-scatter.5.cloned.1.call-done = f32[64,2560]{1,0:T(8,128)} async-done(((f32[512,2560]{1,0:T(8,128)}), f32[64,2560]{1,0:T(8,128)}) %reduce-scatter.5.cloned.1.call-update) | async-done | bytes 655376 | tf_op jit(solution)/shard_map/reduce_scatter | solution.py:207
  (177 shorter events, 40.9 us)
Async XLA Ops:
  6.5 229.2 %copy-start = (bf16[320,2560]{1,0:T(8,128)(2,1)S(1)}, bf16[320,2560]{1,0:T(8,128)(2,1)}, u32[]{:S(2)}) copy-start(bf16[320,2560]{1,0:T(8,128)(2,1)} %param.28) | copy-start | bytes 4915204
  6.5 151.7 %all-gather.3.cloned.1.call-start = ((), (), s32[]{:S(2)}) async-start(), calls=%async_computation.3 | async-start | bytes 13926400 | tf_op jit(solution)/shard_map/all_gather | solution.py:118
  22.7 9.8 %copy-start.2 = (s32[64]{0:T(128)S(1)}, s32[64]{0:T(128)}, u32[]{:S(2)}) copy-start(s32[64]{0:T(128)} %param.40) | copy-start | bytes 772
  22.7 10.4 %copy-start.3 = (s32[64]{0:T(128)S(1)}, s32[64]{0:T(128)}, u32[]{:S(2)}) copy-start(s32[64]{0:T(128)} %param.42) | copy-start | bytes 772
  22.7 11.1 %copy-start.4 = (s32[16]{0:T(128)S(1)}, s32[16]{0:T(128)}, u32[]{:S(2)}) copy-start(s32[16]{0:T(128)} %param.39) | copy-start | bytes 196
  22.7 11.7 %copy-start.5 = (s32[16]{0:T(128)S(1)}, s32[16]{0:T(128)}, u32[]{:S(2)}) copy-start(s32[16]{0:T(128)} %param.41) | copy-start | bytes 196
  22.7 12.4 %copy-start.25 = (s32[16,16]{1,0:T(8,128)S(1)}, s32[16,16]{1,0:T(8,128)}, u32[]{:S(2)}) copy-start(s32[16,16]{1,0:T(8,128)} %param.36) | copy-start | bytes 3076
  22.7 13.0 %copy-start.6 = (s32[4]{0:T(128)S(1)}, s32[4]{0:T(128)}, u32[]{:S(2)}) copy-start(s32[4]{0:T(128)} %param.38) | copy-start | bytes 52
  22.7 13.7 %copy-start.24 = (s32[4,16]{1,0:T(4,128)S(1)}, s32[4,16]{1,0:T(4,128)}, u32[]{:S(2)}) copy-start(s32[4,16]{1,0:T(4,128)} %param.35) | copy-start | bytes 772
  22.7 14.3 %copy-start.31 = (bf16[2560]{0:T(1024)(128)(2,1)S(1)}, bf16[2560]{0:T(1024)(128)(2,1)}, u32[]{:S(2)}) copy-start(bf16[2560]{0:T(1024)(128)(2,1)} %param.24) | copy-start | bytes 15364
  22.7 105.2 %all-to-all-start = ((bf16[16,8,1,2,80,128]{5,4,3,1,2,0:T(8,128)(2,1)}), bf16[16,8,1,2,80,128]{5,4,3,1,2,0:T(8,128)(2,1)}, u32[]{:S(2)}, u32[]{:S(2)}) async-start(bf16[16,8,1,2,80,128]{5,4,3,1,2,0:T(8,128)(2,1)} %select_select_fusion), calls=%async_computation | async-start | bytes 10485760 | tf_op jit(solution)/shard_map/all_to_all | solution.py:162
  31.1 249.6 %reduce-scatter.3.cloned.1.call-start = ((), (), s32[]{:S(2)}) async-start(), calls=%async_computation.4 | async-start | bytes 5898240 | tf_op jit(solution)/shard_map/reduce_scatter | solution.py:194
  40.4 8.9 %copy-start.19 = (bf16[2560,80]{0,1:T(8,128)(2,1)S(1)}, bf16[2560,80]{0,1:T(8,128)(2,1)}, u32[]{:S(2)}) copy-start(bf16[2560,80]{0,1:T(8,128)(2,1)} %param.27) | copy-start | bytes 1228804
  43.4 11.6 %copy-start.36 = (bf16[2560,80]{0,1:T(8,128)(2,1)S(1)}, bf16[2560,80]{0,1:T(8,128)(2,1)}, u32[]{:S(2)}) copy-start(bf16[2560,80]{0,1:T(8,128)(2,1)} %param.26) | copy-start | bytes 1228804
  65.7 71.0 %copy-start.14 = (pred[128,4,1024]{0,2,1:T(8,128)(4,1)}, pred[128,4,1024]{0,2,1:T(8,128)(4,1)S(1)}, u32[]{:S(2)}) copy-start(pred[128,4,1024]{0,2,1:T(8,128)(4,1)S(1)} %fusion.37) | copy-start | bytes 1572868
  140.0 18.2 %copy-start.30 = (s32[1024]{0:T(1024)S(1)}, s32[1024]{0:T(1024)}, u32[]{:S(2)}) copy-start(s32[1024]{0:T(1024)} %pad_clamp_fusion.4) | copy-start | bytes 12292
  142.7 22.6 %copy-start.29 = (s32[1024]{0:T(1024)S(1)}, s32[1024]{0:T(1024)}, u32[]{:S(2)}) copy-start(s32[1024]{0:T(1024)} %pad_clamp_fusion.5) | copy-start | bytes 12292
  158.2 14.3 %copy-start.34 = (pred[4,16]{1,0:T(4,128)(4,1)S(1)}, pred[4,16]{1,0:T(4,128)(4,1)}, u32[]{:S(2)}) copy-start(pred[4,16]{1,0:T(4,128)(4,1)} %compare_and_fusion.2) | copy-start | bytes 196
  172.5 9.4 %copy-start.33 = (pred[4,16]{1,0:T(4,128)(4,1)S(1)}, pred[4,16]{1,0:T(4,128)(4,1)}, u32[]{:S(2)}) copy-start(pred[4,16]{1,0:T(4,128)(4,1)} %compare_and_fusion.1) | copy-start | bytes 196
  181.8 9.5 %copy-start.12 = (pred[128,4,2048]{0,2,1:T(8,128)(4,1)S(1)}, pred[128,4,2048]{0,2,1:T(8,128)(4,1)}, u32[]{:S(2)}) copy-start(pred[128,4,2048]{0,2,1:T(8,128)(4,1)} %get-tuple-element.26) | copy-start | bytes 3145732
  181.8 9.5 %copy-start.21 = (bf16[128,4,4,40]{0,3,2,1:T(8,128)(2,1)S(1)}, bf16[128,4,4,40]{0,3,2,1:T(8,128)(2,1)}, u32[]{:S(2)}) copy-start(bf16[128,4,4,40]{0,3,2,1:T(8,128)(2,1)} %copy-done.20) | copy-start | bytes 491524
  181.8 9.5 %copy-start.23 = (bf16[128,4,4,40]{0,3,2,1:T(8,128)(2,1)S(1)}, bf16[128,4,4,40]{0,3,2,1:T(8,128)(2,1)}, u32[]{:S(2)}) copy-start(bf16[128,4,4,40]{0,3,2,1:T(8,128)(2,1)} %copy-done.22) | copy-start | bytes 491524
  191.3 8.8 %copy-start.11 = (pred[128,4,2048]{0,2,1:T(8,128)(4,1)S(1)}, pred[128,4,2048]{0,2,1:T(8,128)(4,1)}, u32[]{:S(2)}) copy-start(pred[128,4,2048]{0,2,1:T(8,128)(4,1)} %get-tuple-element.25) | copy-start | bytes 3145732
  191.3 8.8 %copy-start.13 = (bf16[4,1,2,80,2048]{4,3,0,2,1:T(8,128)(2,1)S(1)}, bf16[4,1,2,80,2048]{4,3,0,2,1:T(8,128)(2,1)}, u32[]{:S(2)}) copy-start(bf16[4,1,2,80,2048]{4,3,0,2,1:T(8,128)(2,1)} %reshape.777) | copy-start | bytes 7864324
  200.1 13.6 %slice-start = ((s8[8388608]{0:T(1024)(128)(4,1)}), s8[4194304]{0:T(1024)(128)(4,1)S(1)}, s32[]{:S(2)}) async-start(s8[8388608]{0:T(1024)(128)(4,1)} %bitcast.323), calls=%async_computation.7 | async-start | bytes 8388608
  202.9 10.8 %copy-start.27 = (f32[128,4,4]{0,2,1:T(4,128)S(1)}, f32[128,4,4]{0,2,1:T(4,128)}, u32[]{:S(2)}) copy-start(f32[128,4,4]{0,2,1:T(4,128)} %copy-done.26) | copy-start | bytes 24580
  202.9 10.8 %copy-start.28 = (f32[128,4,4]{0,2,1:T(4,128)S(1)}, f32[128,4,4]{0,2,1:T(4,128)}, u32[]{:S(2)}) copy-start(f32[128,4,4]{0,2,1:T(4,128)} %fusion.15) | copy-start | bytes 24580
  202.9 10.8 %slice-start.1 = ((s8[8388608]{0:T(1024)(128)(4,1)}), s8[4194304]{0:T(1024)(128)(4,1)S(1)}, s32[]{:S(2)}) async-start(s8[8388608]{0:T(1024)(128)(4,1)} %bitcast.323), calls=%async_computation.8 | async-start | bytes 8388608
  202.9 10.8 %copy-start.15 = (pred[128,4,1024]{0,2,1:T(8,128)(4,1)S(1)}, pred[128,4,1024]{0,2,1:T(8,128)(4,1)}, u32[]{:S(2)}) copy-start(pred[128,4,1024]{0,2,1:T(8,128)(4,1)} %copy-done.14) | copy-start | bytes 1572868
  202.9 10.8 %copy-start.16 = (bf16[4,1,2,80,1024]{4,3,0,2,1:T(8,128)(2,1)S(1)}, bf16[4,1,2,80,1024]{4,3,0,2,1:T(8,128)(2,1)}, u32[]{:S(2)}) copy-start(bf16[4,1,2,80,1024]{4,3,0,2,1:T(8,128)(2,1)} %reshape.788) | copy-start | bytes 3932164
  239.6 71.4 %all-gather.5.cloned.1.call-start = ((), (), s32[]{:S(2)}) async-start(), calls=%async_computation.5 | async-start | bytes 2949120 | tf_op jit(solution)/shard_map/all_gather | solution.py:203
  285.2 85.7 %reduce-scatter.5.cloned.1.call-start = ((), (), s32[]{:S(2)}) async-start(), calls=%async_computation.6 | async-start | bytes 5898240 | tf_op jit(solution)/shard_map/reduce_scatter | solution.py:207
  (12 other events, 42.0 us)
Sparse Core Ops, SparseCore 0:
  9.5 148.6 all-gather.2
  239.7 40.8 reduce-scatter.2
  285.4 25.6 all-gather.4
  330.5 40.4 reduce-scatter.4

commit v2 on v1

--- a/solution.py
+++ b/solution.py
@@ -2,6 +2,8 @@
 import jax.numpy as jnp
 from jax import lax
 from jax.sharding import PartitionSpec as P
+from jax.experimental import pallas as pl
+from jax.experimental.pallas import tpu as pltpu
 
 QH = 32
 KVH = 8
@@ -69,6 +71,146 @@
         maximum,
         first[2] * first_scale + second[2] * second_scale,
     )
+
+
+ROOT_PAGES = 16
+MID_PAGES = 16
+LEAF_SLOTS = 8
+
+
+def paged_kernel(tbl, meta, q_ref, fresh_ref, shared_hbm, leaf_hbm, out_ref, kv, sc, sem):
+    i = pl.program_id(0)
+    steps = pl.num_programs(0)
+    slot = i % 2
+    shared_count = ROOT_PAGES + MID_PAGES
+    page_count = shared_count + LEAF_SLOTS
+
+    def start_request(j, into):
+        def shared_body(p, carry):
+            pltpu.make_async_copy(shared_hbm.at[tbl[j, p]], kv.at[into, p], sem.at[into]).start()
+            return carry
+
+        def leaf_body(p, carry):
+            pltpu.make_async_copy(leaf_hbm.at[tbl[j, p]], kv.at[into, p], sem.at[into]).start()
+            return carry
+
+        lax.fori_loop(0, shared_count, shared_body, 0)
+        lax.fori_loop(shared_count, page_count, leaf_body, 0)
+
+    @pl.when(i == 0)
+    def _():
+        start_request(0, 0)
+
+    @pl.when(i + 1 < steps)
+    def _():
+        start_request(i + 1, 1 - slot)
+
+    def wait_body(p, carry):
+        pltpu.make_async_copy(shared_hbm.at[0], kv.at[slot, p], sem.at[slot]).wait()
+        return carry
+
+    lax.fori_loop(0, page_count, wait_body, 0)
+
+    root_span = meta[i, 0]
+    mid_span = meta[i, 1]
+    leaf_span = meta[i, 2]
+    context = meta[i, 3]
+    q = q_ref[0]
+    rows, width = q.shape[0], kv.shape[-1]
+    query_pos = context + (lax.broadcasted_iota(jnp.int32, (rows, 1), 0) % width)
+    lanes = lax.broadcasted_iota(jnp.int32, (1, width), 1)
+    scale = HD ** (-0.5)
+
+    def scores_of(keys, key_pos, present):
+        s = jnp.dot(q, keys, preferred_element_type=jnp.float32) * scale
+        distance = query_pos - key_pos
+        allowed = present & (distance >= 0) & (distance < WINDOW)
+        return jnp.where(allowed, s, masked_score)
+
+    def geometry(c):
+        in_root = c < ROOT_PAGES
+        in_mid = c < shared_count
+        first = jnp.where(
+            in_root, c * width, jnp.where(in_mid, (c - ROOT_PAGES) * width, (c - shared_count) * width)
+        )
+        base = jnp.where(in_root, 0, jnp.where(in_mid, root_span, root_span + mid_span))
+        limit = jnp.where(in_root, root_span, jnp.where(in_mid, mid_span, leaf_span))
+        return first, base, limit
+
+    fresh_scores = scores_of(fresh_ref[0, 0], context + lanes, lanes >= 0)
+    sc[page_count] = fresh_scores
+    maximum = jnp.max(fresh_scores, -1, keepdims=True)
+
+    def max_body(c, running):
+        first, base, limit = geometry(c)
+
+        def live():
+            steps_in = first + lanes
+            s = scores_of(kv[slot, c, 0], base + steps_in, steps_in < limit)
+            sc[c] = s
+            return jnp.maximum(running, jnp.max(s, -1, keepdims=True))
+
+        return lax.cond(first < limit, live, lambda: running)
+
+    maximum = lax.fori_loop(0, page_count, max_body, maximum)
+
+    def weigh(s, values, totals, acc):
+        w = jnp.exp(s - maximum)
+        totals = totals + jnp.sum(w, -1, keepdims=True)
+        acc = acc + lax.dot_general(
+            w.astype(jnp.bfloat16), values, (((1,), (1,)), ((), ())), preferred_element_type=jnp.float32
+        )
+        return totals, acc
+
+    carry = weigh(
+        sc[page_count],
+        fresh_ref[0, 1],
+        jnp.zeros((rows, 1), jnp.float32),
+        jnp.zeros((rows, q.shape[1]), jnp.float32),
+    )
+
+    def sum_body(c, carry):
+        first, base, limit = geometry(c)
+        return lax.cond(
+            first < limit, lambda: weigh(sc[c], kv[slot, c, 1], *carry), lambda: carry
+        )
+
+    totals, acc = lax.fori_loop(0, page_count, sum_body, carry)
+    out_ref[0] = (acc / totals).astype(out_ref.dtype)
+
+
+def paged_attention(tbl, meta, queries, fresh, shared_store, leaf_store):
+    reqs, rows, head = queries.shape
+    page_shape = shared_store.shape[1:]
+    pages = tbl.shape[1]
+    keys_total = (pages + 1) * page_shape[-1]
+    grid_spec = pltpu.PrefetchScalarGridSpec(
+        num_scalar_prefetch=2,
+        grid=(reqs,),
+        in_specs=[
+            pl.BlockSpec((1, rows, head), lambda i, t, m: (i, 0, 0)),
+            pl.BlockSpec((1,) + page_shape, lambda i, t, m: (i, 0, 0, 0)),
+            pl.BlockSpec(memory_space=pl.ANY),
+            pl.BlockSpec(memory_space=pl.ANY),
+        ],
+        out_specs=pl.BlockSpec((1, rows, head), lambda i, t, m: (i, 0, 0)),
+        scratch_shapes=[
+            pltpu.VMEM((2, pages) + page_shape, shared_store.dtype),
+            pltpu.VMEM((pages + 1, rows, page_shape[-1]), jnp.float32),
+            pltpu.SemaphoreType.DMA((2,)),
+        ],
+    )
+    return pl.pallas_call(
+        paged_kernel,
+        grid_spec=grid_spec,
+        out_shape=jax.ShapeDtypeStruct((reqs, rows, head), jnp.bfloat16),
+        compiler_params=pltpu.CompilerParams(dimension_semantics=("arbitrary",)),
+        cost_estimate=pl.CostEstimate(
+            flops=4 * reqs * rows * keys_total * head,
+            transcendentals=reqs * rows * keys_total,
+            bytes_accessed=reqs * (pages + 1) * 2 * head * page_shape[-1] * 2,
+        ),
+    )(tbl, meta, queries, fresh, shared_store, leaf_store)
 
 
 def spans(request_ids, root_len, mid_len, leaf_len, mid_parent, leaf_parent):
@@ -145,48 +287,30 @@
     page_ids = jnp.where(
         sender_have[:, None], leaf_table[picked_request] - seq_index * pages_here, 0
     )
-    leaf_steps = jnp.arange(leaf_table.shape[1] * leaf_pages.shape[-1], dtype=jnp.int32)
-    fresh_pack = jnp.stack(
-        [jnp.transpose(new_keys, (1, 2, 3, 0)), jnp.transpose(new_values, (1, 2, 3, 0))], 2
-    )
-    fresh_part = attend(
-        queries,
-        fresh_pack,
-        context[:, None] + new_index[None, :],
-        jnp.ones((local_reqs, new_rows), bool),
-        query_pos,
-    )
+    leaf_slots = leaf_table.shape[1]
     outgoing = jnp.where(
         sender_have[:, None, None, None, None, None], jnp.take(leaf_pages, page_ids, axis=0), 0
     )
     arrived = lax.all_to_all(outgoing, "seq", split_axis=0, concat_axis=0, tiled=True)
-    leaf_pack = page_columns(jnp.take(arrived, own_homes, axis=0))
-    leaf_pos = (root_span + mid_span)[:, None] + leaf_steps[None, :]
-    leaf_part = attend(
-        queries, leaf_pack, leaf_pos, leaf_steps[None, :] < leaf_span[:, None], query_pos
-    )
-    root_pack = page_columns(jnp.take(page_store, root_index, axis=0))
-    root_steps = jnp.arange(root_pack.shape[-1], dtype=jnp.int32)
-    root_part = attend(
-        queries,
-        root_pack,
-        root_steps[None, :] + 0 * root_span[:, None],
-        root_steps[None, :] < root_span[:, None],
-        query_pos,
-    )
-    mid_pack = page_columns(jnp.take(page_store, mid_index, axis=0))
-    mid_steps = jnp.arange(mid_pack.shape[-1], dtype=jnp.int32)
-    mid_part = attend(
-        queries,
-        mid_pack,
-        root_span[:, None] + mid_steps[None, :],
-        mid_steps[None, :] < mid_span[:, None],
-        query_pos,
-    )
-    combined = merge_parts(merge_parts(root_part, mid_part), merge_parts(leaf_part, fresh_part))
+    page_shape = arrived.shape[-3:]
+    leaf_store = arrived.reshape((-1,) + page_shape)
+    shared_store = page_store.reshape((-1,) + page_shape)
+    tbl = jnp.concatenate(
+        [
+            root_index,
+            mid_index,
+            own_homes[:, None] * leaf_slots + jnp.arange(leaf_slots, dtype=jnp.int32)[None, :],
+        ],
+        1,
+    ).astype(jnp.int32)
+    meta = jnp.stack([root_span, mid_span, leaf_span, context], 1).astype(jnp.int32)
+    fresh_pack = jnp.stack(
+        [jnp.transpose(new_keys[:, :, 0], (1, 2, 0)), jnp.transpose(new_values[:, :, 0], (1, 2, 0))], 1
+    )
+    query_rows = jnp.transpose(queries[:, :, 0], (1, 2, 0, 3)).reshape(local_reqs, -1, HD)
+    attended = paged_attention(tbl, meta, query_rows, fresh_pack, shared_store, leaf_store)
     attended = (
-        (combined[0] / combined[2][..., None])
-        .astype(jnp.bfloat16)
+        jnp.transpose(attended.reshape(local_reqs, group_size, new_rows, HD), (2, 0, 1, 3))
         .reshape(new_rows * local_reqs, -1)
     )
     tp_count = lax.axis_size("tp")

time: 387 us -> 406 us (1.049)
  Pallas kernels: 0 us -> 83.4 us
  waiting for transfers between devices: 179 us -> 217 us
  matrix products: 65.3 us -> 29.6 us
  local copies, waits for them, and re-layouts: 59.5 us -> 26.3 us
  other arithmetic: 54.4 us -> 24.4 us
    pallas_call x0 -> x1, Pallas kernels: none -> 83.4 us  [paged_attention(): pl.pallas_call(paged_kernel, grid_spec=grid_spec, out_shape=jax.ShapeDtyp...]
    dot_general x8 -> x0, matrix products: 35.6 us -> none  [the longest x4 21.1 us: attend(): jnp.einsum('nbkgt,bket->nbkge', weights.astype(jnp.bfloat16), key_pack[:,...]
    gather x3 -> x0, local copies, waits for them, and re-layouts: 17.7 us -> none  [the longest x1 7.18 us: shards(): root_pack = page_columns(jnp.take(page_store, root_index, axis=0))]
    all_gather x1, waiting for transfers between devices: 15.5 us -> 30.3 us  [shards(): page_store = lax.all_gather(shared_pages, 'seq', axis=0, tiled=True)]
    reduce_scatter x1, waiting for transfers between devices: 40.4 us -> 55 us  [shards(): lax.psum_scatter(jnp.dot(attended, w_out, preferred_element_type=jnp.floa...]
    reduce_sum x3 -> x0, other arithmetic: 13.6 us -> none  [attend(): totals = jnp.sum(weights, -1)]
    reshape x4 -> x2, local copies, waits for them, and re-layouts: 12.2 us -> 1.79 us  [the longest x1 1.45 us: shards(): attended.reshape(local_reqs, group_size, new_rows, HD)]
    transpose x3 -> x1, other arithmetic: 9.24 us -> 0.03 us  [shards(): jnp.transpose(queries[:, :, 0], (1, 2, 0, 3)).reshape(local_reqs, -1, HD)]
  transfers between devices with their start and end apart: 5 -> 5, of which waited for: 5 -> 5; matrix products, arithmetic and copies ran while one was open for 17% -> 12% of each run, Pallas kernels for 0% -> 0%
where the time goes in v2:
time: 406 us; the launch traced here: 403 us
  waiting for transfers between devices  217 us (53%)
  Pallas kernels  83.4 us (21%)
  matrix products  29.6 us (7%)
  local copies, waits for them, and re-layouts  26.3 us (6%)
  other arithmetic  24.4 us (6%)
  between operations  13.5 us (3%)
  starting transfers between devices  8.85 us (2%)
    pallas_call x1, Pallas kernels, paged_attention(): pl.pallas_call(paged_kernel, grid_spec=grid_spec, out_shape=jax.ShapeDtyp...  83.4 us
    all_to_all x1, waiting for transfers between devices, shards(): lax.all_to_all(outgoing, 'seq', split_axis=0, concat_axis=0, tiled=True)  64.7 us
    reduce_scatter x1, waiting for transfers between devices, shards(): lax.psum_scatter(jnp.dot(attended, w_out, preferred_element_type=jnp.floa...  55 us
    reduce_scatter x1, waiting for transfers between devices, shards(): lax.psum_scatter(jnp.dot(activated, w_down, preferred_element_type=jnp.fl...  40.6 us
    all_gather x1, waiting for transfers between devices, shards(): page_store = lax.all_gather(shared_pages, 'seq', axis=0, tiled=True)  30.3 us
    all_gather x1, waiting for transfers between devices, shards(): normed_ffn = lax.all_gather(normed_own, 'tp', axis=0, tiled=True)  25.7 us
    dot_general x1, matrix products, shards(): jnp.dot(activated, w_down, preferred_element_type=jnp.float32)  12.5 us
    all_to_all x1, starting transfers between devices, shards(): lax.all_to_all(outgoing, 'seq', split_axis=0, concat_axis=0, tiled=True)  8.32 us
  transfers between devices with their start and end apart: 5, of which 5 were waited for; matrix products, arithmetic and copies ran while one was open for 12% of the time, Pallas kernels for 0%

profile of v2, /device:TPU:0, one launch (start us, length us, event | category | flops | bytes accessed | tf_op | source)
XLA Modules:
  0.0 403.1 jit_solution(13081288155234119227)
XLA Ops:
  6.5 0.7 all-gather.3.cloned.1.call-update
  7.3 0.7 reshape.329
  8.0 0.7 reshape.330
  8.8 0.8 copy.95
  10.3 0.8 gather_fusion.9
  13.6 3.5 gather_fusion.11
  17.1 5.5 %select_select_fusion = bf16[16,8,1,2,80,128]{5,4,3,1,2,0:T(8,128)(2,1)} fusion(bf16[16,8,1,2,80,128]{5,4,3,1,2,0:T(8,128)(2,1)} %bitcast.84, pred[16]{0:T(512)(128)(4,1)S(1)} %reduce_or.9, pred[16,8]{1,0:T(8,128)(4,1)S(1)} %get-tuple-element.7), kind=kLoop, calls=%fused_computation.18 | loop fusion | flops 5242880 | bytes 10485904 | tf_op jit(solution)/shard_map/jit(_where)/select_n | solution.py:291
  22.6 8.3 %all-to-all-start = ((bf16[16,8,1,2,80,128]{5,4,3,1,2,0:T(8,128)(2,1)}), bf16[16,8,1,2,80,128]{5,4,3,1,2,0:T(8,128)(2,1)}, u32[]{:S(2)}, u32[]{:S(2)}) async-start(bf16[16,8,1,2,80,128]{5,4,3,1,2,0:T(8,128)(2,1)} %select_select_fusion), calls=%async_computation | async-start | bytes 10485760 | tf_op jit(solution)/shard_map/all_to_all | solution.py:294
  35.9 3.4 fusion
  39.7 1.5 fusion.41
  41.2 1.1 fusion.3
  42.4 1.0 copy.91
  43.4 4.8 %fusion.2 = bf16[128,4,2560]{2,1,0:T(4,128)(2,1)} fusion(bf16[128,4,2560]{2,1,0:T(4,128)(2,1)} %param.21, f32[2560]{0:T(1024)S(1)} %convert_element_type.43, f32[128,4]{1,0:T(8,128)S(1)} %add_rsqrt_fusion), kind=kLoop, calls=%fused_computation.17 | loop fusion | flops 5242880 | bytes 5255168 | tf_op jit(solution)/shard_map/convert_element_type | solution.py:21
  48.2 5.4 %reshape.327 = bf16[512,2560]{1,0:T(8,128)(2,1)} reshape(bf16[128,4,2560]{2,1,0:T(4,128)(2,1)} %fusion.2) | data formatting | bytes 5242880 | tf_op jit(solution)/shard_map/reshape | solution.py:263
  53.6 2.7 convolution_convert_fusion
  59.4 2.7 fusion.7
  63.2 64.7 %all-to-all-done = bf16[16,8,1,2,80,128]{5,4,3,1,2,0:T(8,128)(2,1)} async-done(((bf16[16,8,1,2,80,128]{5,4,3,1,2,0:T(8,128)(2,1)}), bf16[16,8,1,2,80,128]{5,4,3,1,2,0:T(8,128)(2,1)}, u32[]{:S(2)}, u32[]{:S(2)}) %all-to-all-start) | async-done | bytes 5242912 | tf_op jit(solution)/shard_map/all_to_all | solution.py:294
  127.9 30.3 %all-gather.3.cloned.1.call-done = bf16[320,1,2,80,128]{4,3,2,1,0:T(8,128)(2,1)} async-done(((bf16[20,1,2,80,128]{4,3,2,1,0:T(8,128)(2,1)}), bf16[320,1,2,80,128]{4,3,2,1,0:T(8,128)(2,1)}) %all-gather.3.cloned.1.call-update) | async-done | bytes 13107216 | tf_op jit(solution)/shard_map/all_gather | solution.py:260
  158.2 83.4 %shard_map.199 = bf16[4,512,80]{2,1,0:T(8,128)(2,1)} custom-call(s32[4,40]{1,0:T(4,128)} %pad_add_fusion.tbl, s32[4,4]{1,0:T(4,128)} %pad_add_fusion.1.meta, bf16[4,512,80]{2,1,0:T(8,128)(2,1)} %bitcast.88, bf16[4,2,80,128]{3,2,1,0:T(8,128)(2,1)} %pad_maximum_fusion.fresh_ref, bf16[320,2,80,128]{3,2,1,0:T(8,128)(2,1)} %bitcast.94, ...), custom_call_target="tpu_custom_call" | custom-call | flops 3439329280 | bytes 6717440 | tf_op jit(solution)/shard_map/pallas_call | solution.py:203
  241.6 1.4 copy.110
  243.4 3.8 fusion.29
  248.0 55.0 %reduce-scatter.3.cloned.1.call-done = f32[64,2560]{1,0:T(8,128)} async-done(((f32[512,2560]{1,0:T(8,128)}), f32[64,2560]{1,0:T(8,128)}) %reduce-scatter.3.cloned.1.call-update) | async-done | bytes 655376 | tf_op jit(solution)/shard_map/reduce_scatter | solution.py:318
  302.9 1.3 reshape.335
  304.2 1.3 multiply_reduce_fusion
  305.5 1.2 multiply_convert_fusion.1
  306.7 0.8 reshape.336
  307.6 25.7 %all-gather.5.cloned.1.call-done = bf16[512,2560]{1,0:T(8,128)(2,1)} async-done(((bf16[64,2560]{1,0:T(8,128)(2,1)}), bf16[512,2560]{1,0:T(8,128)(2,1)}) %all-gather.5.cloned.1.call-update) | async-done | bytes 2621456 | tf_op jit(solution)/shard_map/all_gather | solution.py:327
  333.3 6.8 %fusion.30 = f32[512,864]{0,1:T(8,128)} fusion(bf16[512,2560]{1,0:T(8,128)(2,1)} %all-gather.5.cloned.1.call-done, bf16[2560,864]{0,1:T(8,128)(2,1)} %param.28), kind=kOutput, calls=%fused_computation.98 | convolution fusion | flops 2264924160 | bytes 8814592 | tf_op jit(solution)/shard_map/dot_general | solution.py:328
  340.2 12.5 %fusion.10 = f32[512,2560]{1,0:T(8,128)} fusion(bf16[864,2560]{1,0:T(8,128)(2,1)} %param.30, f32[512,864]{0,1:T(8,128)} %fusion.30, bf16[512,2560]{1,0:T(8,128)(2,1)} %all-gather.5.cloned.1.call-done, bf16[2560,864]{0,1:T(8,128)(2,1)} %param.29), kind=kOutput, calls=%fused_computation.26 | convolution fusion | flops 4532502528 | bytes 18481152 | tf_op jit(solution)/shard_map/dot_general | solution.py:332
  352.7 40.6 %reduce-scatter.5.cloned.1.call-done = f32[64,2560]{1,0:T(8,128)} async-done(((f32[512,2560]{1,0:T(8,128)}), f32[64,2560]{1,0:T(8,128)}) %reduce-scatter.5.cloned.1.call-update) | async-done | bytes 655376 | tf_op jit(solution)/shard_map/reduce_scatter | solution.py:331
  393.3 1.3 reshape.337
  394.6 2.0 fusion.22
  (104 shorter events, 13.9 us)
Async XLA Ops:
  6.5 236.9 %copy-start = (bf16[320,2560]{1,0:T(8,128)(2,1)S(1)}, bf16[320,2560]{1,0:T(8,128)(2,1)}, u32[]{:S(2)}) copy-start(bf16[320,2560]{1,0:T(8,128)(2,1)} %param.26) | copy-start | bytes 4915204
  6.5 151.6 %all-gather.3.cloned.1.call-start = ((), (), s32[]{:S(2)}) async-start(), calls=%async_computation.3 | async-start | bytes 13926400 | tf_op jit(solution)/shard_map/all_gather | solution.py:260
  10.3 3.3 copy-start.9
  22.6 8.6 %copy-start.2 = (s32[64]{0:T(128)S(1)}, s32[64]{0:T(128)}, u32[]{:S(2)}) copy-start(s32[64]{0:T(128)} %param.41) | copy-start | bytes 772
  22.6 9.9 %copy-start.3 = (s32[64]{0:T(128)S(1)}, s32[64]{0:T(128)}, u32[]{:S(2)}) copy-start(s32[64]{0:T(128)} %param.40) | copy-start | bytes 772
  22.6 10.6 %copy-start.4 = (s32[16]{0:T(128)S(1)}, s32[16]{0:T(128)}, u32[]{:S(2)}) copy-start(s32[16]{0:T(128)} %param.39) | copy-start | bytes 196
  22.6 11.2 %copy-start.5 = (s32[16]{0:T(128)S(1)}, s32[16]{0:T(128)}, u32[]{:S(2)}) copy-start(s32[16]{0:T(128)} %param.37) | copy-start | bytes 196
  22.6 105.3 %all-to-all-start = ((bf16[16,8,1,2,80,128]{5,4,3,1,2,0:T(8,128)(2,1)}), bf16[16,8,1,2,80,128]{5,4,3,1,2,0:T(8,128)(2,1)}, u32[]{:S(2)}, u32[]{:S(2)}) async-start(bf16[16,8,1,2,80,128]{5,4,3,1,2,0:T(8,128)(2,1)} %select_select_fusion), calls=%async_computation | async-start | bytes 10485760 | tf_op jit(solution)/shard_map/all_to_all | solution.py:294
  30.9 3.6 copy-start.6
  30.9 4.2 %copy-start.13 = (bf16[2560]{0:T(1024)(128)(2,1)S(1)}, bf16[2560]{0:T(1024)(128)(2,1)}, u32[]{:S(2)}) copy-start(bf16[2560]{0:T(1024)(128)(2,1)} %param.22) | copy-start | bytes 15364
  31.0 4.2 %copy-start.7 = (s32[4]{0:T(128)S(1)}, s32[4]{0:T(128)}, u32[]{:S(2)}) copy-start(s32[4]{0:T(128)} %param.36) | copy-start | bytes 52
  31.0 272.0 %reduce-scatter.3.cloned.1.call-start = ((), (), s32[]{:S(2)}) async-start(), calls=%async_computation.4 | async-start | bytes 5898240 | tf_op jit(solution)/shard_map/reduce_scatter | solution.py:318
  35.8 3.9 copy-start.8
  39.7 1.5 copy-start.15
  48.2 5.4 %copy-start.10 = (bf16[2560,80]{0,1:T(8,128)(2,1)S(1)}, bf16[2560,80]{0,1:T(8,128)(2,1)}, u32[]{:S(2)}) copy-start(bf16[2560,80]{0,1:T(8,128)(2,1)} %param.25) | copy-start | bytes 1228804
  53.6 3.3 copy-start.11
  53.6 3.8 copy-start.12
  53.6 5.8 %copy-start.16 = (bf16[2560,80]{0,1:T(8,128)(2,1)S(1)}, bf16[2560,80]{0,1:T(8,128)(2,1)}, u32[]{:S(2)}) copy-start(bf16[2560,80]{0,1:T(8,128)(2,1)} %param.24) | copy-start | bytes 1228804
  247.3 0.7 copy-start.14
  247.3 86.0 %all-gather.5.cloned.1.call-start = ((), (), s32[]{:S(2)}) async-start(), calls=%async_computation.5 | async-start | bytes 2949120 | tf_op jit(solution)/shard_map/all_gather | solution.py:327
  307.6 85.7 %reduce-scatter.5.cloned.1.call-start = ((), (), s32[]{:S(2)}) async-start(), calls=%async_computation.6 | async-start | bytes 5898240 | tf_op jit(solution)/shard_map/reduce_scatter | solution.py:331
  352.7 43.9 %copy-start.1 = (bf16[320,2560]{1,0:T(8,128)(2,1)S(1)}, bf16[320,2560]{1,0:T(8,128)(2,1)}, u32[]{:S(2)}) copy-start(bf16[320,2560]{1,0:T(8,128)(2,1)} %param.26) | copy-start | bytes 4915204
Sparse Core Ops, SparseCore 0:
  9.5 148.6 all-gather.2
  247.4 55.4 reduce-scatter.2
  307.7 25.6 all-gather.4
  352.8 40.4 reduce-scatter.4

commit v3 on v2

--- a/solution.py
+++ b/solution.py
@@ -315,12 +315,16 @@
     )
     tp_count = lax.axis_size("tp")
     own_count = new_rows // tp_count
-    attn_proj = lax.psum_scatter(
-        jnp.dot(attended, w_out, preferred_element_type=jnp.float32),
-        "tp",
-        scatter_dimension=0,
-        tiled=True,
-    ).reshape(own_count, local_reqs, model_width)
+    attn_proj = (
+        lax.psum_scatter(
+            jnp.dot(attended, w_out, preferred_element_type=jnp.float32).astype(jnp.bfloat16),
+            "tp",
+            scatter_dimension=0,
+            tiled=True,
+        )
+        .astype(jnp.float32)
+        .reshape(own_count, local_reqs, model_width)
+    )
     own_hidden = lax.dynamic_slice_in_dim(hidden, lax.axis_index("tp") * own_count, own_count, 0)
     resid = own_hidden.astype(jnp.float32) + attn_proj
     normed_own = rms_norm(resid, gain_ffn).reshape(-1, model_width)
@@ -328,12 +332,16 @@
     gate_rows = jnp.dot(normed_ffn, w_gate, preferred_element_type=jnp.float32)
     up_rows = jnp.dot(normed_ffn, w_up, preferred_element_type=jnp.float32)
     activated = (jax.nn.silu(gate_rows) * up_rows).astype(jnp.bfloat16)
-    ffn_proj = lax.psum_scatter(
-        jnp.dot(activated, w_down, preferred_element_type=jnp.float32),
-        "tp",
-        scatter_dimension=0,
-        tiled=True,
-    ).reshape(own_count, local_reqs, model_width)
+    ffn_proj = (
+        lax.psum_scatter(
+            jnp.dot(activated, w_down, preferred_element_type=jnp.float32).astype(jnp.bfloat16),
+            "tp",
+            scatter_dimension=0,
+            tiled=True,
+        )
+        .astype(jnp.float32)
+        .reshape(own_count, local_reqs, model_width)
+    )
     return resid + ffn_proj
 
 

time: 406 us -> 394 us (0.970)
  waiting for transfers between devices: 217 us -> 198 us
  Pallas kernels: 83.4 us -> 91.3 us
    reduce_scatter x1, waiting for transfers between devices: 55 us -> 42.3 us  [shards(): lax.psum_scatter(jnp.dot(attended, w_out, preferred_element_type=jnp.floa...]
    pallas_call x1, Pallas kernels: 83.4 us -> 91.3 us  [paged_attention(): pl.pallas_call(paged_kernel, grid_spec=grid_spec, out_shape=jax.ShapeDtyp...]
    reduce_scatter x1, waiting for transfers between devices: 40.6 us -> 35.3 us  [shards(): lax.psum_scatter(jnp.dot(activated, w_down, preferred_element_type=jnp.fl...]
where the time goes in v3:
time: 394 us; the launch traced here: 391 us
  waiting for transfers between devices  198 us (50%)
  Pallas kernels  91.3 us (23%)
  matrix products  28 us (7%)
  local copies, waits for them, and re-layouts  26.1 us (7%)
  other arithmetic  24.4 us (6%)
  between operations  13.4 us (3%)
  starting transfers between devices  8.85 us (2%)
    pallas_call x1, Pallas kernels, paged_attention(): pl.pallas_call(paged_kernel, grid_spec=grid_spec, out_shape=jax.ShapeDtyp...  91.3 us
    all_to_all x1, waiting for transfers between devices, shards(): lax.all_to_all(outgoing, 'seq', split_axis=0, concat_axis=0, tiled=True)  64.7 us
    reduce_scatter x1, waiting for transfers between devices, shards(): lax.psum_scatter(jnp.dot(attended, w_out, preferred_element_type=jnp.floa...  42.3 us
    reduce_scatter x1, waiting for transfers between devices, shards(): lax.psum_scatter(jnp.dot(activated, w_down, preferred_element_type=jnp.fl...  35.3 us
    all_gather x1, waiting for transfers between devices, shards(): page_store = lax.all_gather(shared_pages, 'seq', axis=0, tiled=True)  30.3 us
    all_gather x1, waiting for transfers between devices, shards(): normed_ffn = lax.all_gather(normed_own, 'tp', axis=0, tiled=True)  25 us
    dot_general x1, matrix products, shards(): jnp.dot(activated, w_down, preferred_element_type=jnp.float32)  11.7 us
    all_to_all x1, starting transfers between devices, shards(): lax.all_to_all(outgoing, 'seq', split_axis=0, concat_axis=0, tiled=True)  8.32 us
  transfers between devices with their start and end apart: 5, of which 5 were waited for; matrix products, arithmetic and copies ran while one was open for 12% of the time, Pallas kernels for 0%

profile of v3, /device:TPU:0, one launch (start us, length us, event | category | flops | bytes accessed | tf_op | source)
XLA Modules:
  0.0 390.6 jit_solution(14342111392642678691)
XLA Ops:
  6.5 0.7 all-gather.3.cloned.1.call-update
  7.3 0.7 reshape.335
  8.0 0.7 reshape.336
  8.8 0.8 copy.95
  10.3 0.8 gather_fusion.9
  13.6 3.5 gather_fusion.11
  17.1 5.5 %select_select_fusion = bf16[16,8,1,2,80,128]{5,4,3,1,2,0:T(8,128)(2,1)} fusion(bf16[16,8,1,2,80,128]{5,4,3,1,2,0:T(8,128)(2,1)} %bitcast.84, pred[16]{0:T(512)(128)(4,1)S(1)} %reduce_or.9, pred[16,8]{1,0:T(8,128)(4,1)S(1)} %get-tuple-element.7), kind=kLoop, calls=%fused_computation.18 | loop fusion | flops 5242880 | bytes 10485904 | tf_op jit(solution)/shard_map/jit(_where)/select_n | solution.py:291
  22.6 8.3 %all-to-all-start = ((bf16[16,8,1,2,80,128]{5,4,3,1,2,0:T(8,128)(2,1)}), bf16[16,8,1,2,80,128]{5,4,3,1,2,0:T(8,128)(2,1)}, u32[]{:S(2)}, u32[]{:S(2)}) async-start(bf16[16,8,1,2,80,128]{5,4,3,1,2,0:T(8,128)(2,1)} %select_select_fusion), calls=%async_computation | async-start | bytes 10485760 | tf_op jit(solution)/shard_map/all_to_all | solution.py:294
  35.9 3.4 fusion
  39.7 1.5 fusion.39
  41.2 1.1 fusion.3
  42.4 1.0 copy.91
  43.4 4.8 %fusion.2 = bf16[128,4,2560]{2,1,0:T(4,128)(2,1)} fusion(bf16[128,4,2560]{2,1,0:T(4,128)(2,1)} %param.21, f32[2560]{0:T(1024)S(1)} %convert_element_type.51, f32[128,4]{1,0:T(8,128)S(1)} %add_rsqrt_fusion), kind=kLoop, calls=%fused_computation.17 | loop fusion | flops 5242880 | bytes 5255168 | tf_op jit(solution)/shard_map/convert_element_type | solution.py:21
  48.2 5.4 %reshape.333 = bf16[512,2560]{1,0:T(8,128)(2,1)} reshape(bf16[128,4,2560]{2,1,0:T(4,128)(2,1)} %fusion.2) | data formatting | bytes 5242880 | tf_op jit(solution)/shard_map/reshape | solution.py:263
  53.6 2.7 convolution_convert_fusion.2
  59.4 2.7 fusion.7
  63.2 64.7 %all-to-all-done = bf16[16,8,1,2,80,128]{5,4,3,1,2,0:T(8,128)(2,1)} async-done(((bf16[16,8,1,2,80,128]{5,4,3,1,2,0:T(8,128)(2,1)}), bf16[16,8,1,2,80,128]{5,4,3,1,2,0:T(8,128)(2,1)}, u32[]{:S(2)}, u32[]{:S(2)}) %all-to-all-start) | async-done | bytes 5242912 | tf_op jit(solution)/shard_map/all_to_all | solution.py:294
  127.9 30.3 %all-gather.3.cloned.1.call-done = bf16[320,1,2,80,128]{4,3,2,1,0:T(8,128)(2,1)} async-done(((bf16[20,1,2,80,128]{4,3,2,1,0:T(8,128)(2,1)}), bf16[320,1,2,80,128]{4,3,2,1,0:T(8,128)(2,1)}) %all-gather.3.cloned.1.call-update) | async-done | bytes 13107216 | tf_op jit(solution)/shard_map/all_gather | solution.py:260
  158.2 91.3 %shard_map.199 = bf16[4,512,80]{2,1,0:T(8,128)(2,1)} custom-call(s32[4,40]{1,0:T(4,128)} %pad_add_fusion.tbl, s32[4,4]{1,0:T(4,128)} %pad_add_fusion.1.meta, bf16[4,512,80]{2,1,0:T(8,128)(2,1)} %bitcast.88, bf16[4,2,80,128]{3,2,1,0:T(8,128)(2,1)} %pad_maximum_fusion.fresh_ref, bf16[320,2,80,128]{3,2,1,0:T(8,128)(2,1)} %bitcast.94, ...), custom_call_target="tpu_custom_call" | custom-call | flops 3439329280 | bytes 6717440 | tf_op jit(solution)/shard_map/pallas_call | solution.py:203
  249.5 1.4 copy.110
  251.3 3.0 convolution_convert_fusion.1
  255.0 42.3 %reduce-scatter.3.cloned.1.call-done = bf16[64,2560]{1,0:T(8,128)(2,1)} async-done(((bf16[512,2560]{1,0:T(8,128)(2,1)}), bf16[64,2560]{1,0:T(8,128)(2,1)}) %reduce-scatter.3.cloned.1.call-update) | async-done | bytes 327696 | tf_op jit(solution)/shard_map/reduce_scatter | solution.py:319
  297.4 1.2 reshape.347
  298.5 1.3 multiply_reduce_fusion
  299.8 1.2 multiply_convert_fusion.1
  301.1 0.8 reshape.343
  301.9 25.0 %all-gather.5.cloned.1.call-done = bf16[512,2560]{1,0:T(8,128)(2,1)} async-done(((bf16[64,2560]{1,0:T(8,128)(2,1)}), bf16[512,2560]{1,0:T(8,128)(2,1)}) %all-gather.5.cloned.1.call-update) | async-done | bytes 2621456 | tf_op jit(solution)/shard_map/all_gather | solution.py:331
  327.0 6.8 %fusion.28 = f32[512,864]{0,1:T(8,128)} fusion(bf16[512,2560]{1,0:T(8,128)(2,1)} %all-gather.5.cloned.1.call-done, bf16[2560,864]{0,1:T(8,128)(2,1)} %param.28), kind=kOutput, calls=%fused_computation.98 | convolution fusion | flops 2264924160 | bytes 8814592 | tf_op jit(solution)/shard_map/dot_general | solution.py:332
  333.8 11.7 %convolution_convert_fusion = bf16[512,2560]{1,0:T(8,128)(2,1)} fusion(bf16[864,2560]{1,0:T(8,128)(2,1)} %param.30, f32[512,864]{0,1:T(8,128)} %fusion.28, bf16[512,2560]{1,0:T(8,128)(2,1)} %all-gather.5.cloned.1.call-done, bf16[2560,864]{0,1:T(8,128)(2,1)} %param.29), kind=kOutput, calls=%fused_computation.19 | convolution fusion | flops 4533813248 | bytes 15859712 | tf_op jit(solution)/shard_map/dot_general | solution.py:337
  345.5 35.3 %reduce-scatter.5.cloned.1.call-done = bf16[64,2560]{1,0:T(8,128)(2,1)} async-done(((bf16[512,2560]{1,0:T(8,128)(2,1)}), bf16[64,2560]{1,0:T(8,128)(2,1)}) %reduce-scatter.5.cloned.1.call-update) | async-done | bytes 327696 | tf_op jit(solution)/shard_map/reduce_scatter | solution.py:336
  380.8 1.2 reshape.349
  382.0 2.0 fusion.21
  (102 shorter events, 13.9 us)
Async XLA Ops:
  6.5 244.7 %copy-start = (bf16[320,2560]{1,0:T(8,128)(2,1)S(1)}, bf16[320,2560]{1,0:T(8,128)(2,1)}, u32[]{:S(2)}) copy-start(bf16[320,2560]{1,0:T(8,128)(2,1)} %param.26) | copy-start | bytes 4915204
  6.5 151.7 %all-gather.3.cloned.1.call-start = ((), (), s32[]{:S(2)}) async-start(), calls=%async_computation.3 | async-start | bytes 13926400 | tf_op jit(solution)/shard_map/all_gather | solution.py:260
  10.3 3.3 copy-start.8
  22.6 8.6 %copy-start.1 = (s32[64]{0:T(128)S(1)}, s32[64]{0:T(128)}, u32[]{:S(2)}) copy-start(s32[64]{0:T(128)} %param.41) | copy-start | bytes 772
  22.6 9.9 %copy-start.2 = (s32[64]{0:T(128)S(1)}, s32[64]{0:T(128)}, u32[]{:S(2)}) copy-start(s32[64]{0:T(128)} %param.40) | copy-start | bytes 772
  22.6 10.6 %copy-start.3 = (s32[16]{0:T(128)S(1)}, s32[16]{0:T(128)}, u32[]{:S(2)}) copy-start(s32[16]{0:T(128)} %param.39) | copy-start | bytes 196
  22.6 11.2 %copy-start.4 = (s32[16]{0:T(128)S(1)}, s32[16]{0:T(128)}, u32[]{:S(2)}) copy-start(s32[16]{0:T(128)} %param.37) | copy-start | bytes 196
  22.6 105.3 %all-to-all-start = ((bf16[16,8,1,2,80,128]{5,4,3,1,2,0:T(8,128)(2,1)}), bf16[16,8,1,2,80,128]{5,4,3,1,2,0:T(8,128)(2,1)}, u32[]{:S(2)}, u32[]{:S(2)}) async-start(bf16[16,8,1,2,80,128]{5,4,3,1,2,0:T(8,128)(2,1)} %select_select_fusion), calls=%async_computation | async-start | bytes 10485760 | tf_op jit(solution)/shard_map/all_to_all | solution.py:294
  30.9 3.6 copy-start.5
  31.0 4.2 %copy-start.12 = (bf16[2560]{0:T(1024)(128)(2,1)S(1)}, bf16[2560]{0:T(1024)(128)(2,1)}, u32[]{:S(2)}) copy-start(bf16[2560]{0:T(1024)(128)(2,1)} %param.22) | copy-start | bytes 15364
  31.0 4.2 %copy-start.6 = (s32[4]{0:T(128)S(1)}, s32[4]{0:T(128)}, u32[]{:S(2)}) copy-start(s32[4]{0:T(128)} %param.36) | copy-start | bytes 52
  31.0 266.4 %reduce-scatter.3.cloned.1.call-start = ((), (), s32[]{:S(2)}) async-start(), calls=%async_computation.4 | async-start | bytes 2949120 | tf_op jit(solution)/shard_map/reduce_scatter | solution.py:319
  35.8 3.9 copy-start.7
  39.7 1.5 copy-start.14
  48.2 5.4 %copy-start.9 = (bf16[2560,80]{0,1:T(8,128)(2,1)S(1)}, bf16[2560,80]{0,1:T(8,128)(2,1)}, u32[]{:S(2)}) copy-start(bf16[2560,80]{0,1:T(8,128)(2,1)} %param.25) | copy-start | bytes 1228804
  53.6 3.3 copy-start.10
  53.6 3.8 copy-start.11
  53.6 5.8 %copy-start.15 = (bf16[2560,80]{0,1:T(8,128)(2,1)S(1)}, bf16[2560,80]{0,1:T(8,128)(2,1)}, u32[]{:S(2)}) copy-start(bf16[2560,80]{0,1:T(8,128)(2,1)} %param.24) | copy-start | bytes 1228804
  254.3 0.7 copy-start.13
  254.3 72.6 %all-gather.5.cloned.1.call-start = ((), (), s32[]{:S(2)}) async-start(), calls=%async_computation.5 | async-start | bytes 2949120 | tf_op jit(solution)/shard_map/all_gather | solution.py:331
  301.9 78.9 %reduce-scatter.5.cloned.1.call-start = ((), (), s32[]{:S(2)}) async-start(), calls=%async_computation.6 | async-start | bytes 2949120 | tf_op jit(solution)/shard_map/reduce_scatter | solution.py:336
Sparse Core Ops, SparseCore 0:
  9.5 148.6 all-gather.2
  254.5 42.8 reduce-scatter.2
  302.0 24.9 all-gather.4
  345.6 35.1 reduce-scatter.4

commit v4 on v3

--- a/solution.py
+++ b/solution.py
@@ -78,12 +78,15 @@
 LEAF_SLOTS = 8
 
 
-def paged_kernel(tbl, meta, q_ref, fresh_ref, shared_hbm, leaf_hbm, out_ref, kv, sc, sem):
-    i = pl.program_id(0)
-    steps = pl.num_programs(0)
-    slot = i % 2
+def paged_kernel(tbl, meta, q_ref, fresh_ref, shared_hbm, leaf_hbm, out_ref, kv, sc, fresh_sc, top, mass, acc, sem):
+    b = pl.program_id(0)
+    h = pl.program_id(1)
+    requests = pl.num_programs(0)
+    slot = b % 2
     shared_count = ROOT_PAGES + MID_PAGES
     page_count = shared_count + LEAF_SLOTS
+    width = kv.shape[-1]
+    span = 2 * width
 
     def start_request(j, into):
         def shared_body(p, carry):
@@ -97,106 +100,137 @@
         lax.fori_loop(0, shared_count, shared_body, 0)
         lax.fori_loop(shared_count, page_count, leaf_body, 0)
 
-    @pl.when(i == 0)
+    @pl.when((h == 0) & (b == 0))
     def _():
         start_request(0, 0)
 
-    @pl.when(i + 1 < steps)
+    @pl.when((h == 0) & (b + 1 < requests))
     def _():
-        start_request(i + 1, 1 - slot)
-
-    def wait_body(p, carry):
-        pltpu.make_async_copy(shared_hbm.at[0], kv.at[slot, p], sem.at[slot]).wait()
-        return carry
-
-    lax.fori_loop(0, page_count, wait_body, 0)
-
-    root_span = meta[i, 0]
-    mid_span = meta[i, 1]
-    leaf_span = meta[i, 2]
-    context = meta[i, 3]
+        start_request(b + 1, 1 - slot)
+
+    @pl.when(h == 0)
+    def _():
+        def wait_body(p, carry):
+            pltpu.make_async_copy(shared_hbm.at[0], kv.at[slot, p], sem.at[slot]).wait()
+            return carry
+
+        lax.fori_loop(0, page_count, wait_body, 0)
+
+    root_span = meta[b, 0]
+    mid_span = meta[b, 1]
+    leaf_span = meta[b, 2]
+    context = meta[b, 3]
     q = q_ref[0]
-    rows, width = q.shape[0], kv.shape[-1]
-    query_pos = context + (lax.broadcasted_iota(jnp.int32, (rows, 1), 0) % width)
-    lanes = lax.broadcasted_iota(jnp.int32, (1, width), 1)
+    rows = q.shape[0]
+    query_pos = context + lax.broadcasted_iota(jnp.int32, (rows, 1), 0)
+    lanes = lax.broadcasted_iota(jnp.int32, (1, span), 1)
     scale = HD ** (-0.5)
 
-    def scores_of(keys, key_pos, present):
-        s = jnp.dot(q, keys, preferred_element_type=jnp.float32) * scale
+    def masked(s, key_pos, present):
         distance = query_pos - key_pos
         allowed = present & (distance >= 0) & (distance < WINDOW)
         return jnp.where(allowed, s, masked_score)
 
     def geometry(c):
-        in_root = c < ROOT_PAGES
-        in_mid = c < shared_count
+        page = 2 * c
+        in_root = page < ROOT_PAGES
+        in_mid = page < shared_count
         first = jnp.where(
-            in_root, c * width, jnp.where(in_mid, (c - ROOT_PAGES) * width, (c - shared_count) * width)
+            in_root, page * width, jnp.where(in_mid, (page - ROOT_PAGES) * width, (page - shared_count) * width)
         )
         base = jnp.where(in_root, 0, jnp.where(in_mid, root_span, root_span + mid_span))
         limit = jnp.where(in_root, root_span, jnp.where(in_mid, mid_span, leaf_span))
         return first, base, limit
 
-    fresh_scores = scores_of(fresh_ref[0, 0], context + lanes, lanes >= 0)
-    sc[page_count] = fresh_scores
-    maximum = jnp.max(fresh_scores, -1, keepdims=True)
-
-    def max_body(c, running):
+    def pair(c, part):
+        return jnp.concatenate([kv[slot, 2 * c, part], kv[slot, 2 * c + 1, part]], 1)
+
+    fresh_lanes = lax.broadcasted_iota(jnp.int32, (1, width), 1)
+    fresh_scores = masked(
+        jnp.dot(q, fresh_ref[0, 0], preferred_element_type=jnp.float32) * scale,
+        context + fresh_lanes,
+        fresh_lanes >= 0,
+    )
+    fresh_sc[...] = fresh_scores
+    top[...] = fresh_scores
+
+    def keep(c, s):
+        sc[c] = s
+        top[...] = jnp.maximum(top[...], jnp.maximum(s[:, :width], s[:, width:]))
+
+    def max_body(c, carry):
         first, base, limit = geometry(c)
-
-        def live():
+        live = first < limit
+        full = (first + span <= limit) & (context + rows - 1 - (base + first) < WINDOW)
+
+        @pl.when(full)
+        def _():
+            keep(c, jnp.dot(q, pair(c, 0), preferred_element_type=jnp.float32) * scale)
+
+        @pl.when(live & jnp.logical_not(full))
+        def _():
             steps_in = first + lanes
-            s = scores_of(kv[slot, c, 0], base + steps_in, steps_in < limit)
-            sc[c] = s
-            return jnp.maximum(running, jnp.max(s, -1, keepdims=True))
-
-        return lax.cond(first < limit, live, lambda: running)
-
-    maximum = lax.fori_loop(0, page_count, max_body, maximum)
-
-    def weigh(s, values, totals, acc):
-        w = jnp.exp(s - maximum)
-        totals = totals + jnp.sum(w, -1, keepdims=True)
-        acc = acc + lax.dot_general(
-            w.astype(jnp.bfloat16), values, (((1,), (1,)), ((), ())), preferred_element_type=jnp.float32
-        )
-        return totals, acc
-
-    carry = weigh(
-        sc[page_count],
-        fresh_ref[0, 1],
-        jnp.zeros((rows, 1), jnp.float32),
-        jnp.zeros((rows, q.shape[1]), jnp.float32),
+            s = jnp.dot(q, pair(c, 0), preferred_element_type=jnp.float32) * scale
+            keep(c, masked(s, base + steps_in, steps_in < limit))
+
+        return carry
+
+    chunks = page_count // 2
+    lax.fori_loop(0, chunks, max_body, 0)
+    top[...] = jnp.broadcast_to(jnp.max(top[...], -1, keepdims=True), top.shape)
+    row_top = top[...]
+
+    fresh_w = jnp.exp(fresh_sc[...] - row_top)
+    mass[...] = fresh_w
+    acc[...] = lax.dot_general(
+        fresh_w.astype(jnp.bfloat16), fresh_ref[0, 1], (((1,), (1,)), ((), ())), preferred_element_type=jnp.float32
     )
 
     def sum_body(c, carry):
         first, base, limit = geometry(c)
-        return lax.cond(
-            first < limit, lambda: weigh(sc[c], kv[slot, c, 1], *carry), lambda: carry
-        )
-
-    totals, acc = lax.fori_loop(0, page_count, sum_body, carry)
-    out_ref[0] = (acc / totals).astype(out_ref.dtype)
+
+        @pl.when(first < limit)
+        def _():
+            s = sc[c]
+            w0 = jnp.exp(s[:, :width] - row_top)
+            w1 = jnp.exp(s[:, width:] - row_top)
+            mass[...] = mass[...] + w0 + w1
+            w = jnp.concatenate([w0, w1], 1).astype(jnp.bfloat16)
+            acc[...] = acc[...] + lax.dot_general(
+                w, pair(c, 1), (((1,), (1,)), ((), ())), preferred_element_type=jnp.float32
+            )
+
+        return carry
+
+    lax.fori_loop(0, chunks, sum_body, 0)
+    totals = jnp.sum(mass[...], -1, keepdims=True)
+    out_ref[0] = (acc[...] / totals).astype(out_ref.dtype)
 
 
 def paged_attention(tbl, meta, queries, fresh, shared_store, leaf_store):
     reqs, rows, head = queries.shape
     page_shape = shared_store.shape[1:]
+    width = page_shape[-1]
+    groups = rows // width
     pages = tbl.shape[1]
-    keys_total = (pages + 1) * page_shape[-1]
+    keys_total = (pages + 1) * width
     grid_spec = pltpu.PrefetchScalarGridSpec(
         num_scalar_prefetch=2,
-        grid=(reqs,),
+        grid=(reqs, groups),
         in_specs=[
-            pl.BlockSpec((1, rows, head), lambda i, t, m: (i, 0, 0)),
-            pl.BlockSpec((1,) + page_shape, lambda i, t, m: (i, 0, 0, 0)),
+            pl.BlockSpec((1, width, head), lambda i, g, t, m: (i, g, 0)),
+            pl.BlockSpec((1,) + page_shape, lambda i, g, t, m: (i, 0, 0, 0)),
             pl.BlockSpec(memory_space=pl.ANY),
             pl.BlockSpec(memory_space=pl.ANY),
         ],
-        out_specs=pl.BlockSpec((1, rows, head), lambda i, t, m: (i, 0, 0)),
+        out_specs=pl.BlockSpec((1, width, head), lambda i, g, t, m: (i, g, 0)),
         scratch_shapes=[
             pltpu.VMEM((2, pages) + page_shape, shared_store.dtype),
-            pltpu.VMEM((pages + 1, rows, page_shape[-1]), jnp.float32),
+            pltpu.VMEM((pages // 2, width, 2 * width), jnp.float32),
+            pltpu.VMEM((width, width), jnp.float32),
+            pltpu.VMEM((width, width), jnp.float32),
+            pltpu.VMEM((width, width), jnp.float32),
+            pltpu.VMEM((width, head), jnp.float32),
             pltpu.SemaphoreType.DMA((2,)),
         ],
     )
@@ -204,11 +238,11 @@
         paged_kernel,
         grid_spec=grid_spec,
         out_shape=jax.ShapeDtypeStruct((reqs, rows, head), jnp.bfloat16),
-        compiler_params=pltpu.CompilerParams(dimension_semantics=("arbitrary",)),
+        compiler_params=pltpu.CompilerParams(dimension_semantics=("arbitrary", "arbitrary")),
         cost_estimate=pl.CostEstimate(
             flops=4 * reqs * rows * keys_total * head,
             transcendentals=reqs * rows * keys_total,
-            bytes_accessed=reqs * (pages + 1) * 2 * head * page_shape[-1] * 2,
+            bytes_accessed=reqs * (pages + 1) * 2 * head * width * 2,
         ),
     )(tbl, meta, queries, fresh, shared_store, leaf_store)
 

time: 394 us -> 389 us (0.987)
  no operation moved by 1% of the time
where the time goes in v4:
time: 389 us; the launch traced here: 385 us
  waiting for transfers between devices  196 us (50%)
  Pallas kernels  88 us (23%)
  matrix products  28 us (7%)
  local copies, waits for them, and re-layouts  26.3 us (7%)
  other arithmetic  24.4 us (6%)
  between operations  13.4 us (3%)
  starting transfers between devices  8.85 us (2%)
    pallas_call x1, Pallas kernels, paged_attention(): pl.pallas_call(paged_kernel, grid_spec=grid_spec, out_shape=jax.ShapeDtyp...  88 us
    all_to_all x1, waiting for transfers between devices, shards(): lax.all_to_all(outgoing, 'seq', split_axis=0, concat_axis=0, tiled=True)  64.7 us
    reduce_scatter x1, waiting for transfers between devices, shards(): lax.psum_scatter(jnp.dot(attended, w_out, preferred_element_type=jnp.floa...  39.6 us
    reduce_scatter x1, waiting for transfers between devices, shards(): lax.psum_scatter(jnp.dot(activated, w_down, preferred_element_type=jnp.fl...  35.3 us
    all_gather x1, waiting for transfers between devices, shards(): page_store = lax.all_gather(shared_pages, 'seq', axis=0, tiled=True)  30.3 us
    all_gather x1, waiting for transfers between devices, shards(): normed_ffn = lax.all_gather(normed_own, 'tp', axis=0, tiled=True)  24.8 us
    dot_general x1, matrix products, shards(): jnp.dot(activated, w_down, preferred_element_type=jnp.float32)  11.7 us
    all_to_all x1, starting transfers between devices, shards(): lax.all_to_all(outgoing, 'seq', split_axis=0, concat_axis=0, tiled=True)  8.32 us
  transfers between devices with their start and end apart: 5, of which 5 were waited for; matrix products, arithmetic and copies ran while one was open for 12% of the time, Pallas kernels for 0%

profile of v4, /device:TPU:0, one launch (start us, length us, event | category | flops | bytes accessed | tf_op | source)
XLA Modules:
  0.0 384.6 jit_solution(9459886626599702630)
XLA Ops:
  6.5 0.7 all-gather.3.cloned.1.call-update
  7.3 0.7 reshape.335
  8.0 0.7 reshape.336
  8.8 0.8 copy.95
  10.3 0.8 gather_fusion.9
  13.6 3.5 gather_fusion.11
  17.1 5.5 %select_select_fusion = bf16[16,8,1,2,80,128]{5,4,3,1,2,0:T(8,128)(2,1)} fusion(bf16[16,8,1,2,80,128]{5,4,3,1,2,0:T(8,128)(2,1)} %bitcast.84, pred[16]{0:T(512)(128)(4,1)S(1)} %reduce_or.9, pred[16,8]{1,0:T(8,128)(4,1)S(1)} %get-tuple-element.7), kind=kLoop, calls=%fused_computation.18 | loop fusion | flops 5242880 | bytes 10485904 | tf_op jit(solution)/shard_map/jit(_where)/select_n | solution.py:325
  22.6 8.3 %all-to-all-start = ((bf16[16,8,1,2,80,128]{5,4,3,1,2,0:T(8,128)(2,1)}), bf16[16,8,1,2,80,128]{5,4,3,1,2,0:T(8,128)(2,1)}, u32[]{:S(2)}, u32[]{:S(2)}) async-start(bf16[16,8,1,2,80,128]{5,4,3,1,2,0:T(8,128)(2,1)} %select_select_fusion), calls=%async_computation | async-start | bytes 10485760 | tf_op jit(solution)/shard_map/all_to_all | solution.py:328
  35.9 3.4 fusion
  39.7 1.5 fusion.39
  41.2 1.1 fusion.3
  42.4 1.0 copy.91
  43.4 4.8 %fusion.2 = bf16[128,4,2560]{2,1,0:T(4,128)(2,1)} fusion(bf16[128,4,2560]{2,1,0:T(4,128)(2,1)} %param.21, f32[2560]{0:T(1024)S(1)} %convert_element_type.51, f32[128,4]{1,0:T(8,128)S(1)} %add_rsqrt_fusion), kind=kLoop, calls=%fused_computation.17 | loop fusion | flops 5242880 | bytes 5255168 | tf_op jit(solution)/shard_map/convert_element_type | solution.py:21
  48.2 5.4 %reshape.333 = bf16[512,2560]{1,0:T(8,128)(2,1)} reshape(bf16[128,4,2560]{2,1,0:T(4,128)(2,1)} %fusion.2) | data formatting | bytes 5242880 | tf_op jit(solution)/shard_map/reshape | solution.py:297
  53.6 2.7 convolution_convert_fusion.2
  59.4 2.7 fusion.7
  63.2 64.7 %all-to-all-done = bf16[16,8,1,2,80,128]{5,4,3,1,2,0:T(8,128)(2,1)} async-done(((bf16[16,8,1,2,80,128]{5,4,3,1,2,0:T(8,128)(2,1)}), bf16[16,8,1,2,80,128]{5,4,3,1,2,0:T(8,128)(2,1)}, u32[]{:S(2)}, u32[]{:S(2)}) %all-to-all-start) | async-done | bytes 5242912 | tf_op jit(solution)/shard_map/all_to_all | solution.py:328
  127.9 30.3 %all-gather.3.cloned.1.call-done = bf16[320,1,2,80,128]{4,3,2,1,0:T(8,128)(2,1)} async-done(((bf16[20,1,2,80,128]{4,3,2,1,0:T(8,128)(2,1)}), bf16[320,1,2,80,128]{4,3,2,1,0:T(8,128)(2,1)}) %all-gather.3.cloned.1.call-update) | async-done | bytes 13107216 | tf_op jit(solution)/shard_map/all_gather | solution.py:294
  158.2 88.0 %shard_map.199 = bf16[4,512,80]{2,1,0:T(8,128)(2,1)} custom-call(s32[4,40]{1,0:T(4,128)} %pad_add_fusion.tbl, s32[4,4]{1,0:T(4,128)} %pad_add_fusion.1.meta, bf16[4,512,80]{2,1,0:T(8,128)(2,1)} %bitcast.88, bf16[4,2,80,128]{3,2,1,0:T(8,128)(2,1)} %pad_maximum_fusion.fresh_ref, bf16[320,2,80,128]{3,2,1,0:T(8,128)(2,1)} %bitcast.94, ...), custom_call_target="tpu_custom_call" | custom-call | flops 3439329280 | bytes 6717440 | tf_op jit(solution)/shard_map/pallas_call | solution.py:237
  246.2 1.4 copy.110
  248.0 3.0 convolution_convert_fusion.1
  251.8 39.6 %reduce-scatter.3.cloned.1.call-done = bf16[64,2560]{1,0:T(8,128)(2,1)} async-done(((bf16[512,2560]{1,0:T(8,128)(2,1)}), bf16[64,2560]{1,0:T(8,128)(2,1)}) %reduce-scatter.3.cloned.1.call-update) | async-done | bytes 327696 | tf_op jit(solution)/shard_map/reduce_scatter | solution.py:353
  291.4 1.2 reshape.347
  292.6 1.3 multiply_reduce_fusion
  293.9 1.2 multiply_convert_fusion.1
  295.1 0.8 reshape.343
  296.2 24.8 %all-gather.5.cloned.1.call-done = bf16[512,2560]{1,0:T(8,128)(2,1)} async-done(((bf16[64,2560]{1,0:T(8,128)(2,1)}), bf16[512,2560]{1,0:T(8,128)(2,1)}) %all-gather.5.cloned.1.call-update) | async-done | bytes 2621456 | tf_op jit(solution)/shard_map/all_gather | solution.py:365
  321.0 6.8 %fusion.28 = f32[512,864]{0,1:T(8,128)} fusion(bf16[512,2560]{1,0:T(8,128)(2,1)} %all-gather.5.cloned.1.call-done, bf16[2560,864]{0,1:T(8,128)(2,1)} %param.28), kind=kOutput, calls=%fused_computation.98 | convolution fusion | flops 2264924160 | bytes 8814592 | tf_op jit(solution)/shard_map/dot_general | solution.py:366
  327.8 11.7 %convolution_convert_fusion = bf16[512,2560]{1,0:T(8,128)(2,1)} fusion(bf16[864,2560]{1,0:T(8,128)(2,1)} %param.30, f32[512,864]{0,1:T(8,128)} %fusion.28, bf16[512,2560]{1,0:T(8,128)(2,1)} %all-gather.5.cloned.1.call-done, bf16[2560,864]{0,1:T(8,128)(2,1)} %param.29), kind=kOutput, calls=%fused_computation.19 | convolution fusion | flops 4533813248 | bytes 15859712 | tf_op jit(solution)/shard_map/dot_general | solution.py:371
  339.5 35.3 %reduce-scatter.5.cloned.1.call-done = bf16[64,2560]{1,0:T(8,128)(2,1)} async-done(((bf16[512,2560]{1,0:T(8,128)(2,1)}), bf16[64,2560]{1,0:T(8,128)(2,1)}) %reduce-scatter.5.cloned.1.call-update) | async-done | bytes 327696 | tf_op jit(solution)/shard_map/reduce_scatter | solution.py:370
  374.8 1.2 reshape.349
  376.0 2.0 fusion.21
  (102 shorter events, 14.1 us)
Async XLA Ops:
  6.5 241.5 %copy-start = (bf16[320,2560]{1,0:T(8,128)(2,1)S(1)}, bf16[320,2560]{1,0:T(8,128)(2,1)}, u32[]{:S(2)}) copy-start(bf16[320,2560]{1,0:T(8,128)(2,1)} %param.26) | copy-start | bytes 4915204
  6.5 151.7 %all-gather.3.cloned.1.call-start = ((), (), s32[]{:S(2)}) async-start(), calls=%async_computation.3 | async-start | bytes 13926400 | tf_op jit(solution)/shard_map/all_gather | solution.py:294
  10.3 3.3 copy-start.8
  22.6 8.6 %copy-start.1 = (s32[64]{0:T(128)S(1)}, s32[64]{0:T(128)}, u32[]{:S(2)}) copy-start(s32[64]{0:T(128)} %param.41) | copy-start | bytes 772
  22.6 9.9 %copy-start.2 = (s32[64]{0:T(128)S(1)}, s32[64]{0:T(128)}, u32[]{:S(2)}) copy-start(s32[64]{0:T(128)} %param.40) | copy-start | bytes 772
  22.6 10.6 %copy-start.3 = (s32[16]{0:T(128)S(1)}, s32[16]{0:T(128)}, u32[]{:S(2)}) copy-start(s32[16]{0:T(128)} %param.39) | copy-start | bytes 196
  22.6 11.2 %copy-start.4 = (s32[16]{0:T(128)S(1)}, s32[16]{0:T(128)}, u32[]{:S(2)}) copy-start(s32[16]{0:T(128)} %param.37) | copy-start | bytes 196
  22.6 105.3 %all-to-all-start = ((bf16[16,8,1,2,80,128]{5,4,3,1,2,0:T(8,128)(2,1)}), bf16[16,8,1,2,80,128]{5,4,3,1,2,0:T(8,128)(2,1)}, u32[]{:S(2)}, u32[]{:S(2)}) async-start(bf16[16,8,1,2,80,128]{5,4,3,1,2,0:T(8,128)(2,1)} %select_select_fusion), calls=%async_computation | async-start | bytes 10485760 | tf_op jit(solution)/shard_map/all_to_all | solution.py:328
  30.9 3.6 copy-start.5
  31.0 4.2 %copy-start.12 = (bf16[2560]{0:T(1024)(128)(2,1)S(1)}, bf16[2560]{0:T(1024)(128)(2,1)}, u32[]{:S(2)}) copy-start(bf16[2560]{0:T(1024)(128)(2,1)} %param.22) | copy-start | bytes 15364
  31.0 4.2 %copy-start.6 = (s32[4]{0:T(128)S(1)}, s32[4]{0:T(128)}, u32[]{:S(2)}) copy-start(s32[4]{0:T(128)} %param.36) | copy-start | bytes 52
  31.0 260.4 %reduce-scatter.3.cloned.1.call-start = ((), (), s32[]{:S(2)}) async-start(), calls=%async_computation.4 | async-start | bytes 2949120 | tf_op jit(solution)/shard_map/reduce_scatter | solution.py:353
  35.8 3.9 %copy-start.7 = (bf16[128,4,2560]{2,1,0:T(4,128)(2,1)S(1)}, bf16[128,4,2560]{2,1,0:T(4,128)(2,1)}, u32[]{:S(2)}) copy-start(bf16[128,4,2560]{2,1,0:T(4,128)(2,1)} %param.21) | copy-start | bytes 7864324
  39.7 1.5 copy-start.14
  48.2 5.4 %copy-start.9 = (bf16[2560,80]{0,1:T(8,128)(2,1)S(1)}, bf16[2560,80]{0,1:T(8,128)(2,1)}, u32[]{:S(2)}) copy-start(bf16[2560,80]{0,1:T(8,128)(2,1)} %param.25) | copy-start | bytes 1228804
  53.6 3.3 copy-start.10
  53.6 3.8 copy-start.11
  53.6 5.8 %copy-start.15 = (bf16[2560,80]{0,1:T(8,128)(2,1)S(1)}, bf16[2560,80]{0,1:T(8,128)(2,1)}, u32[]{:S(2)}) copy-start(bf16[2560,80]{0,1:T(8,128)(2,1)} %param.24) | copy-start | bytes 1228804
  251.1 0.7 copy-start.13
  251.1 69.9 %all-gather.5.cloned.1.call-start = ((), (), s32[]{:S(2)}) async-start(), calls=%async_computation.5 | async-start | bytes 2949120 | tf_op jit(solution)/shard_map/all_gather | solution.py:365
  295.9 78.9 %reduce-scatter.5.cloned.1.call-start = ((), (), s32[]{:S(2)}) async-start(), calls=%async_computation.6 | async-start | bytes 2949120 | tf_op jit(solution)/shard_map/reduce_scatter | solution.py:370
Sparse Core Ops, SparseCore 0:
  9.5 148.6 all-gather.2
  251.2 40.1 reduce-scatter.2
  296.0 24.9 all-gather.4
  339.6 35.1 reduce-scatter.4

commit v5 on v4

--- a/solution.py
+++ b/solution.py
@@ -76,17 +76,18 @@
 ROOT_PAGES = 16
 MID_PAGES = 16
 LEAF_SLOTS = 8
+CHUNK_PAGES = 4
 
 
 def paged_kernel(tbl, meta, q_ref, fresh_ref, shared_hbm, leaf_hbm, out_ref, kv, sc, fresh_sc, top, mass, acc, sem):
     b = pl.program_id(0)
-    h = pl.program_id(1)
     requests = pl.num_programs(0)
     slot = b % 2
     shared_count = ROOT_PAGES + MID_PAGES
     page_count = shared_count + LEAF_SLOTS
     width = kv.shape[-1]
-    span = 2 * width
+    group = CHUNK_PAGES
+    span = group * width
 
     def start_request(j, into):
         def shared_body(p, carry):
@@ -100,21 +101,19 @@
         lax.fori_loop(0, shared_count, shared_body, 0)
         lax.fori_loop(shared_count, page_count, leaf_body, 0)
 
-    @pl.when((h == 0) & (b == 0))
+    @pl.when(b == 0)
     def _():
         start_request(0, 0)
 
-    @pl.when((h == 0) & (b + 1 < requests))
+    @pl.when(b + 1 < requests)
     def _():
         start_request(b + 1, 1 - slot)
 
-    @pl.when(h == 0)
-    def _():
-        def wait_body(p, carry):
-            pltpu.make_async_copy(shared_hbm.at[0], kv.at[slot, p], sem.at[slot]).wait()
-            return carry
-
-        lax.fori_loop(0, page_count, wait_body, 0)
+    def wait_body(p, carry):
+        pltpu.make_async_copy(shared_hbm.at[0], kv.at[slot, p], sem.at[slot]).wait()
+        return carry
+
+    lax.fori_loop(0, page_count, wait_body, 0)
 
     root_span = meta[b, 0]
     mid_span = meta[b, 1]
@@ -122,7 +121,7 @@
     context = meta[b, 3]
     q = q_ref[0]
     rows = q.shape[0]
-    query_pos = context + lax.broadcasted_iota(jnp.int32, (rows, 1), 0)
+    query_pos = context + (lax.broadcasted_iota(jnp.int32, (rows, 1), 0) % width)
     lanes = lax.broadcasted_iota(jnp.int32, (1, span), 1)
     scale = HD ** (-0.5)
 
@@ -132,7 +131,7 @@
         return jnp.where(allowed, s, masked_score)
 
     def geometry(c):
-        page = 2 * c
+        page = group * c
         in_root = page < ROOT_PAGES
         in_mid = page < shared_count
         first = jnp.where(
@@ -142,8 +141,8 @@
         limit = jnp.where(in_root, root_span, jnp.where(in_mid, mid_span, leaf_span))
         return first, base, limit
 
-    def pair(c, part):
-        return jnp.concatenate([kv[slot, 2 * c, part], kv[slot, 2 * c + 1, part]], 1)
+    def pages_of(c, part):
+        return jnp.concatenate([kv[slot, group * c + k, part] for k in range(group)], 1)
 
     fresh_lanes = lax.broadcasted_iota(jnp.int32, (1, width), 1)
     fresh_scores = masked(
@@ -156,26 +155,29 @@
 
     def keep(c, s):
         sc[c] = s
-        top[...] = jnp.maximum(top[...], jnp.maximum(s[:, :width], s[:, width:]))
+        m = top[...]
+        for k in range(group):
+            m = jnp.maximum(m, s[:, k * width:(k + 1) * width])
+        top[...] = m
 
     def max_body(c, carry):
         first, base, limit = geometry(c)
-        live = first < limit
-        full = (first + span <= limit) & (context + rows - 1 - (base + first) < WINDOW)
+        live = (first < limit) & (context - (base + first + span - 1) < WINDOW)
+        full = (first + span <= limit) & (context + width - 1 - (base + first) < WINDOW)
 
         @pl.when(full)
         def _():
-            keep(c, jnp.dot(q, pair(c, 0), preferred_element_type=jnp.float32) * scale)
+            keep(c, jnp.dot(q, pages_of(c, 0), preferred_element_type=jnp.float32) * scale)
 
         @pl.when(live & jnp.logical_not(full))
         def _():
             steps_in = first + lanes
-            s = jnp.dot(q, pair(c, 0), preferred_element_type=jnp.float32) * scale
+            s = jnp.dot(q, pages_of(c, 0), preferred_element_type=jnp.float32) * scale
             keep(c, masked(s, base + steps_in, steps_in < limit))
 
         return carry
 
-    chunks = page_count // 2
+    chunks = page_count // group
     lax.fori_loop(0, chunks, max_body, 0)
     top[...] = jnp.broadcast_to(jnp.max(top[...], -1, keepdims=True), top.shape)
     row_top = top[...]
@@ -188,16 +190,19 @@
 
     def sum_body(c, carry):
         first, base, limit = geometry(c)
-
-        @pl.when(first < limit)
+        live = (first < limit) & (context - (base + first + span - 1) < WINDOW)
+
+        @pl.when(live)
         def _():
             s = sc[c]
-            w0 = jnp.exp(s[:, :width] - row_top)
-            w1 = jnp.exp(s[:, width:] - row_top)
-            mass[...] = mass[...] + w0 + w1
-            w = jnp.concatenate([w0, w1], 1).astype(jnp.bfloat16)
+            parts = [jnp.exp(s[:, k * width:(k + 1) * width] - row_top) for k in range(group)]
+            total = mass[...]
+            for part in parts:
+                total = total + part
+            mass[...] = total
+            w = jnp.concatenate(parts, 1).astype(jnp.bfloat16)
             acc[...] = acc[...] + lax.dot_general(
-                w, pair(c, 1), (((1,), (1,)), ((), ())), preferred_element_type=jnp.float32
+                w, pages_of(c, 1), (((1,), (1,)), ((), ())), preferred_element_type=jnp.float32
             )
 
         return carry
@@ -211,26 +216,25 @@
     reqs, rows, head = queries.shape
     page_shape = shared_store.shape[1:]
     width = page_shape[-1]
-    groups = rows // width
     pages = tbl.shape[1]
     keys_total = (pages + 1) * width
     grid_spec = pltpu.PrefetchScalarGridSpec(
         num_scalar_prefetch=2,
-        grid=(reqs, groups),
+        grid=(reqs,),
         in_specs=[
-            pl.BlockSpec((1, width, head), lambda i, g, t, m: (i, g, 0)),
-            pl.BlockSpec((1,) + page_shape, lambda i, g, t, m: (i, 0, 0, 0)),
+            pl.BlockSpec((1, rows, head), lambda i, t, m: (i, 0, 0)),
+            pl.BlockSpec((1,) + page_shape, lambda i, t, m: (i, 0, 0, 0)),
             pl.BlockSpec(memory_space=pl.ANY),
             pl.BlockSpec(memory_space=pl.ANY),
         ],
-        out_specs=pl.BlockSpec((1, width, head), lambda i, g, t, m: (i, g, 0)),
+        out_specs=pl.BlockSpec((1, rows, head), lambda i, t, m: (i, 0, 0)),
         scratch_shapes=[
             pltpu.VMEM((2, pages) + page_shape, shared_store.dtype),
-            pltpu.VMEM((pages // 2, width, 2 * width), jnp.float32),
-            pltpu.VMEM((width, width), jnp.float32),
-            pltpu.VMEM((width, width), jnp.float32),
-            pltpu.VMEM((width, width), jnp.float32),
-            pltpu.VMEM((width, head), jnp.float32),
+            pltpu.VMEM((pages // CHUNK_PAGES, rows, CHUNK_PAGES * width), jnp.float32),
+            pltpu.VMEM((rows, width), jnp.float32),
+            pltpu.VMEM((rows, width), jnp.float32),
+            pltpu.VMEM((rows, width), jnp.float32),
+            pltpu.VMEM((rows, head), jnp.float32),
             pltpu.SemaphoreType.DMA((2,)),
         ],
     )
@@ -238,7 +242,7 @@
         paged_kernel,
         grid_spec=grid_spec,
         out_shape=jax.ShapeDtypeStruct((reqs, rows, head), jnp.bfloat16),
-        compiler_params=pltpu.CompilerParams(dimension_semantics=("arbitrary", "arbitrary")),
+        compiler_params=pltpu.CompilerParams(dimension_semantics=("arbitrary",)),
         cost_estimate=pl.CostEstimate(
             flops=4 * reqs * rows * keys_total * head,
             transcendentals=reqs * rows * keys_total,

time: 389 us -> 323 us (0.83)
  Pallas kernels: 88 us -> 26.2 us
    pallas_call x1, Pallas kernels: 88 us -> 26.2 us  [paged_attention(): pl.pallas_call(paged_kernel, grid_spec=grid_spec, out_shape=jax.ShapeDtyp...]
  transfers between devices with their start and end apart: 5 -> 5, of which waited for: 5 -> 5; matrix products, arithmetic and copies ran while one was open for 12% -> 15% of each run, Pallas kernels for 0% -> 0%
where the time goes in v5:
time: 323 us; the launch traced here: 322 us
  waiting for transfers between devices  195 us (60%)
  matrix products  28 us (9%)
  Pallas kernels  26.2 us (8%)
  local copies, waits for them, and re-layouts  26.1 us (8%)
  other arithmetic  24.4 us (8%)
  between operations  13.4 us (4%)
  starting transfers between devices  8.85 us (3%)
    all_to_all x1, waiting for transfers between devices, shards(): lax.all_to_all(outgoing, 'seq', split_axis=0, concat_axis=0, tiled=True)  64.7 us
    reduce_scatter x1, waiting for transfers between devices, shards(): lax.psum_scatter(jnp.dot(attended, w_out, preferred_element_type=jnp.floa...  38.9 us
    reduce_scatter x1, waiting for transfers between devices, shards(): lax.psum_scatter(jnp.dot(activated, w_down, preferred_element_type=jnp.fl...  35.3 us
    all_gather x1, waiting for transfers between devices, shards(): page_store = lax.all_gather(shared_pages, 'seq', axis=0, tiled=True)  30.3 us
    pallas_call x1, Pallas kernels, paged_attention(): pl.pallas_call(paged_kernel, grid_spec=grid_spec, out_shape=jax.ShapeDtyp...  26.2 us
    all_gather x1, waiting for transfers between devices, shards(): normed_ffn = lax.all_gather(normed_own, 'tp', axis=0, tiled=True)  25.1 us
    dot_general x1, matrix products, shards(): jnp.dot(activated, w_down, preferred_element_type=jnp.float32)  11.7 us
    all_to_all x1, starting transfers between devices, shards(): lax.all_to_all(outgoing, 'seq', split_axis=0, concat_axis=0, tiled=True)  8.32 us
  transfers between devices with their start and end apart: 5, of which 5 were waited for; matrix products, arithmetic and copies ran while one was open for 15% of the time, Pallas kernels for 0%

profile of v5, /device:TPU:0, one launch (start us, length us, event | category | flops | bytes accessed | tf_op | source)
XLA Modules:
  0.0 322.1 jit_solution(9623131679123969487)
XLA Ops:
  6.5 0.7 all-gather.3.cloned.1.call-update
  7.3 0.7 reshape.335
  8.0 0.7 reshape.336
  8.8 0.8 copy.95
  10.3 0.8 gather_fusion.9
  13.6 3.5 %gather_fusion.11 = bf16[128,2,80,128]{3,2,1,0:T(8,128)(2,1)} fusion(bf16[32,2,80,128]{3,2,1,0:T(8,128)(2,1)S(1)} %bitcast.85, s32[1024]{0:T(1024)S(1)} %pad_clamp_fusion), kind=kCustom, calls=%fused_computation.11 | custom fusion | bytes 10486272 | tf_op jit(solution)/shard_map/jit(_take)/gather | solution.py:330
  17.1 5.5 %select_select_fusion = bf16[16,8,1,2,80,128]{5,4,3,1,2,0:T(8,128)(2,1)} fusion(bf16[16,8,1,2,80,128]{5,4,3,1,2,0:T(8,128)(2,1)} %bitcast.84, pred[16]{0:T(512)(128)(4,1)S(1)} %reduce_or.9, pred[16,8]{1,0:T(8,128)(4,1)S(1)} %get-tuple-element.7), kind=kLoop, calls=%fused_computation.18 | loop fusion | flops 5242880 | bytes 10485904 | tf_op jit(solution)/shard_map/jit(_where)/select_n | solution.py:329
  22.6 8.3 %all-to-all-start = ((bf16[16,8,1,2,80,128]{5,4,3,1,2,0:T(8,128)(2,1)}), bf16[16,8,1,2,80,128]{5,4,3,1,2,0:T(8,128)(2,1)}, u32[]{:S(2)}, u32[]{:S(2)}) async-start(bf16[16,8,1,2,80,128]{5,4,3,1,2,0:T(8,128)(2,1)} %select_select_fusion), calls=%async_computation | async-start | bytes 10485760 | tf_op jit(solution)/shard_map/all_to_all | solution.py:332
  35.9 3.4 %fusion = f32[128,4]{1,0:T(8,128)S(1)} fusion(bf16[128,4,2560]{2,1,0:T(4,128)(2,1)} %param.21), kind=kLoop, calls=%fused_computation.15 | loop fusion | flops 3931648 | bytes 2623488 | tf_op jit(solution)/shard_map/reduce_sum | solution.py:20
  39.7 1.5 fusion.39
  41.2 1.1 fusion.3
  42.4 1.0 copy.91
  43.4 4.8 %fusion.2 = bf16[128,4,2560]{2,1,0:T(4,128)(2,1)} fusion(bf16[128,4,2560]{2,1,0:T(4,128)(2,1)} %param.21, f32[2560]{0:T(1024)S(1)} %convert_element_type.51, f32[128,4]{1,0:T(8,128)S(1)} %add_rsqrt_fusion), kind=kLoop, calls=%fused_computation.17 | loop fusion | flops 5242880 | bytes 5255168 | tf_op jit(solution)/shard_map/convert_element_type | solution.py:21
  48.2 5.4 %reshape.333 = bf16[512,2560]{1,0:T(8,128)(2,1)} reshape(bf16[128,4,2560]{2,1,0:T(4,128)(2,1)} %fusion.2) | data formatting | bytes 5242880 | tf_op jit(solution)/shard_map/reshape | solution.py:301
  53.6 2.7 convolution_convert_fusion.2
  59.4 2.7 fusion.7
  63.2 64.7 %all-to-all-done = bf16[16,8,1,2,80,128]{5,4,3,1,2,0:T(8,128)(2,1)} async-done(((bf16[16,8,1,2,80,128]{5,4,3,1,2,0:T(8,128)(2,1)}), bf16[16,8,1,2,80,128]{5,4,3,1,2,0:T(8,128)(2,1)}, u32[]{:S(2)}, u32[]{:S(2)}) %all-to-all-start) | async-done | bytes 5242912 | tf_op jit(solution)/shard_map/all_to_all | solution.py:332
  127.9 30.3 %all-gather.3.cloned.1.call-done = bf16[320,1,2,80,128]{4,3,2,1,0:T(8,128)(2,1)} async-done(((bf16[20,1,2,80,128]{4,3,2,1,0:T(8,128)(2,1)}), bf16[320,1,2,80,128]{4,3,2,1,0:T(8,128)(2,1)}) %all-gather.3.cloned.1.call-update) | async-done | bytes 13107216 | tf_op jit(solution)/shard_map/all_gather | solution.py:298
  158.2 26.2 %shard_map.199 = bf16[4,512,80]{2,1,0:T(8,128)(2,1)} custom-call(s32[4,40]{1,0:T(4,128)} %pad_add_fusion.tbl, s32[4,4]{1,0:T(4,128)} %pad_add_fusion.1.meta, bf16[4,512,80]{2,1,0:T(8,128)(2,1)} %bitcast.88, bf16[4,2,80,128]{3,2,1,0:T(8,128)(2,1)} %pad_maximum_fusion.fresh_ref, bf16[320,2,80,128]{3,2,1,0:T(8,128)(2,1)} %bitcast.94, ...), custom_call_target="tpu_custom_call" | custom-call | flops 3439329280 | bytes 6717440 | tf_op jit(solution)/shard_map/pallas_call | solution.py:241
  184.4 1.4 copy.110
  186.2 3.0 convolution_convert_fusion.1
  189.9 38.9 %reduce-scatter.3.cloned.1.call-done = bf16[64,2560]{1,0:T(8,128)(2,1)} async-done(((bf16[512,2560]{1,0:T(8,128)(2,1)}), bf16[64,2560]{1,0:T(8,128)(2,1)}) %reduce-scatter.3.cloned.1.call-update) | async-done | bytes 327696 | tf_op jit(solution)/shard_map/reduce_scatter | solution.py:357
  228.8 1.2 reshape.347
  230.0 1.3 multiply_reduce_fusion
  231.3 1.2 multiply_convert_fusion.1
  232.5 0.8 reshape.343
  233.4 25.1 %all-gather.5.cloned.1.call-done = bf16[512,2560]{1,0:T(8,128)(2,1)} async-done(((bf16[64,2560]{1,0:T(8,128)(2,1)}), bf16[512,2560]{1,0:T(8,128)(2,1)}) %all-gather.5.cloned.1.call-update) | async-done | bytes 2621456 | tf_op jit(solution)/shard_map/all_gather | solution.py:369
  258.4 6.8 %fusion.28 = f32[512,864]{0,1:T(8,128)} fusion(bf16[512,2560]{1,0:T(8,128)(2,1)} %all-gather.5.cloned.1.call-done, bf16[2560,864]{0,1:T(8,128)(2,1)} %param.28), kind=kOutput, calls=%fused_computation.98 | convolution fusion | flops 2264924160 | bytes 8814592 | tf_op jit(solution)/shard_map/dot_general | solution.py:370
  265.2 11.7 %convolution_convert_fusion = bf16[512,2560]{1,0:T(8,128)(2,1)} fusion(bf16[864,2560]{1,0:T(8,128)(2,1)} %param.30, f32[512,864]{0,1:T(8,128)} %fusion.28, bf16[512,2560]{1,0:T(8,128)(2,1)} %all-gather.5.cloned.1.call-done, bf16[2560,864]{0,1:T(8,128)(2,1)} %param.29), kind=kOutput, calls=%fused_computation.19 | convolution fusion | flops 4533813248 | bytes 15859712 | tf_op jit(solution)/shard_map/dot_general | solution.py:375
  276.9 35.3 %reduce-scatter.5.cloned.1.call-done = bf16[64,2560]{1,0:T(8,128)(2,1)} async-done(((bf16[512,2560]{1,0:T(8,128)(2,1)}), bf16[64,2560]{1,0:T(8,128)(2,1)}) %reduce-scatter.5.cloned.1.call-update) | async-done | bytes 327696 | tf_op jit(solution)/shard_map/reduce_scatter | solution.py:374
  312.3 1.2 reshape.349
  313.5 2.0 fusion.21
  (102 shorter events, 13.9 us)
Async XLA Ops:
  6.5 179.6 %copy-start = (bf16[320,2560]{1,0:T(8,128)(2,1)S(1)}, bf16[320,2560]{1,0:T(8,128)(2,1)}, u32[]{:S(2)}) copy-start(bf16[320,2560]{1,0:T(8,128)(2,1)} %param.26) | copy-start | bytes 4915204
  6.5 151.6 %all-gather.3.cloned.1.call-start = ((), (), s32[]{:S(2)}) async-start(), calls=%async_computation.3 | async-start | bytes 13926400 | tf_op jit(solution)/shard_map/all_gather | solution.py:298
  10.3 3.3 %copy-start.8 = (bf16[32,1,2,80,128]{4,3,2,1,0:T(8,128)(2,1)S(1)}, bf16[32,1,2,80,128]{4,3,2,1,0:T(8,128)(2,1)}, u32[]{:S(2)}) copy-start(bf16[32,1,2,80,128]{4,3,2,1,0:T(8,128)(2,1)} %param.32) | copy-start | bytes 3932164
  22.6 8.6 %copy-start.1 = (s32[64]{0:T(128)S(1)}, s32[64]{0:T(128)}, u32[]{:S(2)}) copy-start(s32[64]{0:T(128)} %param.41) | copy-start | bytes 772
  22.6 9.9 %copy-start.2 = (s32[64]{0:T(128)S(1)}, s32[64]{0:T(128)}, u32[]{:S(2)}) copy-start(s32[64]{0:T(128)} %param.40) | copy-start | bytes 772
  22.6 10.6 %copy-start.3 = (s32[16]{0:T(128)S(1)}, s32[16]{0:T(128)}, u32[]{:S(2)}) copy-start(s32[16]{0:T(128)} %param.39) | copy-start | bytes 196
  22.6 11.2 %copy-start.4 = (s32[16]{0:T(128)S(1)}, s32[16]{0:T(128)}, u32[]{:S(2)}) copy-start(s32[16]{0:T(128)} %param.37) | copy-start | bytes 196
  22.6 105.3 %all-to-all-start = ((bf16[16,8,1,2,80,128]{5,4,3,1,2,0:T(8,128)(2,1)}), bf16[16,8,1,2,80,128]{5,4,3,1,2,0:T(8,128)(2,1)}, u32[]{:S(2)}, u32[]{:S(2)}) async-start(bf16[16,8,1,2,80,128]{5,4,3,1,2,0:T(8,128)(2,1)} %select_select_fusion), calls=%async_computation | async-start | bytes 10485760 | tf_op jit(solution)/shard_map/all_to_all | solution.py:332
  30.9 3.6 %copy-start.5 = (s32[64]{0:T(128)S(1)}, s32[64]{0:T(128)}, u32[]{:S(2)}) copy-start(s32[64]{0:T(128)} %param.38) | copy-start | bytes 772
  31.0 4.2 %copy-start.12 = (bf16[2560]{0:T(1024)(128)(2,1)S(1)}, bf16[2560]{0:T(1024)(128)(2,1)}, u32[]{:S(2)}) copy-start(bf16[2560]{0:T(1024)(128)(2,1)} %param.22) | copy-start | bytes 15364
  31.0 4.2 %copy-start.6 = (s32[4]{0:T(128)S(1)}, s32[4]{0:T(128)}, u32[]{:S(2)}) copy-start(s32[4]{0:T(128)} %param.36) | copy-start | bytes 52
  31.0 197.8 %reduce-scatter.3.cloned.1.call-start = ((), (), s32[]{:S(2)}) async-start(), calls=%async_computation.4 | async-start | bytes 2949120 | tf_op jit(solution)/shard_map/reduce_scatter | solution.py:357
  35.8 3.9 %copy-start.7 = (bf16[128,4,2560]{2,1,0:T(4,128)(2,1)S(1)}, bf16[128,4,2560]{2,1,0:T(4,128)(2,1)}, u32[]{:S(2)}) copy-start(bf16[128,4,2560]{2,1,0:T(4,128)(2,1)} %param.21) | copy-start | bytes 7864324
  39.7 1.5 copy-start.14
  48.2 5.4 %copy-start.9 = (bf16[2560,80]{0,1:T(8,128)(2,1)S(1)}, bf16[2560,80]{0,1:T(8,128)(2,1)}, u32[]{:S(2)}) copy-start(bf16[2560,80]{0,1:T(8,128)(2,1)} %param.25) | copy-start | bytes 1228804
  53.6 3.3 %copy-start.10 = (s32[4,16]{1,0:T(4,128)S(1)}, s32[4,16]{1,0:T(4,128)}, u32[]{:S(2)}) copy-start(s32[4,16]{1,0:T(4,128)} %param.33) | copy-start | bytes 772
  53.6 3.8 %copy-start.11 = (s32[16,16]{1,0:T(8,128)S(1)}, s32[16,16]{1,0:T(8,128)}, u32[]{:S(2)}) copy-start(s32[16,16]{1,0:T(8,128)} %param.34) | copy-start | bytes 3076
  53.6 5.8 %copy-start.15 = (bf16[2560,80]{0,1:T(8,128)(2,1)S(1)}, bf16[2560,80]{0,1:T(8,128)(2,1)}, u32[]{:S(2)}) copy-start(bf16[2560,80]{0,1:T(8,128)(2,1)} %param.24) | copy-start | bytes 1228804
  189.2 0.7 copy-start.13
  189.2 69.2 %all-gather.5.cloned.1.call-start = ((), (), s32[]{:S(2)}) async-start(), calls=%async_computation.5 | async-start | bytes 2949120 | tf_op jit(solution)/shard_map/all_gather | solution.py:369
  233.3 79.0 %reduce-scatter.5.cloned.1.call-start = ((), (), s32[]{:S(2)}) async-start(), calls=%async_computation.6 | async-start | bytes 2949120 | tf_op jit(solution)/shard_map/reduce_scatter | solution.py:374
Sparse Core Ops, SparseCore 0:
  9.5 148.6 all-gather.2
  189.4 39.3 reduce-scatter.2
  233.4 24.9 all-gather.4
  277.1 35.1 reduce-scatter.4

commit v6 on v5

--- a/solution.py
+++ b/solution.py
@@ -98,8 +98,8 @@
             pltpu.make_async_copy(leaf_hbm.at[tbl[j, p]], kv.at[into, p], sem.at[into]).start()
             return carry
 
-        lax.fori_loop(0, shared_count, shared_body, 0)
-        lax.fori_loop(shared_count, page_count, leaf_body, 0)
+        lax.fori_loop(0, ROOT_PAGES, shared_body, 0)
+        lax.fori_loop(ROOT_PAGES, page_count, leaf_body, 0)
 
     @pl.when(b == 0)
     def _():
@@ -295,9 +295,17 @@
     new_index = jnp.arange(new_rows, dtype=jnp.int32)
     query_pos = context[None, :] + new_index[:, None]
     all_slots = slot_request.reshape(seq_count, local_reqs)
-    page_store = lax.all_gather(shared_pages, "seq", axis=0, tiled=True)
-    root_index = root_table[root_nodes]
-    mid_index = mid_table[mid_nodes]
+    per_index = shared_pages.shape[0]
+    root_home = root_table // per_index
+    root_local = jnp.take_along_axis(
+        root_table, jnp.argmax(root_home == seq_index, 1)[:, None], 1
+    )[:, 0] - seq_index * per_index
+    mid_home = mid_table // per_index
+    mid_local = jnp.take_along_axis(
+        mid_table, jnp.argmax(mid_home == seq_index, 1)[:, None], 1
+    )[:, 0] - seq_index * per_index
+    root_store = lax.all_gather(jnp.take(shared_pages, root_local, axis=0), "seq", axis=0, tiled=True)
+    root_count = root_table.shape[0]
     normed = rms_norm(hidden, gain_attn).reshape(-1, model_width)
     query_proj = jnp.dot(normed, w_query, preferred_element_type=jnp.float32).reshape(
         new_rows, local_reqs, -1, HD
@@ -326,18 +334,19 @@
         sender_have[:, None], leaf_table[picked_request] - seq_index * pages_here, 0
     )
     leaf_slots = leaf_table.shape[1]
-    outgoing = jnp.where(
-        sender_have[:, None, None, None, None, None], jnp.take(leaf_pages, page_ids, axis=0), 0
-    )
+    mid_out = jnp.take(shared_pages, mid_local[leaf_parent[all_slots]], axis=0)
+    outgoing = jnp.concatenate([jnp.take(leaf_pages, page_ids, axis=0), mid_out], 1)
     arrived = lax.all_to_all(outgoing, "seq", split_axis=0, concat_axis=0, tiled=True)
+    per_source = arrived.shape[1]
     page_shape = arrived.shape[-3:]
-    leaf_store = arrived.reshape((-1,) + page_shape)
-    shared_store = page_store.reshape((-1,) + page_shape)
+    rest_store = arrived.reshape((-1,) + page_shape)
+    root_pages = root_store.reshape((-1,) + page_shape)
+    slot_ids_local = jnp.arange(local_reqs, dtype=jnp.int32)
     tbl = jnp.concatenate(
         [
-            root_index,
-            mid_index,
-            own_homes[:, None] * leaf_slots + jnp.arange(leaf_slots, dtype=jnp.int32)[None, :],
+            root_home[root_nodes] * root_count + root_nodes[:, None],
+            mid_home[mid_nodes] * per_source + leaf_slots + slot_ids_local[:, None],
+            own_homes[:, None] * per_source + jnp.arange(leaf_slots, dtype=jnp.int32)[None, :],
         ],
         1,
     ).astype(jnp.int32)
@@ -346,7 +355,7 @@
         [jnp.transpose(new_keys[:, :, 0], (1, 2, 0)), jnp.transpose(new_values[:, :, 0], (1, 2, 0))], 1
     )
     query_rows = jnp.transpose(queries[:, :, 0], (1, 2, 0, 3)).reshape(local_reqs, -1, HD)
-    attended = paged_attention(tbl, meta, query_rows, fresh_pack, shared_store, leaf_store)
+    attended = paged_attention(tbl, meta, query_rows, fresh_pack, root_pages, rest_store)
     attended = (
         jnp.transpose(attended.reshape(local_reqs, group_size, new_rows, HD), (2, 0, 1, 3))
         .reshape(new_rows * local_reqs, -1)

time: 323 us -> 338 us (1.046)
  other arithmetic: 24.4 us -> 36.9 us
  waiting for transfers between devices: 195 us -> 188 us
  local copies, waits for them, and re-layouts: 26.1 us -> 32.6 us
  Pallas kernels: 26.2 us -> 31.6 us
    all_to_all x1, waiting for transfers between devices: 64.7 us -> 5.23 us  [shards(): lax.all_to_all(outgoing, 'seq', split_axis=0, concat_axis=0, tiled=True)]
    all_gather x1, waiting for transfers between devices: 30.3 us -> 89 us  [shards(): lax.all_gather(jnp.take(shared_pages, root_local, axis=0), 'seq', axis=0,...]
    concatenate x1 -> x2, other arithmetic: 0.67 us -> 7.69 us  [the longest x1 7.04 us: shards(): jnp.concatenate([jnp.take(leaf_pages, page_ids, axis=0), mid_out], 1)]
    gather x2 -> x11, local copies, waits for them, and re-layouts: 1.12 us -> 7.19 us  [the longest x6 4.19 us: shards(): mid_out = jnp.take(shared_pages, mid_local[leaf_parent[all_slots]], axis=0)]
    reduce_scatter x1, waiting for transfers between devices: 38.9 us -> 33 us  [shards(): lax.psum_scatter(jnp.dot(attended, w_out, preferred_element_type=jnp.floa...]
    pallas_call x1, Pallas kernels: 26.2 us -> 31.6 us  [paged_attention(): pl.pallas_call(paged_kernel, grid_spec=grid_spec, out_shape=jax.ShapeDtyp...]
    select_n x1 -> x2, other arithmetic: 0.01 us -> 5.41 us  [shards(): jnp.take(leaf_pages, page_ids, axis=0)]
  transfers between devices with their start and end apart: 5 -> 5, of which waited for: 5 -> 5; matrix products, arithmetic and copies ran while one was open for 15% -> 10% of each run, Pallas kernels for 0% -> 0%
where the time goes in v6:
time: 338 us; the launch traced here: 339 us
  waiting for transfers between devices  188 us (56%)
  other arithmetic  36.9 us (11%)
  local copies, waits for them, and re-layouts  32.6 us (10%)
  Pallas kernels  31.6 us (9%)
  matrix products  28 us (8%)
  between operations  13.6 us (4%)
  starting transfers between devices  8.88 us (3%)
    all_gather x1, waiting for transfers between devices, shards(): lax.all_gather(jnp.take(shared_pages, root_local, axis=0), 'seq', axis=0,...  89 us
    reduce_scatter x1, waiting for transfers between devices, shards(): lax.psum_scatter(jnp.dot(activated, w_down, preferred_element_type=jnp.fl...  35.4 us
    reduce_scatter x1, waiting for transfers between devices, shards(): lax.psum_scatter(jnp.dot(attended, w_out, preferred_element_type=jnp.floa...  33 us
    pallas_call x1, Pallas kernels, paged_attention(): pl.pallas_call(paged_kernel, grid_spec=grid_spec, out_shape=jax.ShapeDtyp...  31.6 us
    all_gather x1, waiting for transfers between devices, shards(): normed_ffn = lax.all_gather(normed_own, 'tp', axis=0, tiled=True)  25.1 us
    dot_general x1, matrix products, shards(): jnp.dot(activated, w_down, preferred_element_type=jnp.float32)  11.7 us
    all_to_all x1, starting transfers between devices, shards(): lax.all_to_all(outgoing, 'seq', split_axis=0, concat_axis=0, tiled=True)  8.31 us
    convert_element_type x3, other arithmetic, rms_norm(): (values * inverse_rms * gain_vector.astype(jnp.float32)).astype(jnp.bfloa...  7.35 us
  transfers between devices with their start and end apart: 5, of which 5 were waited for; matrix products, arithmetic and copies ran while one was open for 10% of the time, Pallas kernels for 0%

profile of v6, /device:TPU:0, one launch (start us, length us, event | category | flops | bytes accessed | tf_op | source)
XLA Modules:
  0.0 339.2 jit_solution(13425270651488352269)
XLA Ops:
  6.5 0.9 reshape.426
  12.6 0.8 gather_fusion.13
  16.4 3.5 %gather_fusion.12 = bf16[128,2,80,128]{3,2,1,0:T(8,128)(2,1)} fusion(bf16[32,2,80,128]{3,2,1,0:T(8,128)(2,1)S(1)} %bitcast.105, s32[1024]{0:T(1024)S(1)} %pad_clamp_fusion.2), kind=kCustom, calls=%fused_computation.12 | custom fusion | bytes 10486272 | tf_op jit(solution)/shard_map/jit(_take)/gather | solution.py:338
  20.0 5.4 %broadcast_select_fusion = bf16[16,8,1,2,80,128]{5,4,3,1,2,0:T(8,128)(2,1)} fusion(bf16[16,8,1,2,80,128]{5,4,3,1,2,0:T(8,128)(2,1)} %bitcast.104, pred[16,8]{1,0:T(8,128)(4,1)S(1)} %get-tuple-element.11), kind=kLoop, calls=%fused_computation.25 | loop fusion | flops 2621440 | bytes 10485888 | tf_op jit(solution)/shard_map/jit(_take)/select_n | solution.py:338
  25.4 2.4 gather_fusion.15
  27.8 3.5 %broadcast_select_fusion.1 = bf16[16,4,1,2,80,128]{5,4,3,1,2,0:T(8,128)(2,1)} fusion(bf16[16,4,1,2,80,128]{5,4,3,1,2,0:T(8,128)(2,1)} %bitcast.106, pred[16,4]{1,0:T(8,128)(4,1)S(1)} %compare_and_fusion), kind=kLoop, calls=%fused_computation.32 | loop fusion | flops 1310720 | bytes 5242944 | tf_op jit(solution)/shard_map/jit(_take)/select_n | solution.py:337
  31.3 7.0 %pad_maximum_fusion = bf16[16,12,1,2,80,128]{5,4,3,1,2,0:T(8,128)(2,1)} fusion(bf16[16,4,1,2,80,128]{5,4,3,1,2,0:T(8,128)(2,1)} %broadcast_select_fusion.1, bf16[16,8,1,2,80,128]{5,4,3,1,2,0:T(8,128)(2,1)} %broadcast_select_fusion), kind=kLoop, calls=%fused_computation.19 | loop fusion | flops 3932160 | bytes 15728640 | tf_op jit(solution)/shard_map/concatenate | solution.py:338
  38.3 8.3 %all-to-all-start = ((bf16[16,12,1,2,80,128]{5,4,3,1,2,0:T(8,128)(2,1)}), bf16[16,12,1,2,80,128]{5,4,3,1,2,0:T(8,128)(2,1)}, u32[]{:S(2)}, u32[]{:S(2)}) async-start(bf16[16,12,1,2,80,128]{5,4,3,1,2,0:T(8,128)(2,1)} %pad_maximum_fusion), calls=%async_computation | async-start | bytes 15728640 | tf_op jit(solution)/shard_map/all_to_all | solution.py:339
  54.4 3.3 fusion
  58.1 1.5 fusion.46
  59.6 1.1 fusion.3
  60.9 1.0 copy.89
  61.9 4.7 %fusion.2 = bf16[128,4,2560]{2,1,0:T(4,128)(2,1)} fusion(bf16[128,4,2560]{2,1,0:T(4,128)(2,1)} %param.21, f32[2560]{0:T(1024)S(1)} %convert_element_type.49, f32[128,4]{1,0:T(8,128)S(1)} %add_rsqrt_fusion), kind=kLoop, calls=%fused_computation.24 | loop fusion | flops 5242880 | bytes 5255168 | tf_op jit(solution)/shard_map/convert_element_type | solution.py:21
  66.5 5.4 %reshape.423 = bf16[512,2560]{1,0:T(8,128)(2,1)} reshape(bf16[128,4,2560]{2,1,0:T(4,128)(2,1)} %fusion.2) | data formatting | bytes 5242880 | tf_op jit(solution)/shard_map/reshape | solution.py:309
  71.9 2.7 convolution_convert_fusion.2
  77.8 2.7 fusion.7
  81.6 89.0 %all-gather.3.cloned.1.call-done = bf16[64,1,2,80,128]{4,3,2,1,0:T(8,128)(2,1)} async-done(((bf16[4,1,2,80,128]{4,3,2,1,0:T(8,128)(2,1)}), bf16[64,1,2,80,128]{4,3,2,1,0:T(8,128)(2,1)}) %all-gather.3.cloned.1.call-update) | async-done | bytes 2621456 | tf_op jit(solution)/shard_map/all_gather | solution.py:307
  170.6 5.2 %all-to-all-done = bf16[16,12,1,2,80,128]{5,4,3,1,2,0:T(8,128)(2,1)} async-done(((bf16[16,12,1,2,80,128]{5,4,3,1,2,0:T(8,128)(2,1)}), bf16[16,12,1,2,80,128]{5,4,3,1,2,0:T(8,128)(2,1)}, u32[]{:S(2)}, u32[]{:S(2)}) %all-to-all-start) | async-done | bytes 7864352 | tf_op jit(solution)/shard_map/all_to_all | solution.py:339
  175.8 31.6 %shard_map.199 = bf16[4,512,80]{2,1,0:T(8,128)(2,1)} custom-call(s32[4,40]{1,0:T(4,128)} %pad_add_fusion.tbl, s32[4,4]{1,0:T(4,128)} %pad_add_fusion.1.meta, bf16[4,512,80]{2,1,0:T(8,128)(2,1)} %bitcast.111, bf16[4,2,80,128]{3,2,1,0:T(8,128)(2,1)} %pad_maximum_fusion.1.fresh_ref, bf16[64,2,80,128]{3,2,1,0:T(8,128)(2,1)} %bitcast.117, ...), custom_call_target="tpu_custom_call" | custom-call | flops 3439329280 | bytes 6717440 | tf_op jit(solution)/shard_map/pallas_call | solution.py:241
  207.4 1.4 copy.108
  209.2 3.0 convolution_convert_fusion.1
  213.0 33.0 %reduce-scatter.3.cloned.1.call-done = bf16[64,2560]{1,0:T(8,128)(2,1)} async-done(((bf16[512,2560]{1,0:T(8,128)(2,1)}), bf16[64,2560]{1,0:T(8,128)(2,1)}) %reduce-scatter.3.cloned.1.call-update) | async-done | bytes 327696 | tf_op jit(solution)/shard_map/reduce_scatter | solution.py:366
  245.9 1.2 reshape.439
  247.1 1.3 multiply_reduce_fusion
  248.4 1.2 multiply_convert_fusion.1
  249.6 0.8 reshape.435
  250.5 25.1 %all-gather.5.cloned.1.call-done = bf16[512,2560]{1,0:T(8,128)(2,1)} async-done(((bf16[64,2560]{1,0:T(8,128)(2,1)}), bf16[512,2560]{1,0:T(8,128)(2,1)}) %all-gather.5.cloned.1.call-update) | async-done | bytes 2621456 | tf_op jit(solution)/shard_map/all_gather | solution.py:378
  275.6 6.8 %fusion.35 = f32[512,864]{0,1:T(8,128)} fusion(bf16[512,2560]{1,0:T(8,128)(2,1)} %all-gather.5.cloned.1.call-done, bf16[2560,864]{0,1:T(8,128)(2,1)} %param.28), kind=kOutput, calls=%fused_computation.141 | convolution fusion | flops 2264924160 | bytes 8814592 | tf_op jit(solution)/shard_map/dot_general | solution.py:379
  282.4 11.7 %convolution_convert_fusion = bf16[512,2560]{1,0:T(8,128)(2,1)} fusion(bf16[864,2560]{1,0:T(8,128)(2,1)} %param.30, f32[512,864]{0,1:T(8,128)} %fusion.35, bf16[512,2560]{1,0:T(8,128)(2,1)} %all-gather.5.cloned.1.call-done, bf16[2560,864]{0,1:T(8,128)(2,1)} %param.29), kind=kOutput, calls=%fused_computation.26 | convolution fusion | flops 4533813248 | bytes 15859712 | tf_op jit(solution)/shard_map/dot_general | solution.py:384
  294.1 35.4 %reduce-scatter.5.cloned.1.call-done = bf16[64,2560]{1,0:T(8,128)(2,1)} async-done(((bf16[512,2560]{1,0:T(8,128)(2,1)}), bf16[64,2560]{1,0:T(8,128)(2,1)}) %reduce-scatter.5.cloned.1.call-update) | async-done | bytes 327696 | tf_op jit(solution)/shard_map/reduce_scatter | solution.py:383
  329.5 1.2 reshape.441
  330.6 2.0 fusion.21
  (136 shorter events, 21.6 us)
Async XLA Ops:
  6.5 202.7 %copy-start = (bf16[320,2560]{1,0:T(8,128)(2,1)S(1)}, bf16[320,2560]{1,0:T(8,128)(2,1)}, u32[]{:S(2)}) copy-start(bf16[320,2560]{1,0:T(8,128)(2,1)} %param.26) | copy-start | bytes 4915204
  9.7 1.6 copy-start.8
  9.7 2.9 copy-start.1
  13.6 2.8 copy-start.10
  20.0 5.4 %copy-start.11 = (bf16[20,1,2,80,128]{4,3,2,1,0:T(8,128)(2,1)S(1)}, bf16[20,1,2,80,128]{4,3,2,1,0:T(8,128)(2,1)}, u32[]{:S(2)}) copy-start(bf16[20,1,2,80,128]{4,3,2,1,0:T(8,128)(2,1)} %param.31) | copy-start | bytes 2457604
  38.3 8.4 %copy-start.7 = (s32[4,16]{1,0:T(4,128)S(1)}, s32[4,16]{1,0:T(4,128)}, u32[]{:S(2)}) copy-start(s32[4,16]{1,0:T(4,128)} %param.33) | copy-start | bytes 772
  38.3 11.4 %copy-start.2 = (s32[64]{0:T(128)S(1)}, s32[64]{0:T(128)}, u32[]{:S(2)}) copy-start(s32[64]{0:T(128)} %param.41) | copy-start | bytes 772
  38.3 137.5 %all-to-all-start = ((bf16[16,12,1,2,80,128]{5,4,3,1,2,0:T(8,128)(2,1)}), bf16[16,12,1,2,80,128]{5,4,3,1,2,0:T(8,128)(2,1)}, u32[]{:S(2)}, u32[]{:S(2)}) async-start(bf16[16,12,1,2,80,128]{5,4,3,1,2,0:T(8,128)(2,1)} %pad_maximum_fusion), calls=%async_computation | async-start | bytes 15728640 | tf_op jit(solution)/shard_map/all_to_all | solution.py:339
  46.6 5.0 %copy-start.3 = (s32[16]{0:T(128)S(1)}, s32[16]{0:T(128)}, u32[]{:S(2)}) copy-start(s32[16]{0:T(128)} %param.39) | copy-start | bytes 196
  46.7 5.7 %copy-start.4 = (s32[16]{0:T(128)S(1)}, s32[16]{0:T(128)}, u32[]{:S(2)}) copy-start(s32[16]{0:T(128)} %param.37) | copy-start | bytes 196
  46.7 6.3 %copy-start.5 = (s32[64]{0:T(128)S(1)}, s32[64]{0:T(128)}, u32[]{:S(2)}) copy-start(s32[64]{0:T(128)} %param.38) | copy-start | bytes 772
  46.7 6.9 %copy-start.13 = (bf16[2560]{0:T(1024)(128)(2,1)S(1)}, bf16[2560]{0:T(1024)(128)(2,1)}, u32[]{:S(2)}) copy-start(bf16[2560]{0:T(1024)(128)(2,1)} %param.22) | copy-start | bytes 15364
  46.7 7.0 %copy-start.6 = (s32[4]{0:T(128)S(1)}, s32[4]{0:T(128)}, u32[]{:S(2)}) copy-start(s32[4]{0:T(128)} %param.36) | copy-start | bytes 52
  46.7 123.9 %all-gather.3.cloned.1.call-start = ((), (), s32[]{:S(2)}) async-start(), calls=%async_computation.3 | async-start | bytes 2785280 | tf_op jit(solution)/shard_map/all_gather | solution.py:307
  49.5 196.5 %reduce-scatter.3.cloned.1.call-start = ((), (), s32[]{:S(2)}) async-start(), calls=%async_computation.4 | async-start | bytes 2949120 | tf_op jit(solution)/shard_map/reduce_scatter | solution.py:366
  54.3 3.8 %copy-start.9 = (bf16[128,4,2560]{2,1,0:T(4,128)(2,1)S(1)}, bf16[128,4,2560]{2,1,0:T(4,128)(2,1)}, u32[]{:S(2)}) copy-start(bf16[128,4,2560]{2,1,0:T(4,128)(2,1)} %param.21) | copy-start | bytes 7864324
  58.1 1.5 copy-start.15
  66.5 5.4 %copy-start.12 = (bf16[2560,80]{0,1:T(8,128)(2,1)S(1)}, bf16[2560,80]{0,1:T(8,128)(2,1)}, u32[]{:S(2)}) copy-start(bf16[2560,80]{0,1:T(8,128)(2,1)} %param.25) | copy-start | bytes 1228804
  71.9 5.9 %copy-start.16 = (bf16[2560,80]{0,1:T(8,128)(2,1)S(1)}, bf16[2560,80]{0,1:T(8,128)(2,1)}, u32[]{:S(2)}) copy-start(bf16[2560,80]{0,1:T(8,128)(2,1)} %param.24) | copy-start | bytes 1228804
  212.3 0.7 copy-start.14
  212.3 63.3 %all-gather.5.cloned.1.call-start = ((), (), s32[]{:S(2)}) async-start(), calls=%async_computation.5 | async-start | bytes 2949120 | tf_op jit(solution)/shard_map/all_gather | solution.py:378
  250.5 79.0 %reduce-scatter.5.cloned.1.call-start = ((), (), s32[]{:S(2)}) async-start(), calls=%async_computation.6 | async-start | bytes 2949120 | tf_op jit(solution)/shard_map/reduce_scatter | solution.py:383
Sparse Core Ops, SparseCore 0:
  49.7 120.8 all-gather.2
  212.4 33.4 reduce-scatter.2
  250.6 24.9 all-gather.4
  294.2 35.2 reduce-scatter.4

commit v7 on v5

--- a/solution.py
+++ b/solution.py
@@ -326,9 +326,7 @@
         sender_have[:, None], leaf_table[picked_request] - seq_index * pages_here, 0
     )
     leaf_slots = leaf_table.shape[1]
-    outgoing = jnp.where(
-        sender_have[:, None, None, None, None, None], jnp.take(leaf_pages, page_ids, axis=0), 0
-    )
+    outgoing = jnp.take(leaf_pages, page_ids, axis=0)
     arrived = lax.all_to_all(outgoing, "seq", split_axis=0, concat_axis=0, tiled=True)
     page_shape = arrived.shape[-3:]
     leaf_store = arrived.reshape((-1,) + page_shape)

time: 323 us -> 329 us (1.019)
  waiting for transfers between devices: 195 us -> 201 us
    all_gather x1, waiting for transfers between devices: 30.3 us -> 35.7 us  [shards(): page_store = lax.all_gather(shared_pages, 'seq', axis=0, tiled=True)]
  transfers between devices with their start and end apart: 5 -> 5, of which waited for: 5 -> 5; matrix products, arithmetic and copies ran while one was open for 15% -> 14% of each run, Pallas kernels for 0% -> 0%
where the time goes in v7:
time: 329 us; the launch traced here: 328 us
  waiting for transfers between devices  201 us (61%)
  matrix products  28 us (9%)
  Pallas kernels  26.3 us (8%)
  local copies, waits for them, and re-layouts  26.1 us (8%)
  other arithmetic  24.2 us (7%)
  between operations  13.4 us (4%)
  starting transfers between devices  8.85 us (3%)
    all_to_all x1, waiting for transfers between devices, shards(): lax.all_to_all(outgoing, 'seq', split_axis=0, concat_axis=0, tiled=True)  66.7 us
    reduce_scatter x1, waiting for transfers between devices, shards(): lax.psum_scatter(jnp.dot(attended, w_out, preferred_element_type=jnp.floa...  37.4 us
    all_gather x1, waiting for transfers between devices, shards(): page_store = lax.all_gather(shared_pages, 'seq', axis=0, tiled=True)  35.7 us
    reduce_scatter x1, waiting for transfers between devices, shards(): lax.psum_scatter(jnp.dot(activated, w_down, preferred_element_type=jnp.fl...  35.3 us
    pallas_call x1, Pallas kernels, paged_attention(): pl.pallas_call(paged_kernel, grid_spec=grid_spec, out_shape=jax.ShapeDtyp...  26.3 us
    all_gather x1, waiting for transfers between devices, shards(): normed_ffn = lax.all_gather(normed_own, 'tp', axis=0, tiled=True)  25 us
    dot_general x1, matrix products, shards(): jnp.dot(activated, w_down, preferred_element_type=jnp.float32)  11.7 us
    all_to_all x1, starting transfers between devices, shards(): lax.all_to_all(outgoing, 'seq', split_axis=0, concat_axis=0, tiled=True)  8.32 us
  transfers between devices with their start and end apart: 5, of which 5 were waited for; matrix products, arithmetic and copies ran while one was open for 14% of the time, Pallas kernels for 0%

profile of v7, /device:TPU:0, one launch (start us, length us, event | category | flops | bytes accessed | tf_op | source)
XLA Modules:
  0.0 327.9 jit_solution(5488140165716454838)
XLA Ops:
  6.5 0.7 all-gather.3.cloned.1.call-update
  7.3 0.7 reshape.328
  8.0 0.7 reshape.329
  8.8 0.8 copy.95
  10.3 0.8 gather_fusion.9
  13.6 3.5 %gather_fusion.11 = bf16[128,2,80,128]{3,2,1,0:T(8,128)(2,1)} fusion(bf16[32,2,80,128]{3,2,1,0:T(8,128)(2,1)S(1)} %bitcast.85, s32[1024]{0:T(1024)S(1)} %pad_clamp_fusion), kind=kCustom, calls=%fused_computation.11 | custom fusion | bytes 10486272 | tf_op jit(solution)/shard_map/jit(_take)/gather | solution.py:329
  17.1 5.3 %broadcast_select_fusion = bf16[16,8,1,2,80,128]{5,4,3,1,2,0:T(8,128)(2,1)} fusion(bf16[16,8,1,2,80,128]{5,4,3,1,2,0:T(8,128)(2,1)} %bitcast.84, pred[16,8]{1,0:T(8,128)(4,1)S(1)} %get-tuple-element.7), kind=kLoop, calls=%fused_computation.18 | loop fusion | flops 2621440 | bytes 10485888 | tf_op jit(solution)/shard_map/jit(_take)/select_n | solution.py:329
  22.5 8.3 %all-to-all-start = ((bf16[16,8,1,2,80,128]{5,4,3,1,2,0:T(8,128)(2,1)}), bf16[16,8,1,2,80,128]{5,4,3,1,2,0:T(8,128)(2,1)}, u32[]{:S(2)}, u32[]{:S(2)}) async-start(bf16[16,8,1,2,80,128]{5,4,3,1,2,0:T(8,128)(2,1)} %broadcast_select_fusion), calls=%async_computation | async-start | bytes 10485760 | tf_op jit(solution)/shard_map/all_to_all | solution.py:330
  35.7 3.3 %fusion = f32[128,4]{1,0:T(8,128)S(1)} fusion(bf16[128,4,2560]{2,1,0:T(4,128)(2,1)} %param.21), kind=kLoop, calls=%fused_computation.15 | loop fusion | flops 3931648 | bytes 2623488 | tf_op jit(solution)/shard_map/reduce_sum | solution.py:20
  39.5 1.5 fusion.39
  41.0 1.1 fusion.3
  42.2 1.0 copy.91
  43.2 4.8 %fusion.2 = bf16[128,4,2560]{2,1,0:T(4,128)(2,1)} fusion(bf16[128,4,2560]{2,1,0:T(4,128)(2,1)} %param.21, f32[2560]{0:T(1024)S(1)} %convert_element_type.49, f32[128,4]{1,0:T(8,128)S(1)} %add_rsqrt_fusion), kind=kLoop, calls=%fused_computation.17 | loop fusion | flops 5242880 | bytes 5255168 | tf_op jit(solution)/shard_map/convert_element_type | solution.py:21
  48.0 5.4 %reshape.326 = bf16[512,2560]{1,0:T(8,128)(2,1)} reshape(bf16[128,4,2560]{2,1,0:T(4,128)(2,1)} %fusion.2) | data formatting | bytes 5242880 | tf_op jit(solution)/shard_map/reshape | solution.py:301
  53.4 2.7 convolution_convert_fusion.2
  59.2 2.7 fusion.7
  63.0 66.7 %all-to-all-done = bf16[16,8,1,2,80,128]{5,4,3,1,2,0:T(8,128)(2,1)} async-done(((bf16[16,8,1,2,80,128]{5,4,3,1,2,0:T(8,128)(2,1)}), bf16[16,8,1,2,80,128]{5,4,3,1,2,0:T(8,128)(2,1)}, u32[]{:S(2)}, u32[]{:S(2)}) %all-to-all-start) | async-done | bytes 5242912 | tf_op jit(solution)/shard_map/all_to_all | solution.py:330
  129.6 35.7 %all-gather.3.cloned.1.call-done = bf16[320,1,2,80,128]{4,3,2,1,0:T(8,128)(2,1)} async-done(((bf16[20,1,2,80,128]{4,3,2,1,0:T(8,128)(2,1)}), bf16[320,1,2,80,128]{4,3,2,1,0:T(8,128)(2,1)}) %all-gather.3.cloned.1.call-update) | async-done | bytes 13107216 | tf_op jit(solution)/shard_map/all_gather | solution.py:298
  165.3 26.3 %shard_map.199 = bf16[4,512,80]{2,1,0:T(8,128)(2,1)} custom-call(s32[4,40]{1,0:T(4,128)} %pad_add_fusion.tbl, s32[4,4]{1,0:T(4,128)} %pad_add_fusion.1.meta, bf16[4,512,80]{2,1,0:T(8,128)(2,1)} %bitcast.88, bf16[4,2,80,128]{3,2,1,0:T(8,128)(2,1)} %pad_maximum_fusion.fresh_ref, bf16[320,2,80,128]{3,2,1,0:T(8,128)(2,1)} %bitcast.94, ...), custom_call_target="tpu_custom_call" | custom-call | flops 3439329280 | bytes 6717440 | tf_op jit(solution)/shard_map/pallas_call | solution.py:241
  191.6 1.4 copy.110
  193.4 3.0 convolution_convert_fusion.1
  197.2 37.4 %reduce-scatter.3.cloned.1.call-done = bf16[64,2560]{1,0:T(8,128)(2,1)} async-done(((bf16[512,2560]{1,0:T(8,128)(2,1)}), bf16[64,2560]{1,0:T(8,128)(2,1)}) %reduce-scatter.3.cloned.1.call-update) | async-done | bytes 327696 | tf_op jit(solution)/shard_map/reduce_scatter | solution.py:355
  234.6 1.2 reshape.340
  235.8 1.3 multiply_reduce_fusion
  237.1 1.2 multiply_convert_fusion.1
  238.3 0.8 reshape.336
  239.2 25.0 %all-gather.5.cloned.1.call-done = bf16[512,2560]{1,0:T(8,128)(2,1)} async-done(((bf16[64,2560]{1,0:T(8,128)(2,1)}), bf16[512,2560]{1,0:T(8,128)(2,1)}) %all-gather.5.cloned.1.call-update) | async-done | bytes 2621456 | tf_op jit(solution)/shard_map/all_gather | solution.py:367
  264.3 6.8 %fusion.28 = f32[512,864]{0,1:T(8,128)} fusion(bf16[512,2560]{1,0:T(8,128)(2,1)} %all-gather.5.cloned.1.call-done, bf16[2560,864]{0,1:T(8,128)(2,1)} %param.28), kind=kOutput, calls=%fused_computation.98 | convolution fusion | flops 2264924160 | bytes 8814592 | tf_op jit(solution)/shard_map/dot_general | solution.py:368
  271.0 11.7 %convolution_convert_fusion = bf16[512,2560]{1,0:T(8,128)(2,1)} fusion(bf16[864,2560]{1,0:T(8,128)(2,1)} %param.30, f32[512,864]{0,1:T(8,128)} %fusion.28, bf16[512,2560]{1,0:T(8,128)(2,1)} %all-gather.5.cloned.1.call-done, bf16[2560,864]{0,1:T(8,128)(2,1)} %param.29), kind=kOutput, calls=%fused_computation.19 | convolution fusion | flops 4533813248 | bytes 15859712 | tf_op jit(solution)/shard_map/dot_general | solution.py:373
  282.8 35.3 %reduce-scatter.5.cloned.1.call-done = bf16[64,2560]{1,0:T(8,128)(2,1)} async-done(((bf16[512,2560]{1,0:T(8,128)(2,1)}), bf16[64,2560]{1,0:T(8,128)(2,1)}) %reduce-scatter.5.cloned.1.call-update) | async-done | bytes 327696 | tf_op jit(solution)/shard_map/reduce_scatter | solution.py:372
  318.1 1.2 reshape.342
  319.3 2.0 fusion.21
  (102 shorter events, 13.9 us)
Async XLA Ops:
  6.5 186.9 %copy-start = (bf16[320,2560]{1,0:T(8,128)(2,1)S(1)}, bf16[320,2560]{1,0:T(8,128)(2,1)}, u32[]{:S(2)}) copy-start(bf16[320,2560]{1,0:T(8,128)(2,1)} %param.26) | copy-start | bytes 4915204
  6.5 158.8 %all-gather.3.cloned.1.call-start = ((), (), s32[]{:S(2)}) async-start(), calls=%async_computation.3 | async-start | bytes 13926400 | tf_op jit(solution)/shard_map/all_gather | solution.py:298
  10.3 3.3 copy-start.8
  22.4 8.6 %copy-start.1 = (s32[64]{0:T(128)S(1)}, s32[64]{0:T(128)}, u32[]{:S(2)}) copy-start(s32[64]{0:T(128)} %param.41) | copy-start | bytes 772
  22.4 9.9 %copy-start.2 = (s32[64]{0:T(128)S(1)}, s32[64]{0:T(128)}, u32[]{:S(2)}) copy-start(s32[64]{0:T(128)} %param.40) | copy-start | bytes 772
  22.4 10.6 %copy-start.3 = (s32[16]{0:T(128)S(1)}, s32[16]{0:T(128)}, u32[]{:S(2)}) copy-start(s32[16]{0:T(128)} %param.39) | copy-start | bytes 196
  22.5 11.2 %copy-start.4 = (s32[16]{0:T(128)S(1)}, s32[16]{0:T(128)}, u32[]{:S(2)}) copy-start(s32[16]{0:T(128)} %param.37) | copy-start | bytes 196
  22.5 107.2 %all-to-all-start = ((bf16[16,8,1,2,80,128]{5,4,3,1,2,0:T(8,128)(2,1)}), bf16[16,8,1,2,80,128]{5,4,3,1,2,0:T(8,128)(2,1)}, u32[]{:S(2)}, u32[]{:S(2)}) async-start(bf16[16,8,1,2,80,128]{5,4,3,1,2,0:T(8,128)(2,1)} %broadcast_select_fusion), calls=%async_computation | async-start | bytes 10485760 | tf_op jit(solution)/shard_map/all_to_all | solution.py:330
  30.8 3.6 %copy-start.5 = (s32[64]{0:T(128)S(1)}, s32[64]{0:T(128)}, u32[]{:S(2)}) copy-start(s32[64]{0:T(128)} %param.38) | copy-start | bytes 772
  30.8 4.2 %copy-start.12 = (bf16[2560]{0:T(1024)(128)(2,1)S(1)}, bf16[2560]{0:T(1024)(128)(2,1)}, u32[]{:S(2)}) copy-start(bf16[2560]{0:T(1024)(128)(2,1)} %param.22) | copy-start | bytes 15364
  30.8 4.2 %copy-start.6 = (s32[4]{0:T(128)S(1)}, s32[4]{0:T(128)}, u32[]{:S(2)}) copy-start(s32[4]{0:T(128)} %param.36) | copy-start | bytes 52
  30.8 203.8 %reduce-scatter.3.cloned.1.call-start = ((), (), s32[]{:S(2)}) async-start(), calls=%async_computation.4 | async-start | bytes 2949120 | tf_op jit(solution)/shard_map/reduce_scatter | solution.py:355
  35.7 3.8 %copy-start.7 = (bf16[128,4,2560]{2,1,0:T(4,128)(2,1)S(1)}, bf16[128,4,2560]{2,1,0:T(4,128)(2,1)}, u32[]{:S(2)}) copy-start(bf16[128,4,2560]{2,1,0:T(4,128)(2,1)} %param.21) | copy-start | bytes 7864324
  39.5 1.5 copy-start.14
  48.0 5.4 %copy-start.9 = (bf16[2560,80]{0,1:T(8,128)(2,1)S(1)}, bf16[2560,80]{0,1:T(8,128)(2,1)}, u32[]{:S(2)}) copy-start(bf16[2560,80]{0,1:T(8,128)(2,1)} %param.25) | copy-start | bytes 1228804
  53.4 3.3 copy-start.10
  53.4 3.8 %copy-start.11 = (s32[16,16]{1,0:T(8,128)S(1)}, s32[16,16]{1,0:T(8,128)}, u32[]{:S(2)}) copy-start(s32[16,16]{1,0:T(8,128)} %param.34) | copy-start | bytes 3076
  53.4 5.8 %copy-start.15 = (bf16[2560,80]{0,1:T(8,128)(2,1)S(1)}, bf16[2560,80]{0,1:T(8,128)(2,1)}, u32[]{:S(2)}) copy-start(bf16[2560,80]{0,1:T(8,128)(2,1)} %param.24) | copy-start | bytes 1228804
  196.5 0.7 copy-start.13
  196.5 67.7 %all-gather.5.cloned.1.call-start = ((), (), s32[]{:S(2)}) async-start(), calls=%async_computation.5 | async-start | bytes 2949120 | tf_op jit(solution)/shard_map/all_gather | solution.py:367
  239.2 78.9 %reduce-scatter.5.cloned.1.call-start = ((), (), s32[]{:S(2)}) async-start(), calls=%async_computation.6 | async-start | bytes 2949120 | tf_op jit(solution)/shard_map/reduce_scatter | solution.py:372
Sparse Core Ops, SparseCore 0:
  9.5 155.7 all-gather.2
  196.6 37.9 reduce-scatter.2
  239.3 24.9 all-gather.4
  282.9 35.1 reduce-scatter.4

commit v8 on v5

--- a/solution.py
+++ b/solution.py
@@ -79,27 +79,22 @@
 CHUNK_PAGES = 4
 
 
-def paged_kernel(tbl, meta, q_ref, fresh_ref, shared_hbm, leaf_hbm, out_ref, kv, sc, fresh_sc, top, mass, acc, sem):
+def part_body(chunk0, with_fresh, tbl, meta, q_ref, store_hbm, kv, sc, top, mass, acc, sem, begin, finish):
     b = pl.program_id(0)
     requests = pl.num_programs(0)
     slot = b % 2
     shared_count = ROOT_PAGES + MID_PAGES
-    page_count = shared_count + LEAF_SLOTS
+    page_count = kv.shape[1]
     width = kv.shape[-1]
     group = CHUNK_PAGES
     span = group * width
 
     def start_request(j, into):
-        def shared_body(p, carry):
-            pltpu.make_async_copy(shared_hbm.at[tbl[j, p]], kv.at[into, p], sem.at[into]).start()
+        def page_body(p, carry):
+            pltpu.make_async_copy(store_hbm.at[tbl[j, p]], kv.at[into, p], sem.at[into]).start()
             return carry
 
-        def leaf_body(p, carry):
-            pltpu.make_async_copy(leaf_hbm.at[tbl[j, p]], kv.at[into, p], sem.at[into]).start()
-            return carry
-
-        lax.fori_loop(0, shared_count, shared_body, 0)
-        lax.fori_loop(shared_count, page_count, leaf_body, 0)
+        lax.fori_loop(0, page_count, page_body, 0)
 
     @pl.when(b == 0)
     def _():
@@ -110,7 +105,7 @@
         start_request(b + 1, 1 - slot)
 
     def wait_body(p, carry):
-        pltpu.make_async_copy(shared_hbm.at[0], kv.at[slot, p], sem.at[slot]).wait()
+        pltpu.make_async_copy(store_hbm.at[0], kv.at[slot, p], sem.at[slot]).wait()
         return carry
 
     lax.fori_loop(0, page_count, wait_body, 0)
@@ -131,7 +126,7 @@
         return jnp.where(allowed, s, masked_score)
 
     def geometry(c):
-        page = group * c
+        page = group * (chunk0 + c)
         in_root = page < ROOT_PAGES
         in_mid = page < shared_count
         first = jnp.where(
@@ -139,19 +134,13 @@
         )
         base = jnp.where(in_root, 0, jnp.where(in_mid, root_span, root_span + mid_span))
         limit = jnp.where(in_root, root_span, jnp.where(in_mid, mid_span, leaf_span))
-        return first, base, limit
+        live = (first < limit) & (context - (base + first + span - 1) < WINDOW)
+        return first, base, limit, live
 
     def pages_of(c, part):
         return jnp.concatenate([kv[slot, group * c + k, part] for k in range(group)], 1)
 
-    fresh_lanes = lax.broadcasted_iota(jnp.int32, (1, width), 1)
-    fresh_scores = masked(
-        jnp.dot(q, fresh_ref[0, 0], preferred_element_type=jnp.float32) * scale,
-        context + fresh_lanes,
-        fresh_lanes >= 0,
-    )
-    fresh_sc[...] = fresh_scores
-    top[...] = fresh_scores
+    begin(q, query_pos, masked, scale)
 
     def keep(c, s):
         sc[c] = s
@@ -161,8 +150,7 @@
         top[...] = m
 
     def max_body(c, carry):
-        first, base, limit = geometry(c)
-        live = (first < limit) & (context - (base + first + span - 1) < WINDOW)
+        first, base, limit, live = geometry(c)
         full = (first + span <= limit) & (context + width - 1 - (base + first) < WINDOW)
 
         @pl.when(full)
@@ -179,18 +167,13 @@
 
     chunks = page_count // group
     lax.fori_loop(0, chunks, max_body, 0)
-    top[...] = jnp.broadcast_to(jnp.max(top[...], -1, keepdims=True), top.shape)
+    earlier = top[...]
+    top[...] = jnp.broadcast_to(jnp.max(earlier, -1, keepdims=True), top.shape)
     row_top = top[...]
-
-    fresh_w = jnp.exp(fresh_sc[...] - row_top)
-    mass[...] = fresh_w
-    acc[...] = lax.dot_general(
-        fresh_w.astype(jnp.bfloat16), fresh_ref[0, 1], (((1,), (1,)), ((), ())), preferred_element_type=jnp.float32
-    )
+    finish(row_top)
 
     def sum_body(c, carry):
-        first, base, limit = geometry(c)
-        live = (first < limit) & (context - (base + first + span - 1) < WINDOW)
+        first, base, limit, live = geometry(c)
 
         @pl.when(live)
         def _():
@@ -208,47 +191,110 @@
         return carry
 
     lax.fori_loop(0, chunks, sum_body, 0)
+
+
+def leaf_kernel(tbl, meta, q_ref, fresh_ref, store_hbm, acc_out, top_out, mass_out, kv, sc, fresh_sc, top, mass, acc, sem):
+    def begin(q, query_pos, masked, scale):
+        width = fresh_sc.shape[-1]
+        fresh_lanes = lax.broadcasted_iota(jnp.int32, (1, width), 1)
+        fresh_scores = masked(
+            jnp.dot(q, fresh_ref[0, 0], preferred_element_type=jnp.float32) * scale,
+            meta[pl.program_id(0), 3] + fresh_lanes,
+            fresh_lanes >= 0,
+        )
+        fresh_sc[...] = fresh_scores
+        top[...] = fresh_scores
+
+    def finish(row_top):
+        fresh_w = jnp.exp(fresh_sc[...] - row_top)
+        mass[...] = fresh_w
+        acc[...] = lax.dot_general(
+            fresh_w.astype(jnp.bfloat16), fresh_ref[0, 1], (((1,), (1,)), ((), ())),
+            preferred_element_type=jnp.float32,
+        )
+
+    part_body(
+        (ROOT_PAGES + MID_PAGES) // CHUNK_PAGES, True, tbl, meta, q_ref, store_hbm, kv, sc, top, mass, acc, sem,
+        begin, finish,
+    )
+    acc_out[0] = acc[...]
+    top_out[0] = top[...]
+    mass_out[0] = mass[...]
+
+
+def shared_kernel(tbl, meta, q_ref, acc_in, top_in, mass_in, store_hbm, out_ref, kv, sc, top, mass, acc, sem):
+    def begin(q, query_pos, masked, scale):
+        top[...] = top_in[0]
+
+    def finish(row_top):
+        factor = jnp.exp(top_in[0] - row_top)
+        mass[...] = mass_in[0] * factor
+        acc[...] = acc_in[0] * factor[:, :1]
+
+    part_body(0, False, tbl, meta, q_ref, store_hbm, kv, sc, top, mass, acc, sem, begin, finish)
     totals = jnp.sum(mass[...], -1, keepdims=True)
     out_ref[0] = (acc[...] / totals).astype(out_ref.dtype)
 
 
-def paged_attention(tbl, meta, queries, fresh, shared_store, leaf_store):
-    reqs, rows, head = queries.shape
-    page_shape = shared_store.shape[1:]
+def part_call(kernel, tbl, meta, inputs, in_blocks, store, out_shapes):
+    reqs, rows, head = inputs[0].shape
+    page_shape = store.shape[1:]
     width = page_shape[-1]
     pages = tbl.shape[1]
-    keys_total = (pages + 1) * width
+
+    def block(shape):
+        return pl.BlockSpec((1,) + shape[1:], lambda i, t, m: (i,) + (0,) * (len(shape) - 1))
+
+    scratch = [
+        pltpu.VMEM((2, pages) + page_shape, store.dtype),
+        pltpu.VMEM((pages // CHUNK_PAGES, rows, CHUNK_PAGES * width), jnp.float32),
+    ]
+    if kernel is leaf_kernel:
+        scratch.append(pltpu.VMEM((rows, width), jnp.float32))
+    scratch += [
+        pltpu.VMEM((rows, width), jnp.float32),
+        pltpu.VMEM((rows, width), jnp.float32),
+        pltpu.VMEM((rows, head), jnp.float32),
+        pltpu.SemaphoreType.DMA((2,)),
+    ]
     grid_spec = pltpu.PrefetchScalarGridSpec(
         num_scalar_prefetch=2,
         grid=(reqs,),
-        in_specs=[
-            pl.BlockSpec((1, rows, head), lambda i, t, m: (i, 0, 0)),
-            pl.BlockSpec((1,) + page_shape, lambda i, t, m: (i, 0, 0, 0)),
-            pl.BlockSpec(memory_space=pl.ANY),
-            pl.BlockSpec(memory_space=pl.ANY),
-        ],
-        out_specs=pl.BlockSpec((1, rows, head), lambda i, t, m: (i, 0, 0)),
-        scratch_shapes=[
-            pltpu.VMEM((2, pages) + page_shape, shared_store.dtype),
-            pltpu.VMEM((pages // CHUNK_PAGES, rows, CHUNK_PAGES * width), jnp.float32),
-            pltpu.VMEM((rows, width), jnp.float32),
-            pltpu.VMEM((rows, width), jnp.float32),
-            pltpu.VMEM((rows, width), jnp.float32),
-            pltpu.VMEM((rows, head), jnp.float32),
-            pltpu.SemaphoreType.DMA((2,)),
-        ],
-    )
+        in_specs=[block(x.shape) for x in inputs] + [pl.BlockSpec(memory_space=pl.ANY)],
+        out_specs=[block(s.shape) for s in out_shapes],
+        scratch_shapes=scratch,
+    )
+    keys_total = pages * width
     return pl.pallas_call(
-        paged_kernel,
+        kernel,
         grid_spec=grid_spec,
-        out_shape=jax.ShapeDtypeStruct((reqs, rows, head), jnp.bfloat16),
+        out_shape=out_shapes,
         compiler_params=pltpu.CompilerParams(dimension_semantics=("arbitrary",)),
         cost_estimate=pl.CostEstimate(
             flops=4 * reqs * rows * keys_total * head,
             transcendentals=reqs * rows * keys_total,
-            bytes_accessed=reqs * (pages + 1) * 2 * head * width * 2,
+            bytes_accessed=reqs * pages * 2 * head * width * 2,
         ),
-    )(tbl, meta, queries, fresh, shared_store, leaf_store)
+    )(tbl, meta, *inputs, store)
+
+
+def paged_attention(tbl, meta, queries, fresh, shared_store, leaf_store):
+    reqs, rows, head = queries.shape
+    width = shared_store.shape[-1]
+    shared_count = ROOT_PAGES + MID_PAGES
+    state = part_call(
+        leaf_kernel, tbl[:, shared_count:], meta, [queries, fresh], None, leaf_store,
+        [
+            jax.ShapeDtypeStruct((reqs, rows, head), jnp.float32),
+            jax.ShapeDtypeStruct((reqs, rows, width), jnp.float32),
+            jax.ShapeDtypeStruct((reqs, rows, width), jnp.float32),
+        ],
+    )
+    (out,) = part_call(
+        shared_kernel, tbl[:, :shared_count], meta, [queries] + list(state), None, shared_store,
+        [jax.ShapeDtypeStruct((reqs, rows, head), jnp.bfloat16)],
+    )
+    return out
 
 
 def spans(request_ids, root_len, mid_len, leaf_len, mid_parent, leaf_parent):

time: 323 us -> 316 us (0.978)
  waiting for transfers between devices: 195 us -> 180 us
  Pallas kernels: 26.2 us -> 34.4 us
    all_gather x1, waiting for transfers between devices: 30.3 us -> 19.4 us  [shards(): page_store = lax.all_gather(shared_pages, 'seq', axis=0, tiled=True)]
    pallas_call x1 -> x2, Pallas kernels: 26.2 us -> 34.4 us  [part_call(): pl.pallas_call(kernel, grid_spec=grid_spec, out_shape=out_shapes, compile...]
    reduce_scatter x1, waiting for transfers between devices: 38.9 us -> 35.2 us  [shards(): lax.psum_scatter(jnp.dot(attended, w_out, preferred_element_type=jnp.floa...]
  transfers between devices with their start and end apart: 5 -> 5, of which waited for: 5 -> 5; matrix products, arithmetic and copies ran while one was open for 15% -> 15% of each run, Pallas kernels for 0% -> 3%
where the time goes in v8:
time: 316 us
  waiting for transfers between devices  180 us (57%)
  Pallas kernels  34.4 us (11%)
  matrix products  28 us (9%)
  local copies, waits for them, and re-layouts  26.3 us (8%)
  other arithmetic  25 us (8%)
  between operations  13.5 us (4%)
  starting transfers between devices  8.67 us (3%)
    all_to_all x1, waiting for transfers between devices, shards(): lax.all_to_all(outgoing, 'seq', split_axis=0, concat_axis=0, tiled=True)  64.3 us
    reduce_scatter x1, waiting for transfers between devices, shards(): lax.psum_scatter(jnp.dot(activated, w_down, preferred_element_type=jnp.fl...  35.3 us
    reduce_scatter x1, waiting for transfers between devices, shards(): lax.psum_scatter(jnp.dot(attended, w_out, preferred_element_type=jnp.floa...  35.2 us
    pallas_call x2, Pallas kernels, part_call(): pl.pallas_call(kernel, grid_spec=grid_spec, out_shape=out_shapes, compile...  34.4 us
    all_gather x1, waiting for transfers between devices, shards(): normed_ffn = lax.all_gather(normed_own, 'tp', axis=0, tiled=True)  24.9 us
    all_gather x1, waiting for transfers between devices, shards(): page_store = lax.all_gather(shared_pages, 'seq', axis=0, tiled=True)  19.4 us
    dot_general x1, matrix products, shards(): jnp.dot(activated, w_down, preferred_element_type=jnp.float32)  11.7 us
    all_to_all x1, starting transfers between devices, shards(): lax.all_to_all(outgoing, 'seq', split_axis=0, concat_axis=0, tiled=True)  8.32 us
  transfers between devices with their start and end apart: 5, of which 5 were waited for; matrix products, arithmetic and copies ran while one was open for 15% of the time, Pallas kernels for 3%

profile of v8, /device:TPU:0, one launch (start us, length us, event | category | flops | bytes accessed | tf_op | source)
XLA Modules:
  0.0 315.7 jit_solution(11367089178691852429)
XLA Ops:
  7.3 0.7 reshape.334
  8.0 0.7 reshape.335
  8.8 0.8 copy.95
  10.3 0.8 gather_fusion.9
  13.6 3.5 %gather_fusion.11 = bf16[128,2,80,128]{3,2,1,0:T(8,128)(2,1)} fusion(bf16[32,2,80,128]{3,2,1,0:T(8,128)(2,1)S(1)} %bitcast.85, s32[1024]{0:T(1024)S(1)} %pad_clamp_fusion), kind=kCustom, calls=%fused_computation.11 | custom fusion | bytes 10486272 | tf_op jit(solution)/shard_map/jit(_take)/gather | solution.py:376
  17.1 5.5 %select_select_fusion = bf16[16,8,1,2,80,128]{5,4,3,1,2,0:T(8,128)(2,1)} fusion(bf16[16,8,1,2,80,128]{5,4,3,1,2,0:T(8,128)(2,1)} %bitcast.84, pred[16]{0:T(512)(128)(4,1)S(1)} %reduce_or.9, pred[16,8]{1,0:T(8,128)(4,1)S(1)} %get-tuple-element.13), kind=kLoop, calls=%fused_computation.18 | loop fusion | flops 5242880 | bytes 10485904 | tf_op jit(solution)/shard_map/jit(_where)/select_n | solution.py:375
  22.6 8.3 %all-to-all-start = ((bf16[16,8,1,2,80,128]{5,4,3,1,2,0:T(8,128)(2,1)}), bf16[16,8,1,2,80,128]{5,4,3,1,2,0:T(8,128)(2,1)}, u32[]{:S(2)}, u32[]{:S(2)}) async-start(bf16[16,8,1,2,80,128]{5,4,3,1,2,0:T(8,128)(2,1)} %select_select_fusion), calls=%async_computation | async-start | bytes 10485760 | tf_op jit(solution)/shard_map/all_to_all | solution.py:378
  35.7 3.3 %fusion = f32[128,4]{1,0:T(8,128)S(1)} fusion(bf16[128,4,2560]{2,1,0:T(4,128)(2,1)} %param.21), kind=kLoop, calls=%fused_computation.15 | loop fusion | flops 3931648 | bytes 2623488 | tf_op jit(solution)/shard_map/reduce_sum | solution.py:20
  39.5 1.5 fusion.39
  41.0 1.1 fusion.3
  42.2 1.0 copy.91
  43.2 4.8 %fusion.2 = bf16[128,4,2560]{2,1,0:T(4,128)(2,1)} fusion(bf16[128,4,2560]{2,1,0:T(4,128)(2,1)} %param.21, f32[2560]{0:T(1024)S(1)} %convert_element_type.51, f32[128,4]{1,0:T(8,128)S(1)} %add_rsqrt_fusion), kind=kLoop, calls=%fused_computation.17 | loop fusion | flops 5242880 | bytes 5255168 | tf_op jit(solution)/shard_map/convert_element_type | solution.py:21
  48.0 5.4 %reshape.333 = bf16[512,2560]{1,0:T(8,128)(2,1)} reshape(bf16[128,4,2560]{2,1,0:T(4,128)(2,1)} %fusion.2) | data formatting | bytes 5242880 | tf_op jit(solution)/shard_map/reshape | solution.py:347
  53.4 2.7 convolution_convert_fusion.2
  59.1 2.7 fusion.7
  63.5 64.3 %all-to-all-done = bf16[16,8,1,2,80,128]{5,4,3,1,2,0:T(8,128)(2,1)} async-done(((bf16[16,8,1,2,80,128]{5,4,3,1,2,0:T(8,128)(2,1)}), bf16[16,8,1,2,80,128]{5,4,3,1,2,0:T(8,128)(2,1)}, u32[]{:S(2)}, u32[]{:S(2)}) %all-to-all-start) | async-done | bytes 5242912 | tf_op jit(solution)/shard_map/all_to_all | solution.py:378
  127.9 10.9 %shard_map.199 = (f32[4,512,80]{2,1,0:T(8,128)}, f32[4,512,128]{2,1,0:T(8,128)}, f32[4,512,128]{2,1,0:T(8,128)}) custom-call(s32[4,8]{1,0:T(4,128)} %iota_add_fusion.tbl, s32[4,4]{1,0:T(4,128)} %pad_add_fusion.1.meta, bf16[4,512,80]{2,1,0:T(8,128)(2,1)} %bitcast.87, bf16[4,2,80,128]{3,2,1,0:T(8,128)(2,1)} %pad_maximum_fusion.fresh_ref, ...), custom_call_target="tpu_custom_call" | custom-call | flops 671088640 | bytes 1310720 | tf_op jit(solution)/shard_map/pallas_call | solution.py:268
  138.8 19.4 %all-gather.3.cloned.1.call-done = bf16[320,1,2,80,128]{4,3,2,1,0:T(8,128)(2,1)} async-done(((bf16[20,1,2,80,128]{4,3,2,1,0:T(8,128)(2,1)}), bf16[320,1,2,80,128]{4,3,2,1,0:T(8,128)(2,1)}) %all-gather.3.cloned.1.call-update) | async-done | bytes 13107216 | tf_op jit(solution)/shard_map/all_gather | solution.py:344
  158.2 23.5 %shard_map.200 = bf16[4,512,80]{2,1,0:T(8,128)(2,1)} custom-call(s32[4,32]{1,0:T(4,128)} %pad_add_fusion.tbl, s32[4,4]{1,0:T(4,128)} %pad_add_fusion.1.meta, bf16[4,512,80]{2,1,0:T(8,128)(2,1)} %bitcast.88, f32[4,512,80]{2,1,0:T(8,128)} %get-tuple-element.10.acc_in, f32[4,512,128]{2,1,0:T(8,128)} %get-tuple-element.11.top_in, ...), custom_call_target="tpu_custom_call" | custom-call | flops 2684354560 | bytes 5242880 | tf_op jit(solution)/shard_map/pallas_call | solution.py:268
  181.7 1.4 copy.110
  183.5 3.0 convolution_convert_fusion.1
  187.2 35.2 %reduce-scatter.3.cloned.1.call-done = bf16[64,2560]{1,0:T(8,128)(2,1)} async-done(((bf16[512,2560]{1,0:T(8,128)(2,1)}), bf16[64,2560]{1,0:T(8,128)(2,1)}) %reduce-scatter.3.cloned.1.call-update) | async-done | bytes 327696 | tf_op jit(solution)/shard_map/reduce_scatter | solution.py:403
  222.5 1.2 reshape.347
  223.6 1.3 multiply_reduce_fusion
  224.9 1.2 multiply_convert_fusion.1
  226.2 0.8 reshape.343
  227.3 24.9 %all-gather.5.cloned.1.call-done = bf16[512,2560]{1,0:T(8,128)(2,1)} async-done(((bf16[64,2560]{1,0:T(8,128)(2,1)}), bf16[512,2560]{1,0:T(8,128)(2,1)}) %all-gather.5.cloned.1.call-update) | async-done | bytes 2621456 | tf_op jit(solution)/shard_map/all_gather | solution.py:415
  252.1 6.8 %fusion.28 = f32[512,864]{0,1:T(8,128)} fusion(bf16[512,2560]{1,0:T(8,128)(2,1)} %all-gather.5.cloned.1.call-done, bf16[2560,864]{0,1:T(8,128)(2,1)} %param.28), kind=kOutput, calls=%fused_computation.98 | convolution fusion | flops 2264924160 | bytes 8814592 | tf_op jit(solution)/shard_map/dot_general | solution.py:416
  258.9 11.7 %convolution_convert_fusion = bf16[512,2560]{1,0:T(8,128)(2,1)} fusion(bf16[864,2560]{1,0:T(8,128)(2,1)} %param.30, f32[512,864]{0,1:T(8,128)} %fusion.28, bf16[512,2560]{1,0:T(8,128)(2,1)} %all-gather.5.cloned.1.call-done, bf16[2560,864]{0,1:T(8,128)(2,1)} %param.29), kind=kOutput, calls=%fused_computation.19 | convolution fusion | flops 4533813248 | bytes 15859712 | tf_op jit(solution)/shard_map/dot_general | solution.py:421
  270.6 35.3 %reduce-scatter.5.cloned.1.call-done = bf16[64,2560]{1,0:T(8,128)(2,1)} async-done(((bf16[512,2560]{1,0:T(8,128)(2,1)}), bf16[64,2560]{1,0:T(8,128)(2,1)}) %reduce-scatter.5.cloned.1.call-update) | async-done | bytes 327696 | tf_op jit(solution)/shard_map/reduce_scatter | solution.py:420
  305.9 1.2 reshape.349
  307.1 2.0 fusion.21
  (103 shorter events, 15.2 us)
Async XLA Ops:
  6.5 176.9 %copy-start = (bf16[320,2560]{1,0:T(8,128)(2,1)S(1)}, bf16[320,2560]{1,0:T(8,128)(2,1)}, u32[]{:S(2)}) copy-start(bf16[320,2560]{1,0:T(8,128)(2,1)} %param.26) | copy-start | bytes 4915204
  6.5 151.6 %all-gather.3.cloned.1.call-start = ((), (), s32[]{:S(2)}) async-start(), calls=%async_computation.3 | async-start | bytes 13926400 | tf_op jit(solution)/shard_map/all_gather | solution.py:344
  10.3 3.3 %copy-start.8 = (bf16[32,1,2,80,128]{4,3,2,1,0:T(8,128)(2,1)S(1)}, bf16[32,1,2,80,128]{4,3,2,1,0:T(8,128)(2,1)}, u32[]{:S(2)}) copy-start(bf16[32,1,2,80,128]{4,3,2,1,0:T(8,128)(2,1)} %param.32) | copy-start | bytes 3932164
  22.6 8.5 %copy-start.1 = (s32[64]{0:T(128)S(1)}, s32[64]{0:T(128)}, u32[]{:S(2)}) copy-start(s32[64]{0:T(128)} %param.41) | copy-start | bytes 772
  22.6 9.8 %copy-start.2 = (s32[64]{0:T(128)S(1)}, s32[64]{0:T(128)}, u32[]{:S(2)}) copy-start(s32[64]{0:T(128)} %param.40) | copy-start | bytes 772
  22.6 10.4 %copy-start.3 = (s32[16]{0:T(128)S(1)}, s32[16]{0:T(128)}, u32[]{:S(2)}) copy-start(s32[16]{0:T(128)} %param.39) | copy-start | bytes 196
  22.6 11.1 %copy-start.4 = (s32[16]{0:T(128)S(1)}, s32[16]{0:T(128)}, u32[]{:S(2)}) copy-start(s32[16]{0:T(128)} %param.37) | copy-start | bytes 196
  22.6 105.3 %all-to-all-start = ((bf16[16,8,1,2,80,128]{5,4,3,1,2,0:T(8,128)(2,1)}), bf16[16,8,1,2,80,128]{5,4,3,1,2,0:T(8,128)(2,1)}, u32[]{:S(2)}, u32[]{:S(2)}) async-start(bf16[16,8,1,2,80,128]{5,4,3,1,2,0:T(8,128)(2,1)} %select_select_fusion), calls=%async_computation | async-start | bytes 10485760 | tf_op jit(solution)/shard_map/all_to_all | solution.py:378
  30.9 3.4 %copy-start.5 = (s32[64]{0:T(128)S(1)}, s32[64]{0:T(128)}, u32[]{:S(2)}) copy-start(s32[64]{0:T(128)} %param.38) | copy-start | bytes 772
  30.9 4.0 %copy-start.12 = (bf16[2560]{0:T(1024)(128)(2,1)S(1)}, bf16[2560]{0:T(1024)(128)(2,1)}, u32[]{:S(2)}) copy-start(bf16[2560]{0:T(1024)(128)(2,1)} %param.22) | copy-start | bytes 15364
  31.0 4.0 %copy-start.6 = (s32[4]{0:T(128)S(1)}, s32[4]{0:T(128)}, u32[]{:S(2)}) copy-start(s32[4]{0:T(128)} %param.36) | copy-start | bytes 52
  31.0 191.5 %reduce-scatter.3.cloned.1.call-start = ((), (), s32[]{:S(2)}) async-start(), calls=%async_computation.4 | async-start | bytes 2949120 | tf_op jit(solution)/shard_map/reduce_scatter | solution.py:403
  35.6 3.8 %copy-start.7 = (bf16[128,4,2560]{2,1,0:T(4,128)(2,1)S(1)}, bf16[128,4,2560]{2,1,0:T(4,128)(2,1)}, u32[]{:S(2)}) copy-start(bf16[128,4,2560]{2,1,0:T(4,128)(2,1)} %param.21) | copy-start | bytes 7864324
  39.5 1.5 copy-start.14
  48.0 5.4 %copy-start.9 = (bf16[2560,80]{0,1:T(8,128)(2,1)S(1)}, bf16[2560,80]{0,1:T(8,128)(2,1)}, u32[]{:S(2)}) copy-start(bf16[2560,80]{0,1:T(8,128)(2,1)} %param.25) | copy-start | bytes 1228804
  53.4 3.3 %copy-start.10 = (s32[4,16]{1,0:T(4,128)S(1)}, s32[4,16]{1,0:T(4,128)}, u32[]{:S(2)}) copy-start(s32[4,16]{1,0:T(4,128)} %param.33) | copy-start | bytes 772
  53.4 3.8 %copy-start.11 = (s32[16,16]{1,0:T(8,128)S(1)}, s32[16,16]{1,0:T(8,128)}, u32[]{:S(2)}) copy-start(s32[16,16]{1,0:T(8,128)} %param.34) | copy-start | bytes 3076
  53.4 5.7 %copy-start.15 = (bf16[2560,80]{0,1:T(8,128)(2,1)S(1)}, bf16[2560,80]{0,1:T(8,128)(2,1)}, u32[]{:S(2)}) copy-start(bf16[2560,80]{0,1:T(8,128)(2,1)} %param.24) | copy-start | bytes 1228804
  186.5 0.7 copy-start.13
  186.6 65.5 %all-gather.5.cloned.1.call-start = ((), (), s32[]{:S(2)}) async-start(), calls=%async_computation.5 | async-start | bytes 2949120 | tf_op jit(solution)/shard_map/all_gather | solution.py:415
  227.0 78.9 %reduce-scatter.5.cloned.1.call-start = ((), (), s32[]{:S(2)}) async-start(), calls=%async_computation.6 | async-start | bytes 2949120 | tf_op jit(solution)/shard_map/reduce_scatter | solution.py:420
Sparse Core Ops, SparseCore 0:
  9.5 148.6 all-gather.2
  186.7 35.7 reduce-scatter.2
  227.1 24.9 all-gather.4
  270.7 35.1 reduce-scatter.4

commit v9 on v8

--- a/solution.py
+++ b/solution.py
@@ -295,6 +295,13 @@
         [jax.ShapeDtypeStruct((reqs, rows, head), jnp.bfloat16)],
     )
     return out
+
+
+def tp_row_sum(partial):
+    count = lax.axis_size("tp")
+    blocks = partial.astype(jnp.bfloat16).reshape((count, -1) + partial.shape[1:])
+    arrived = lax.all_to_all(blocks, "tp", 0, 0, tiled=True)
+    return jnp.sum(arrived.astype(jnp.float32), 0)
 
 
 def spans(request_ids, root_len, mid_len, leaf_len, mid_parent, leaf_parent):
@@ -399,15 +406,8 @@
     )
     tp_count = lax.axis_size("tp")
     own_count = new_rows // tp_count
-    attn_proj = (
-        lax.psum_scatter(
-            jnp.dot(attended, w_out, preferred_element_type=jnp.float32).astype(jnp.bfloat16),
-            "tp",
-            scatter_dimension=0,
-            tiled=True,
-        )
-        .astype(jnp.float32)
-        .reshape(own_count, local_reqs, model_width)
+    attn_proj = tp_row_sum(jnp.dot(attended, w_out, preferred_element_type=jnp.float32)).reshape(
+        own_count, local_reqs, model_width
     )
     own_hidden = lax.dynamic_slice_in_dim(hidden, lax.axis_index("tp") * own_count, own_count, 0)
     resid = own_hidden.astype(jnp.float32) + attn_proj
@@ -416,15 +416,8 @@
     gate_rows = jnp.dot(normed_ffn, w_gate, preferred_element_type=jnp.float32)
     up_rows = jnp.dot(normed_ffn, w_up, preferred_element_type=jnp.float32)
     activated = (jax.nn.silu(gate_rows) * up_rows).astype(jnp.bfloat16)
-    ffn_proj = (
-        lax.psum_scatter(
-            jnp.dot(activated, w_down, preferred_element_type=jnp.float32).astype(jnp.bfloat16),
-            "tp",
-            scatter_dimension=0,
-            tiled=True,
-        )
-        .astype(jnp.float32)
-        .reshape(own_count, local_reqs, model_width)
+    ffn_proj = tp_row_sum(jnp.dot(activated, w_down, preferred_element_type=jnp.float32)).reshape(
+        own_count, local_reqs, model_width
     )
     return resid + ffn_proj
 

time: 316 us -> 325 us (1.028)
  waiting for transfers between devices: 180 us -> 143 us
  blocking collectives: 0 us -> 36.8 us
  starting transfers between devices: 8.67 us -> 12.9 us
  other arithmetic: 25 us -> 28.3 us
    reduce_scatter x2 -> x0, waiting for transfers between devices: 70.6 us -> none  [the longest x1 35.3 us: shards(): lax.psum_scatter(jnp.dot(activated, w_down, preferred_element_type=jnp.fl...]
    all_to_all x0 -> x1, blocking collectives: none -> 36.8 us  [tp_row_sum(): arrived = lax.all_to_all(blocks, 'tp', 0, 0, tiled=True)]
    all_to_all x0 -> x1, waiting for transfers between devices: none -> 32.7 us  [tp_row_sum(): arrived = lax.all_to_all(blocks, 'tp', 0, 0, tiled=True)]
    all_to_all x0 -> x1, starting transfers between devices: none -> 4.54 us  [tp_row_sum(): arrived = lax.all_to_all(blocks, 'tp', 0, 0, tiled=True)]
    reduce_sum x0 -> x2, other arithmetic: none -> 3.35 us  [tp_row_sum(): return jnp.sum(arrived.astype(jnp.float32), 0)]
  transfers between devices with their start and end apart: 5 -> 4, of which waited for: 5 -> 4; matrix products, arithmetic and copies ran while one was open for 15% -> 15% of each run, Pallas kernels for 3% -> 3%
where the time goes in v9:
time: 325 us; the launch traced here: 323 us
  waiting for transfers between devices  143 us (44%)
  blocking collectives  36.8 us (11%)
  Pallas kernels  35.3 us (11%)
  other arithmetic  28.3 us (9%)
  matrix products  28 us (9%)
  local copies, waits for them, and re-layouts  24.8 us (8%)
  between operations  13.8 us (4%)
  starting transfers between devices  12.9 us (4%)
    all_to_all x1, waiting for transfers between devices, shards(): lax.all_to_all(outgoing, 'seq', split_axis=0, concat_axis=0, tiled=True)  64.4 us
    all_to_all x1, blocking collectives, tp_row_sum(): arrived = lax.all_to_all(blocks, 'tp', 0, 0, tiled=True)  36.8 us
    pallas_call x2, Pallas kernels, part_call(): pl.pallas_call(kernel, grid_spec=grid_spec, out_shape=out_shapes, compile...  35.3 us
    all_to_all x1, waiting for transfers between devices, tp_row_sum(): arrived = lax.all_to_all(blocks, 'tp', 0, 0, tiled=True)  32.7 us
    all_gather x1, waiting for transfers between devices, shards(): normed_ffn = lax.all_gather(normed_own, 'tp', axis=0, tiled=True)  24.9 us
    all_gather x1, waiting for transfers between devices, shards(): page_store = lax.all_gather(shared_pages, 'seq', axis=0, tiled=True)  20 us
    dot_general x1, matrix products, shards(): jnp.dot(activated, w_down, preferred_element_type=jnp.float32)  11.7 us
    all_to_all x1, starting transfers between devices, shards(): lax.all_to_all(outgoing, 'seq', split_axis=0, concat_axis=0, tiled=True)  8.33 us
  transfers between devices with their start and end apart: 4, of which 4 were waited for; matrix products, arithmetic and copies ran while one was open for 15% of the time, Pallas kernels for 3%

profile of v9, /device:TPU:0, one launch (start us, length us, event | category | flops | bytes accessed | tf_op | source)
XLA Modules:
  0.0 322.6 jit_solution(10811761955959525622)
XLA Ops:
  8.8 0.8 copy.95
  10.3 0.8 gather_fusion.9
  13.6 3.5 %gather_fusion.11 = bf16[128,2,80,128]{3,2,1,0:T(8,128)(2,1)} fusion(bf16[32,2,80,128]{3,2,1,0:T(8,128)(2,1)S(1)} %bitcast.87, s32[1024]{0:T(1024)S(1)} %pad_clamp_fusion), kind=kCustom, calls=%fused_computation.11 | custom fusion | bytes 10486272 | tf_op jit(solution)/shard_map/jit(_take)/gather | solution.py:383
  17.1 5.5 %select_select_fusion = bf16[16,8,1,2,80,128]{5,4,3,1,2,0:T(8,128)(2,1)} fusion(bf16[16,8,1,2,80,128]{5,4,3,1,2,0:T(8,128)(2,1)} %bitcast.86, pred[16]{0:T(512)(128)(4,1)S(1)} %reduce_or.9, pred[16,8]{1,0:T(8,128)(4,1)S(1)} %get-tuple-element.13), kind=kLoop, calls=%fused_computation.20 | loop fusion | flops 5242880 | bytes 10485904 | tf_op jit(solution)/shard_map/jit(_where)/select_n | solution.py:382
  22.6 8.3 %all-to-all-start = ((bf16[16,8,1,2,80,128]{5,4,3,1,2,0:T(8,128)(2,1)}), bf16[16,8,1,2,80,128]{5,4,3,1,2,0:T(8,128)(2,1)}, u32[]{:S(2)}, u32[]{:S(2)}) async-start(bf16[16,8,1,2,80,128]{5,4,3,1,2,0:T(8,128)(2,1)} %select_select_fusion), calls=%async_computation | async-start | bytes 10485760 | tf_op jit(solution)/shard_map/all_to_all | solution.py:385
  35.7 3.3 %fusion = f32[128,4]{1,0:T(8,128)S(1)} fusion(bf16[128,4,2560]{2,1,0:T(4,128)(2,1)} %param.21), kind=kLoop, calls=%fused_computation.15 | loop fusion | flops 3931648 | bytes 2623488 | tf_op jit(solution)/shard_map/reduce_sum | solution.py:20
  39.4 1.5 fusion.39
  40.9 1.1 fusion.3
  42.2 1.0 copy.91
  43.2 4.8 %fusion.2 = bf16[128,4,2560]{2,1,0:T(4,128)(2,1)} fusion(bf16[128,4,2560]{2,1,0:T(4,128)(2,1)} %param.21, f32[2560]{0:T(1024)S(1)} %convert_element_type.55, f32[128,4]{1,0:T(8,128)S(1)} %add_rsqrt_fusion), kind=kLoop, calls=%fused_computation.17 | loop fusion | flops 5242880 | bytes 5255168 | tf_op jit(solution)/shard_map/convert_element_type | solution.py:21
  48.0 5.3 %reshape.333 = bf16[512,2560]{1,0:T(8,128)(2,1)} reshape(bf16[128,4,2560]{2,1,0:T(4,128)(2,1)} %fusion.2) | data formatting | bytes 5242880 | tf_op jit(solution)/shard_map/reshape | solution.py:354
  53.3 2.7 convolution_convert_fusion.2
  59.0 2.7 fusion.7
  63.5 64.4 %all-to-all-done = bf16[16,8,1,2,80,128]{5,4,3,1,2,0:T(8,128)(2,1)} async-done(((bf16[16,8,1,2,80,128]{5,4,3,1,2,0:T(8,128)(2,1)}), bf16[16,8,1,2,80,128]{5,4,3,1,2,0:T(8,128)(2,1)}, u32[]{:S(2)}, u32[]{:S(2)}) %all-to-all-start) | async-done | bytes 5242912 | tf_op jit(solution)/shard_map/all_to_all | solution.py:385
  127.9 10.3 %shard_map.199 = (f32[4,512,80]{2,1,0:T(8,128)}, f32[4,512,128]{2,1,0:T(8,128)}, f32[4,512,128]{2,1,0:T(8,128)}) custom-call(s32[4,8]{1,0:T(4,128)} %iota_add_fusion.tbl, s32[4,4]{1,0:T(4,128)} %pad_add_fusion.1.meta, bf16[4,512,80]{2,1,0:T(8,128)(2,1)} %bitcast.89, bf16[4,2,80,128]{3,2,1,0:T(8,128)(2,1)} %pad_maximum_fusion.fresh_ref, ...), custom_call_target="tpu_custom_call" | custom-call | flops 671088640 | bytes 1310720 | tf_op jit(solution)/shard_map/pallas_call | solution.py:268
  138.2 20.0 %all-gather.3.cloned.1.call-done = bf16[320,1,2,80,128]{4,3,2,1,0:T(8,128)(2,1)} async-done(((bf16[20,1,2,80,128]{4,3,2,1,0:T(8,128)(2,1)}), bf16[320,1,2,80,128]{4,3,2,1,0:T(8,128)(2,1)}) %all-gather.3.cloned.1.call-update) | async-done | bytes 13107216 | tf_op jit(solution)/shard_map/all_gather | solution.py:351
  158.2 25.0 %shard_map.200 = bf16[4,512,80]{2,1,0:T(8,128)(2,1)} custom-call(s32[4,32]{1,0:T(4,128)} %pad_add_fusion.tbl, s32[4,4]{1,0:T(4,128)} %pad_add_fusion.1.meta, bf16[4,512,80]{2,1,0:T(8,128)(2,1)} %bitcast.90, f32[4,512,80]{2,1,0:T(8,128)} %get-tuple-element.10.acc_in, f32[4,512,128]{2,1,0:T(8,128)} %get-tuple-element.11.top_in, ...), custom_call_target="tpu_custom_call" | custom-call | flops 2684354560 | bytes 5242880 | tf_op jit(solution)/shard_map/pallas_call | solution.py:268
  183.2 1.4 copy.110
  185.0 3.0 convolution_convert_fusion.1
  188.0 4.5 %all-to-all-start.1 = ((bf16[8,64,2560]{2,1,0:T(8,128)(2,1)}), bf16[8,64,2560]{2,1,0:T(8,128)(2,1)}, u32[]{:S(2)}, u32[]{:S(2)}) async-start(bf16[8,64,2560]{2,1,0:T(8,128)(2,1)} %bitcast.91), calls=%async_computation.1 | async-start | bytes 5242880 | tf_op jit(solution)/shard_map/all_to_all | solution.py:303
  192.6 32.7 %all-to-all-done.1 = bf16[8,64,2560]{2,1,0:T(8,128)(2,1)} async-done(((bf16[8,64,2560]{2,1,0:T(8,128)(2,1)}), bf16[8,64,2560]{2,1,0:T(8,128)(2,1)}, u32[]{:S(2)}, u32[]{:S(2)}) %all-to-all-start.1) | async-done | bytes 2621472 | tf_op jit(solution)/shard_map/all_to_all | solution.py:303
  225.4 2.2 convert_reduce_fusion.1
  227.7 1.3 multiply_reduce_fusion
  229.0 1.2 multiply_convert_fusion.1
  230.3 0.8 reshape.343
  231.1 24.9 %all-gather.5.cloned.1.call-done = bf16[512,2560]{1,0:T(8,128)(2,1)} async-done(((bf16[64,2560]{1,0:T(8,128)(2,1)}), bf16[512,2560]{1,0:T(8,128)(2,1)}) %all-gather.5.cloned.1.call-update) | async-done | bytes 2621456 | tf_op jit(solution)/shard_map/all_gather | solution.py:415
  256.0 6.8 %fusion.28 = f32[512,864]{0,1:T(8,128)} fusion(bf16[512,2560]{1,0:T(8,128)(2,1)} %all-gather.5.cloned.1.call-done, bf16[2560,864]{0,1:T(8,128)(2,1)} %param.28), kind=kOutput, calls=%fused_computation.100 | convolution fusion | flops 2264924160 | bytes 8814592 | tf_op jit(solution)/shard_map/dot_general | solution.py:416
  262.8 11.7 %convolution_convert_fusion = bf16[512,2560]{1,0:T(8,128)(2,1)} fusion(bf16[864,2560]{1,0:T(8,128)(2,1)} %param.30, f32[512,864]{0,1:T(8,128)} %fusion.28, bf16[512,2560]{1,0:T(8,128)(2,1)} %all-gather.5.cloned.1.call-done, bf16[2560,864]{0,1:T(8,128)(2,1)} %param.29), kind=kOutput, calls=%fused_computation.21 | convolution fusion | flops 4533813248 | bytes 15859712 | tf_op jit(solution)/shard_map/dot_general | solution.py:419
  274.5 36.8 %all_to_all.15 = bf16[8,64,2560]{2,1,0:T(8,128)(2,1)S(1)} all-to-all(bf16[8,64,2560]{2,1,0:T(8,128)(2,1)} %bitcast.92), channel_id=1, replica_groups=mesh['seq'=16,'tp'=8] {'tp'}, dimensions={0} | all-to-all | bytes 5242880 | tf_op jit(solution)/shard_map/all_to_all | solution.py:303
  311.2 1.2 convert_reduce_fusion
  312.4 1.3 reshape.345
  313.7 2.0 fusion.21
  (104 shorter events, 16.0 us)
Async XLA Ops:
  6.5 178.4 %copy-start = (bf16[320,2560]{1,0:T(8,128)(2,1)S(1)}, bf16[320,2560]{1,0:T(8,128)(2,1)}, u32[]{:S(2)}) copy-start(bf16[320,2560]{1,0:T(8,128)(2,1)} %param.26) | copy-start | bytes 4915204
  6.5 151.7 %all-gather.3.cloned.1.call-start = ((), (), s32[]{:S(2)}) async-start(), calls=%async_computation.3 | async-start | bytes 13926400 | tf_op jit(solution)/shard_map/all_gather | solution.py:351
  10.3 3.3 %copy-start.9 = (bf16[32,1,2,80,128]{4,3,2,1,0:T(8,128)(2,1)S(1)}, bf16[32,1,2,80,128]{4,3,2,1,0:T(8,128)(2,1)}, u32[]{:S(2)}) copy-start(bf16[32,1,2,80,128]{4,3,2,1,0:T(8,128)(2,1)} %param.32) | copy-start | bytes 3932164
  22.6 8.4 %copy-start.2 = (s32[64]{0:T(128)S(1)}, s32[64]{0:T(128)}, u32[]{:S(2)}) copy-start(s32[64]{0:T(128)} %param.41) | copy-start | bytes 772
  22.6 9.7 %copy-start.3 = (s32[64]{0:T(128)S(1)}, s32[64]{0:T(128)}, u32[]{:S(2)}) copy-start(s32[64]{0:T(128)} %param.40) | copy-start | bytes 772
  22.6 10.4 %copy-start.4 = (s32[16]{0:T(128)S(1)}, s32[16]{0:T(128)}, u32[]{:S(2)}) copy-start(s32[16]{0:T(128)} %param.39) | copy-start | bytes 196
  22.6 11.0 %copy-start.5 = (s32[16]{0:T(128)S(1)}, s32[16]{0:T(128)}, u32[]{:S(2)}) copy-start(s32[16]{0:T(128)} %param.37) | copy-start | bytes 196
  22.6 105.3 %all-to-all-start = ((bf16[16,8,1,2,80,128]{5,4,3,1,2,0:T(8,128)(2,1)}), bf16[16,8,1,2,80,128]{5,4,3,1,2,0:T(8,128)(2,1)}, u32[]{:S(2)}, u32[]{:S(2)}) async-start(bf16[16,8,1,2,80,128]{5,4,3,1,2,0:T(8,128)(2,1)} %select_select_fusion), calls=%async_computation | async-start | bytes 10485760 | tf_op jit(solution)/shard_map/all_to_all | solution.py:385
  30.9 3.3 %copy-start.6 = (s32[64]{0:T(128)S(1)}, s32[64]{0:T(128)}, u32[]{:S(2)}) copy-start(s32[64]{0:T(128)} %param.38) | copy-start | bytes 772
  31.0 4.0 %copy-start.13 = (bf16[2560]{0:T(1024)(128)(2,1)S(1)}, bf16[2560]{0:T(1024)(128)(2,1)}, u32[]{:S(2)}) copy-start(bf16[2560]{0:T(1024)(128)(2,1)} %param.22) | copy-start | bytes 15364
  31.0 4.0 %copy-start.7 = (s32[4]{0:T(128)S(1)}, s32[4]{0:T(128)}, u32[]{:S(2)}) copy-start(s32[4]{0:T(128)} %param.36) | copy-start | bytes 52
  35.6 3.8 %copy-start.8 = (bf16[128,4,2560]{2,1,0:T(4,128)(2,1)S(1)}, bf16[128,4,2560]{2,1,0:T(4,128)(2,1)}, u32[]{:S(2)}) copy-start(bf16[128,4,2560]{2,1,0:T(4,128)(2,1)} %param.21) | copy-start | bytes 7864324
  39.4 1.5 copy-start.15
  48.0 5.4 %copy-start.10 = (bf16[2560,80]{0,1:T(8,128)(2,1)S(1)}, bf16[2560,80]{0,1:T(8,128)(2,1)}, u32[]{:S(2)}) copy-start(bf16[2560,80]{0,1:T(8,128)(2,1)} %param.25) | copy-start | bytes 1228804
  53.3 3.3 %copy-start.11 = (s32[4,16]{1,0:T(4,128)S(1)}, s32[4,16]{1,0:T(4,128)}, u32[]{:S(2)}) copy-start(s32[4,16]{1,0:T(4,128)} %param.33) | copy-start | bytes 772
  53.3 3.8 %copy-start.12 = (s32[16,16]{1,0:T(8,128)S(1)}, s32[16,16]{1,0:T(8,128)}, u32[]{:S(2)}) copy-start(s32[16,16]{1,0:T(8,128)} %param.34) | copy-start | bytes 3076
  53.3 5.7 %copy-start.16 = (bf16[2560,80]{0,1:T(8,128)(2,1)S(1)}, bf16[2560,80]{0,1:T(8,128)(2,1)}, u32[]{:S(2)}) copy-start(bf16[2560,80]{0,1:T(8,128)(2,1)} %param.24) | copy-start | bytes 1228804
  188.0 4.6 %copy-start.14 = (bf16[2560]{0:T(1024)(128)(2,1)S(1)}, bf16[2560]{0:T(1024)(128)(2,1)}, u32[]{:S(2)}) copy-start(bf16[2560]{0:T(1024)(128)(2,1)} %param.27) | copy-start | bytes 15364
  188.0 37.4 %all-to-all-start.1 = ((bf16[8,64,2560]{2,1,0:T(8,128)(2,1)}), bf16[8,64,2560]{2,1,0:T(8,128)(2,1)}, u32[]{:S(2)}, u32[]{:S(2)}) async-start(bf16[8,64,2560]{2,1,0:T(8,128)(2,1)} %bitcast.91), calls=%async_computation.1 | async-start | bytes 5242880 | tf_op jit(solution)/shard_map/all_to_all | solution.py:303
  192.6 63.4 %all-gather.5.cloned.1.call-start = ((), (), s32[]{:S(2)}) async-start(), calls=%async_computation.4 | async-start | bytes 2949120 | tf_op jit(solution)/shard_map/all_gather | solution.py:415
  311.2 4.5 %copy-start.1 = (bf16[320,2560]{1,0:T(8,128)(2,1)S(1)}, bf16[320,2560]{1,0:T(8,128)(2,1)}, u32[]{:S(2)}) copy-start(bf16[320,2560]{1,0:T(8,128)(2,1)} %param.26) | copy-start | bytes 4915204
Sparse Core Ops, SparseCore 0:
  9.5 148.6 all-gather.2
  231.2 24.7 all-gather.4

commit v10 on v9

--- a/solution.py
+++ b/solution.py
@@ -302,6 +302,23 @@
     blocks = partial.astype(jnp.bfloat16).reshape((count, -1) + partial.shape[1:])
     arrived = lax.all_to_all(blocks, "tp", 0, 0, tiled=True)
     return jnp.sum(arrived.astype(jnp.float32), 0)
+
+
+def tp_streamed_sum(rows, weight):
+    count = lax.axis_size("tp")
+    me = lax.axis_index("tp")
+    block = rows.shape[0] // count
+    total = None
+    for k in range(count):
+        target = (me + k) % count
+        part = jnp.dot(
+            lax.dynamic_slice_in_dim(rows, target * block, block, 0), weight, preferred_element_type=jnp.float32
+        ).astype(jnp.bfloat16)
+        if k:
+            part = lax.ppermute(part, "tp", [(d, (d + k) % count) for d in range(count)])
+        part = part.astype(jnp.float32)
+        total = part if total is None else total + part
+    return total
 
 
 def spans(request_ids, root_len, mid_len, leaf_len, mid_parent, leaf_parent):
@@ -416,9 +433,7 @@
     gate_rows = jnp.dot(normed_ffn, w_gate, preferred_element_type=jnp.float32)
     up_rows = jnp.dot(normed_ffn, w_up, preferred_element_type=jnp.float32)
     activated = (jax.nn.silu(gate_rows) * up_rows).astype(jnp.bfloat16)
-    ffn_proj = tp_row_sum(jnp.dot(activated, w_down, preferred_element_type=jnp.float32)).reshape(
-        own_count, local_reqs, model_width
-    )
+    ffn_proj = tp_streamed_sum(activated, w_down).reshape(own_count, local_reqs, model_width)
     return resid + ffn_proj
 
 

time: 325 us -> 322 us (level)
  blocking collectives: 36.8 us -> 0 us
  waiting for transfers between devices: 143 us -> 165 us
  starting transfers between devices: 12.9 us -> 23.4 us
  matrix products: 28 us -> 34.4 us
  Pallas kernels: 35.3 us -> 30.1 us
    all_to_all x1 -> x0, blocking collectives: 36.8 us -> none  [tp_row_sum(): arrived = lax.all_to_all(blocks, 'tp', 0, 0, tiled=True)]
    ppermute x0 -> x7, waiting for transfers between devices: none -> 17.9 us  [tp_streamed_sum(): lax.ppermute(part, 'tp', [(d, (d + k) % count) for d in range(count)])]
    ppermute x0 -> x7, starting transfers between devices: none -> 10.5 us  [tp_streamed_sum(): lax.ppermute(part, 'tp', [(d, (d + k) % count) for d in range(count)])]
    dot_general x1 -> x9, matrix products: 11.7 us -> 19.2 us  [the longest x8 14.2 us: tp_streamed_sum(): jnp.dot(lax.dynamic_slice_in_dim(rows, target * block, block, 0), weight,...]
    pallas_call x2, Pallas kernels: 35.3 us -> 30.1 us  [part_call(): pl.pallas_call(kernel, grid_spec=grid_spec, out_shape=out_shapes, compile...]
    all_gather x1, waiting for transfers between devices: 24.9 us -> 29.5 us  [shards(): normed_ffn = lax.all_gather(normed_own, 'tp', axis=0, tiled=True)]
  transfers between devices with their start and end apart: 4 -> 11, of which waited for: 4 -> 9; matrix products, arithmetic and copies ran while one was open for 15% -> 17% of each run, Pallas kernels for 3% -> 3%
where the time goes in v10:
time: 322 us; the launch traced here: 319 us
  waiting for transfers between devices  165 us (51%)
  matrix products  34.4 us (11%)
  Pallas kernels  30.1 us (9%)
  other arithmetic  27.2 us (8%)
  local copies, waits for them, and re-layouts  24.8 us (8%)
  starting transfers between devices  23.4 us (7%)
  between operations  13.9 us (4%)
    all_to_all x1, waiting for transfers between devices, shards(): lax.all_to_all(outgoing, 'seq', split_axis=0, concat_axis=0, tiled=True)  64.4 us
    all_to_all x1, waiting for transfers between devices, tp_row_sum(): arrived = lax.all_to_all(blocks, 'tp', 0, 0, tiled=True)  32.7 us
    pallas_call x2, Pallas kernels, part_call(): pl.pallas_call(kernel, grid_spec=grid_spec, out_shape=out_shapes, compile...  30.1 us
    all_gather x1, waiting for transfers between devices, shards(): normed_ffn = lax.all_gather(normed_own, 'tp', axis=0, tiled=True)  29.5 us
    all_gather x1, waiting for transfers between devices, shards(): page_store = lax.all_gather(shared_pages, 'seq', axis=0, tiled=True)  19.9 us
    ppermute x7, waiting for transfers between devices, tp_streamed_sum(): lax.ppermute(part, 'tp', [(d, (d + k) % count) for d in range(count)])  17.9 us
    dot_general x8, matrix products, tp_streamed_sum(): jnp.dot(lax.dynamic_slice_in_dim(rows, target * block, block, 0), weight,...  14.2 us
    ppermute x7, starting transfers between devices, tp_streamed_sum(): lax.ppermute(part, 'tp', [(d, (d + k) % count) for d in range(count)])  10.5 us
  transfers between devices with their start and end apart: 11, of which 9 were waited for; matrix products, arithmetic and copies ran while one was open for 17% of the time, Pallas kernels for 3%

profile of v10, /device:TPU:0, one launch (start us, length us, event | category | flops | bytes accessed | tf_op | source)
XLA Modules:
  0.0 319.0 jit_solution(5197756062089720484)
XLA Ops:
  13.6 3.5 %gather_fusion.11 = bf16[128,2,80,128]{3,2,1,0:T(8,128)(2,1)} fusion(bf16[32,2,80,128]{3,2,1,0:T(8,128)(2,1)S(1)} %bitcast.95, s32[1024]{0:T(1024)S(1)} %pad_clamp_fusion), kind=kCustom, calls=%fused_computation.11 | custom fusion | bytes 10486272 | tf_op jit(solution)/shard_map/jit(_take)/gather | solution.py:400
  17.1 5.6 %select_select_fusion = bf16[16,8,1,2,80,128]{5,4,3,1,2,0:T(8,128)(2,1)} fusion(bf16[16,8,1,2,80,128]{5,4,3,1,2,0:T(8,128)(2,1)} %bitcast.94, pred[16]{0:T(512)(128)(4,1)S(1)} %reduce_or.9, pred[16,8]{1,0:T(8,128)(4,1)S(1)} %get-tuple-element.13), kind=kLoop, calls=%fused_computation.19 | loop fusion | flops 5242880 | bytes 10485904 | tf_op jit(solution)/shard_map/jit(_where)/select_n | solution.py:399
  22.7 8.3 %all-to-all-start = ((bf16[16,8,1,2,80,128]{5,4,3,1,2,0:T(8,128)(2,1)}), bf16[16,8,1,2,80,128]{5,4,3,1,2,0:T(8,128)(2,1)}, u32[]{:S(2)}, u32[]{:S(2)}) async-start(bf16[16,8,1,2,80,128]{5,4,3,1,2,0:T(8,128)(2,1)} %select_select_fusion), calls=%async_computation | async-start | bytes 10485760 | tf_op jit(solution)/shard_map/all_to_all | solution.py:402
  35.7 3.4 %fusion = f32[128,4]{1,0:T(8,128)S(1)} fusion(bf16[128,4,2560]{2,1,0:T(4,128)(2,1)} %param.21), kind=kLoop, calls=%fused_computation.15 | loop fusion | flops 3931648 | bytes 2623488 | tf_op jit(solution)/shard_map/reduce_sum | solution.py:20
  43.3 4.8 %fusion.2 = bf16[128,4,2560]{2,1,0:T(4,128)(2,1)} fusion(bf16[128,4,2560]{2,1,0:T(4,128)(2,1)} %param.21, f32[2560]{0:T(1024)S(1)} %convert_element_type.97, f32[128,4]{1,0:T(8,128)S(1)} %add_rsqrt_fusion), kind=kLoop, calls=%fused_computation.17 | loop fusion | flops 5242880 | bytes 5255168 | tf_op jit(solution)/shard_map/convert_element_type | solution.py:21
  48.1 5.4 %reshape.330 = bf16[512,2560]{1,0:T(8,128)(2,1)} reshape(bf16[128,4,2560]{2,1,0:T(4,128)(2,1)} %fusion.2) | data formatting | bytes 5242880 | tf_op jit(solution)/shard_map/reshape | solution.py:371
  53.5 2.6 convolution_convert_fusion.9
  59.0 2.7 fusion.8
  63.5 64.4 %all-to-all-done = bf16[16,8,1,2,80,128]{5,4,3,1,2,0:T(8,128)(2,1)} async-done(((bf16[16,8,1,2,80,128]{5,4,3,1,2,0:T(8,128)(2,1)}), bf16[16,8,1,2,80,128]{5,4,3,1,2,0:T(8,128)(2,1)}, u32[]{:S(2)}, u32[]{:S(2)}) %all-to-all-start) | async-done | bytes 5242912 | tf_op jit(solution)/shard_map/all_to_all | solution.py:402
  127.9 10.3 %shard_map.199 = (f32[4,512,80]{2,1,0:T(8,128)}, f32[4,512,128]{2,1,0:T(8,128)}, f32[4,512,128]{2,1,0:T(8,128)}) custom-call(s32[4,8]{1,0:T(4,128)} %iota_add_fusion.tbl, s32[4,4]{1,0:T(4,128)} %pad_add_fusion.1.meta, bf16[4,512,80]{2,1,0:T(8,128)(2,1)} %bitcast.97, bf16[4,2,80,128]{3,2,1,0:T(8,128)(2,1)} %pad_maximum_fusion.fresh_ref, ...), custom_call_target="tpu_custom_call" | custom-call | flops 671088640 | bytes 1310720 | tf_op jit(solution)/shard_map/pallas_call | solution.py:268
  138.3 19.9 %all-gather.3.cloned.1.call-done = bf16[320,1,2,80,128]{4,3,2,1,0:T(8,128)(2,1)} async-done(((bf16[20,1,2,80,128]{4,3,2,1,0:T(8,128)(2,1)}), bf16[320,1,2,80,128]{4,3,2,1,0:T(8,128)(2,1)}) %all-gather.3.cloned.1.call-update) | async-done | bytes 13107216 | tf_op jit(solution)/shard_map/all_gather | solution.py:368
  158.2 19.8 %shard_map.200 = bf16[4,512,80]{2,1,0:T(8,128)(2,1)} custom-call(s32[4,32]{1,0:T(4,128)} %pad_add_fusion.tbl, s32[4,4]{1,0:T(4,128)} %pad_add_fusion.1.meta, bf16[4,512,80]{2,1,0:T(8,128)(2,1)} %bitcast.98, f32[4,512,80]{2,1,0:T(8,128)} %get-tuple-element.10.acc_in, f32[4,512,128]{2,1,0:T(8,128)} %get-tuple-element.11.top_in, ...), custom_call_target="tpu_custom_call" | custom-call | flops 2684354560 | bytes 5242880 | tf_op jit(solution)/shard_map/pallas_call | solution.py:268
  179.8 3.1 convolution_convert_fusion
  182.8 4.5 %all-to-all-start.1 = ((bf16[8,64,2560]{2,1,0:T(8,128)(2,1)}), bf16[8,64,2560]{2,1,0:T(8,128)(2,1)}, u32[]{:S(2)}, u32[]{:S(2)}) async-start(bf16[8,64,2560]{2,1,0:T(8,128)(2,1)} %bitcast.99), calls=%async_computation.1 | async-start | bytes 5242880 | tf_op jit(solution)/shard_map/all_to_all | solution.py:303
  187.4 32.7 %all-to-all-done.1 = bf16[8,64,2560]{2,1,0:T(8,128)(2,1)} async-done(((bf16[8,64,2560]{2,1,0:T(8,128)(2,1)}), bf16[8,64,2560]{2,1,0:T(8,128)(2,1)}, u32[]{:S(2)}, u32[]{:S(2)}) %all-to-all-start.1) | async-done | bytes 2621472 | tf_op jit(solution)/shard_map/all_to_all | solution.py:303
  220.2 2.2 convert_reduce_fusion
  226.0 29.5 %all-gather.5.cloned.1.call-done = bf16[512,2560]{1,0:T(8,128)(2,1)} async-done(((bf16[64,2560]{1,0:T(8,128)(2,1)}), bf16[512,2560]{1,0:T(8,128)(2,1)}) %all-gather.5.cloned.1.call-update) | async-done | bytes 2621456 | tf_op jit(solution)/shard_map/all_gather | solution.py:432
  255.4 5.7 %fusion.46 = f32[512,864]{0,1:T(8,128)S(1)} fusion(bf16[512,2560]{1,0:T(8,128)(2,1)} %all-gather.5.cloned.1.call-done, bf16[2560,864]{0,1:T(8,128)(2,1)} %param.28), kind=kOutput, calls=%fused_computation.123 | convolution fusion | flops 2264924160 | bytes 8814592 | tf_op jit(solution)/shard_map/dot_general | solution.py:433
  261.1 5.0 %multiply_convert_fusion = bf16[512,864]{0,1:T(8,128)(2,1)S(1)} fusion(f32[512,864]{0,1:T(8,128)S(1)} %fusion.46, bf16[512,2560]{1,0:T(8,128)(2,1)S(1)} %copy-done.15, bf16[2560,864]{0,1:T(8,128)(2,1)} %param.29), kind=kOutput, calls=%fused_computation.34 | convolution fusion | flops 2267578368 | bytes 9699328 | tf_op jit(solution)/shard_map/dot_general | solution.py:434
  266.1 3.3 %convolution_convert_fusion.7 = bf16[64,2560]{1,0:T(8,128)(2,1)S(1)} fusion(bf16[864,2560]{1,0:T(8,128)(2,1)} %param.30, bf16[512,864]{0,1:T(8,128)(2,1)S(1)} %multiply_convert_fusion, s32[]{:T(128)S(6)} %select_n.215), kind=kOutput, calls=%fused_computation.27 | convolution fusion | flops 283279360 | bytes 4972548 | tf_op jit(solution)/shard_map/dot_general | solution.py:314
  272.3 1.8 collective-permute-start.2
  275.2 2.2 collective-permute-start.3
  278.4 2.0 collective-permute-start.4
  282.4 1.8 collective-permute-start.5
  284.2 1.8 collective-permute-start.6
  286.0 6.8 %collective-permute-done.2 = bf16[64,2560]{1,0:T(8,128)(2,1)} collective-permute-done((bf16[64,2560]{1,0:T(8,128)(2,1)S(1)}, bf16[64,2560]{1,0:T(8,128)(2,1)}, u32[]{:S(2)}, u32[]{:S(2)}) %collective-permute-start.2) | collective-permute-done | bytes 327712 | tf_op jit(solution)/shard_map/ppermute | solution.py:318
  292.8 3.9 %collective-permute-done.3 = bf16[64,2560]{1,0:T(8,128)(2,1)} collective-permute-done((bf16[64,2560]{1,0:T(8,128)(2,1)S(1)}, bf16[64,2560]{1,0:T(8,128)(2,1)}, u32[]{:S(2)}, u32[]{:S(2)}) %collective-permute-start.3) | collective-permute-done | bytes 327712 | tf_op jit(solution)/shard_map/ppermute | solution.py:318
  296.7 1.9 collective-permute-done.4
  298.6 2.6 collective-permute-done.5
  301.2 2.7 collective-permute-done.6
  303.9 4.9 %convert_add_fusion = f32[64,2560]{1,0:T(8,128)} fusion(bf16[64,2560]{1,0:T(8,128)(2,1)} %collective-permute-done.6, bf16[64,2560]{1,0:T(8,128)(2,1)} %collective-permute-done.5, bf16[64,2560]{1,0:T(8,128)(2,1)} %collective-permute-done.4, bf16[64,2560]{1,0:T(8,128)(2,1)} %collective-permute-done.3, bf16[64,2560]{1,0:T(8,128)(2,1)} %collective-permute-done.2, ...), kind=kOutput, calls=%fused_computation.37 | convolution fusion | flops 285736960 | bytes 7593988 | tf_op jit(solution)/shard_map/dot_general | solution.py:314
  310.1 2.0 fusion.32
  (131 shorter events, 34.0 us)
Async XLA Ops:
  6.5 173.2 %copy-start = (bf16[320,2560]{1,0:T(8,128)(2,1)S(1)}, bf16[320,2560]{1,0:T(8,128)(2,1)}, u32[]{:S(2)}) copy-start(bf16[320,2560]{1,0:T(8,128)(2,1)} %param.26) | copy-start | bytes 4915204
  6.5 151.6 %all-gather.3.cloned.1.call-start = ((), (), s32[]{:S(2)}) async-start(), calls=%async_computation.2 | async-start | bytes 13926400 | tf_op jit(solution)/shard_map/all_gather | solution.py:368
  10.3 3.3 %copy-start.9 = (bf16[32,1,2,80,128]{4,3,2,1,0:T(8,128)(2,1)S(1)}, bf16[32,1,2,80,128]{4,3,2,1,0:T(8,128)(2,1)}, u32[]{:S(2)}) copy-start(bf16[32,1,2,80,128]{4,3,2,1,0:T(8,128)(2,1)} %param.32) | copy-start | bytes 3932164
  22.7 8.4 %copy-start.2 = (s32[64]{0:T(128)S(1)}, s32[64]{0:T(128)}, u32[]{:S(2)}) copy-start(s32[64]{0:T(128)} %param.41) | copy-start | bytes 772
  22.7 9.7 %copy-start.3 = (s32[64]{0:T(128)S(1)}, s32[64]{0:T(128)}, u32[]{:S(2)}) copy-start(s32[64]{0:T(128)} %param.40) | copy-start | bytes 772
  22.7 10.4 %copy-start.4 = (s32[16]{0:T(128)S(1)}, s32[16]{0:T(128)}, u32[]{:S(2)}) copy-start(s32[16]{0:T(128)} %param.39) | copy-start | bytes 196
  22.7 11.0 %copy-start.5 = (s32[16]{0:T(128)S(1)}, s32[16]{0:T(128)}, u32[]{:S(2)}) copy-start(s32[16]{0:T(128)} %param.37) | copy-start | bytes 196
  22.7 11.7 %copy-start.6 = (s32[64]{0:T(128)S(1)}, s32[64]{0:T(128)}, u32[]{:S(2)}) copy-start(s32[64]{0:T(128)} %param.38) | copy-start | bytes 772
  22.7 12.3 %copy-start.13 = (bf16[2560]{0:T(1024)(128)(2,1)S(1)}, bf16[2560]{0:T(1024)(128)(2,1)}, u32[]{:S(2)}) copy-start(bf16[2560]{0:T(1024)(128)(2,1)} %param.22) | copy-start | bytes 15364
  22.7 12.3 %copy-start.7 = (s32[4]{0:T(128)S(1)}, s32[4]{0:T(128)}, u32[]{:S(2)}) copy-start(s32[4]{0:T(128)} %param.36) | copy-start | bytes 52
  22.7 105.2 %all-to-all-start = ((bf16[16,8,1,2,80,128]{5,4,3,1,2,0:T(8,128)(2,1)}), bf16[16,8,1,2,80,128]{5,4,3,1,2,0:T(8,128)(2,1)}, u32[]{:S(2)}, u32[]{:S(2)}) async-start(bf16[16,8,1,2,80,128]{5,4,3,1,2,0:T(8,128)(2,1)} %select_select_fusion), calls=%async_computation | async-start | bytes 10485760 | tf_op jit(solution)/shard_map/all_to_all | solution.py:402
  35.7 3.9 %copy-start.8 = (bf16[128,4,2560]{2,1,0:T(4,128)(2,1)S(1)}, bf16[128,4,2560]{2,1,0:T(4,128)(2,1)}, u32[]{:S(2)}) copy-start(bf16[128,4,2560]{2,1,0:T(4,128)(2,1)} %param.21) | copy-start | bytes 7864324
  35.7 5.3 %copy-start.16 = (bf16[2560,320]{0,1:T(8,128)(2,1)S(1)}, bf16[2560,320]{0,1:T(8,128)(2,1)}, u32[]{:S(2)}) copy-start(bf16[2560,320]{0,1:T(8,128)(2,1)} %param.23) | copy-start | bytes 4915204
  43.3 10.2 %copy-start.10 = (bf16[2560,80]{0,1:T(8,128)(2,1)S(1)}, bf16[2560,80]{0,1:T(8,128)(2,1)}, u32[]{:S(2)}) copy-start(bf16[2560,80]{0,1:T(8,128)(2,1)} %param.25) | copy-start | bytes 1228804
  48.1 8.6 %copy-start.11 = (s32[4,16]{1,0:T(4,128)S(1)}, s32[4,16]{1,0:T(4,128)}, u32[]{:S(2)}) copy-start(s32[4,16]{1,0:T(4,128)} %param.33) | copy-start | bytes 772
  48.1 9.1 %copy-start.12 = (s32[16,16]{1,0:T(8,128)S(1)}, s32[16,16]{1,0:T(8,128)}, u32[]{:S(2)}) copy-start(s32[16,16]{1,0:T(8,128)} %param.34) | copy-start | bytes 3076
  48.1 10.9 %copy-start.17 = (bf16[2560,80]{0,1:T(8,128)(2,1)S(1)}, bf16[2560,80]{0,1:T(8,128)(2,1)}, u32[]{:S(2)}) copy-start(bf16[2560,80]{0,1:T(8,128)(2,1)} %param.24) | copy-start | bytes 1228804
  182.8 4.6 %copy-start.14 = (bf16[2560]{0:T(1024)(128)(2,1)S(1)}, bf16[2560]{0:T(1024)(128)(2,1)}, u32[]{:S(2)}) copy-start(bf16[2560]{0:T(1024)(128)(2,1)} %param.27) | copy-start | bytes 15364
  182.8 37.4 %all-to-all-start.1 = ((bf16[8,64,2560]{2,1,0:T(8,128)(2,1)}), bf16[8,64,2560]{2,1,0:T(8,128)(2,1)}, u32[]{:S(2)}, u32[]{:S(2)}) async-start(bf16[8,64,2560]{2,1,0:T(8,128)(2,1)} %bitcast.99), calls=%async_computation.1 | async-start | bytes 5242880 | tf_op jit(solution)/shard_map/all_to_all | solution.py:303
  187.4 68.1 %all-gather.5.cloned.1.call-start = ((), (), s32[]{:S(2)}) async-start(), calls=%async_computation.3 | async-start | bytes 2949120 | tf_op jit(solution)/shard_map/all_gather | solution.py:432
  255.4 5.7 %copy-start.15 = (bf16[512,2560]{1,0:T(8,128)(2,1)S(1)}, bf16[512,2560]{1,0:T(8,128)(2,1)}, u32[]{:S(2)}) copy-start(bf16[512,2560]{1,0:T(8,128)(2,1)} %all-gather.5.cloned.1.call-done) | copy-start | bytes 7864324
  255.4 14.2 %slice-start = ((s8[4423680]{0:T(1024)(128)(4,1)}), s8[4194304]{0:T(1024)(128)(4,1)S(1)}, s32[]{:S(2)}) async-start(s8[4423680]{0:T(1024)(128)(4,1)} %bitcast.92), calls=%async_computation.4 | async-start | bytes 8388608
  261.1 8.5 %slice-start.1 = ((s8[4423680]{0:T(1024)(128)(4,1)}), s8[229376]{0:T(1024)(128)(4,1)S(1)}, s32[]{:S(2)}) async-start(s8[4423680]{0:T(1024)(128)(4,1)} %bitcast.92), calls=%async_computation.5 | async-start | bytes 458752
  269.4 13.1 %collective-permute-start = (bf16[64,2560]{1,0:T(8,128)(2,1)S(1)}, bf16[64,2560]{1,0:T(8,128)(2,1)S(1)}, u32[]{:S(2)}, u32[]{:S(2)}) collective-permute-start(bf16[64,2560]{1,0:T(8,128)(2,1)S(1)} %convolution_convert_fusion.7), channel_id=1, source_target_pairs={{0,1},{1,2},{2,3},{3,4},{4,5},{5,6},{6,7},{7,0},{8,9},{9,10},{10,1... | collective-permute-start | bytes 983048 | tf_op jit(solution)/shard_map/ppermute | solution.py:318
  270.7 13.5 %collective-permute-start.1 = (bf16[64,2560]{1,0:T(8,128)(2,1)S(1)}, bf16[64,2560]{1,0:T(8,128)(2,1)}, u32[]{:S(2)}, u32[]{:S(2)}) collective-permute-start(bf16[64,2560]{1,0:T(8,128)(2,1)S(1)} %convolution_convert_fusion.6), channel_id=1, source_target_pairs={{0,2},{1,3},{2,4},{3,5},{4,6},{5,7},{6,0},{7,1},{8,10},{9,11},{10,... | collective-permute-start | bytes 983048 | tf_op jit(solution)/shard_map/ppermute | solution.py:318
  272.3 20.5 %collective-permute-start.2 = (bf16[64,2560]{1,0:T(8,128)(2,1)S(1)}, bf16[64,2560]{1,0:T(8,128)(2,1)}, u32[]{:S(2)}, u32[]{:S(2)}) collective-permute-start(bf16[64,2560]{1,0:T(8,128)(2,1)S(1)} %convolution_convert_fusion.5), channel_id=1, source_target_pairs={{0,3},{1,4},{2,5},{3,6},{4,7},{5,0},{6,1},{7,2},{8,11},{9,12},{10,... | collective-permute-start | bytes 983048 | tf_op jit(solution)/shard_map/ppermute | solution.py:318
  275.2 21.5 %collective-permute-start.3 = (bf16[64,2560]{1,0:T(8,128)(2,1)S(1)}, bf16[64,2560]{1,0:T(8,128)(2,1)}, u32[]{:S(2)}, u32[]{:S(2)}) collective-permute-start(bf16[64,2560]{1,0:T(8,128)(2,1)S(1)} %convolution_convert_fusion.4), channel_id=1, source_target_pairs={{0,4},{1,5},{2,6},{3,7},{4,0},{5,1},{6,2},{7,3},{8,12},{9,13},{10,... | collective-permute-start | bytes 983048 | tf_op jit(solution)/shard_map/ppermute | solution.py:318
  278.4 20.2 %collective-permute-start.4 = (bf16[64,2560]{1,0:T(8,128)(2,1)S(1)}, bf16[64,2560]{1,0:T(8,128)(2,1)}, u32[]{:S(2)}, u32[]{:S(2)}) collective-permute-start(bf16[64,2560]{1,0:T(8,128)(2,1)S(1)} %convolution_convert_fusion.3), channel_id=1, source_target_pairs={{0,5},{1,6},{2,7},{3,0},{4,1},{5,2},{6,3},{7,4},{8,13},{9,14},{10,... | collective-permute-start | bytes 983048 | tf_op jit(solution)/shard_map/ppermute | solution.py:318
  282.4 18.8 %collective-permute-start.5 = (bf16[64,2560]{1,0:T(8,128)(2,1)S(1)}, bf16[64,2560]{1,0:T(8,128)(2,1)}, u32[]{:S(2)}, u32[]{:S(2)}) collective-permute-start(bf16[64,2560]{1,0:T(8,128)(2,1)S(1)} %convolution_convert_fusion.2), channel_id=1, source_target_pairs={{0,6},{1,7},{2,0},{3,1},{4,2},{5,3},{6,4},{7,5},{8,14},{9,15},{10,... | collective-permute-start | bytes 983048 | tf_op jit(solution)/shard_map/ppermute | solution.py:318
  284.2 19.7 %collective-permute-start.6 = (bf16[64,2560]{1,0:T(8,128)(2,1)S(1)}, bf16[64,2560]{1,0:T(8,128)(2,1)}, u32[]{:S(2)}, u32[]{:S(2)}) collective-permute-start(bf16[64,2560]{1,0:T(8,128)(2,1)S(1)} %convolution_convert_fusion.1), channel_id=1, source_target_pairs={{0,7},{1,0},{2,1},{3,2},{4,3},{5,4},{6,5},{7,6},{8,15},{9,8},{10,9... | collective-permute-start | bytes 983048 | tf_op jit(solution)/shard_map/ppermute | solution.py:318
  303.9 8.3 %copy-start.1 = (bf16[320,2560]{1,0:T(8,128)(2,1)S(1)}, bf16[320,2560]{1,0:T(8,128)(2,1)}, u32[]{:S(2)}) copy-start(bf16[320,2560]{1,0:T(8,128)(2,1)} %param.26) | copy-start | bytes 4915204
Sparse Core Ops, SparseCore 0:
  9.5 148.6 all-gather.2
  226.0 29.3 all-gather.4

commit v11 on v8

--- a/solution.py
+++ b/solution.py
@@ -222,7 +222,7 @@
     mass_out[0] = mass[...]
 
 
-def shared_kernel(tbl, meta, q_ref, acc_in, top_in, mass_in, store_hbm, out_ref, kv, sc, top, mass, acc, sem):
+def carry_kernel(tbl, meta, q_ref, acc_in, top_in, mass_in, store_hbm, acc_out, top_out, mass_out, kv, sc, top, mass, acc, sem):
     def begin(q, query_pos, masked, scale):
         top[...] = top_in[0]
 
@@ -232,6 +232,23 @@
         acc[...] = acc_in[0] * factor[:, :1]
 
     part_body(0, False, tbl, meta, q_ref, store_hbm, kv, sc, top, mass, acc, sem, begin, finish)
+    acc_out[0] = acc[...]
+    top_out[0] = top[...]
+    mass_out[0] = mass[...]
+
+
+def shared_kernel(tbl, meta, q_ref, acc_in, top_in, mass_in, store_hbm, out_ref, kv, sc, top, mass, acc, sem):
+    def begin(q, query_pos, masked, scale):
+        top[...] = top_in[0]
+
+    def finish(row_top):
+        factor = jnp.exp(top_in[0] - row_top)
+        mass[...] = mass_in[0] * factor
+        acc[...] = acc_in[0] * factor[:, :1]
+
+    part_body(
+        ROOT_PAGES // CHUNK_PAGES, False, tbl, meta, q_ref, store_hbm, kv, sc, top, mass, acc, sem, begin, finish
+    )
     totals = jnp.sum(mass[...], -1, keepdims=True)
     out_ref[0] = (acc[...] / totals).astype(out_ref.dtype)
 
@@ -278,20 +295,21 @@
     )(tbl, meta, *inputs, store)
 
 
-def paged_attention(tbl, meta, queries, fresh, shared_store, leaf_store):
+def paged_attention(tbl, meta, queries, fresh, root_store, mid_store, leaf_store):
     reqs, rows, head = queries.shape
-    width = shared_store.shape[-1]
+    width = leaf_store.shape[-1]
     shared_count = ROOT_PAGES + MID_PAGES
+    state_shapes = [
+        jax.ShapeDtypeStruct((reqs, rows, head), jnp.float32),
+        jax.ShapeDtypeStruct((reqs, rows, width), jnp.float32),
+        jax.ShapeDtypeStruct((reqs, rows, width), jnp.float32),
+    ]
+    state = part_call(leaf_kernel, tbl[:, shared_count:], meta, [queries, fresh], None, leaf_store, state_shapes)
     state = part_call(
-        leaf_kernel, tbl[:, shared_count:], meta, [queries, fresh], None, leaf_store,
-        [
-            jax.ShapeDtypeStruct((reqs, rows, head), jnp.float32),
-            jax.ShapeDtypeStruct((reqs, rows, width), jnp.float32),
-            jax.ShapeDtypeStruct((reqs, rows, width), jnp.float32),
-        ],
+        carry_kernel, tbl[:, :ROOT_PAGES], meta, [queries] + list(state), None, root_store, state_shapes
     )
     (out,) = part_call(
-        shared_kernel, tbl[:, :shared_count], meta, [queries] + list(state), None, shared_store,
+        shared_kernel, tbl[:, ROOT_PAGES:shared_count], meta, [queries] + list(state), None, mid_store,
         [jax.ShapeDtypeStruct((reqs, rows, head), jnp.bfloat16)],
     )
     return out
@@ -341,9 +359,19 @@
     new_index = jnp.arange(new_rows, dtype=jnp.int32)
     query_pos = context[None, :] + new_index[:, None]
     all_slots = slot_request.reshape(seq_count, local_reqs)
-    page_store = lax.all_gather(shared_pages, "seq", axis=0, tiled=True)
-    root_index = root_table[root_nodes]
-    mid_index = mid_table[mid_nodes]
+    per_index = shared_pages.shape[0]
+    root_home = root_table // per_index
+    root_local = jnp.take_along_axis(
+        root_table, jnp.argmax(root_home == seq_index, 1)[:, None], 1
+    )[:, 0] - seq_index * per_index
+    mid_home = mid_table // per_index
+    mid_local = jnp.take_along_axis(
+        mid_table, jnp.argmax(mid_home == seq_index, 1)[:, None], 1
+    )[:, 0] - seq_index * per_index
+    root_gathered = lax.all_gather(jnp.take(shared_pages, root_local, axis=0), "seq", axis=0, tiled=True)
+    mid_gathered = lax.all_gather(jnp.take(shared_pages, mid_local, axis=0), "seq", axis=0, tiled=True)
+    root_count = root_table.shape[0]
+    mid_count = mid_table.shape[0]
     normed = rms_norm(hidden, gain_attn).reshape(-1, model_width)
     query_proj = jnp.dot(normed, w_query, preferred_element_type=jnp.float32).reshape(
         new_rows, local_reqs, -1, HD
@@ -378,11 +406,12 @@
     arrived = lax.all_to_all(outgoing, "seq", split_axis=0, concat_axis=0, tiled=True)
     page_shape = arrived.shape[-3:]
     leaf_store = arrived.reshape((-1,) + page_shape)
-    shared_store = page_store.reshape((-1,) + page_shape)
+    root_store = root_gathered.reshape((-1,) + page_shape)
+    mid_store = mid_gathered.reshape((-1,) + page_shape)
     tbl = jnp.concatenate(
         [
-            root_index,
-            mid_index,
+            root_home[root_nodes] * root_count + root_nodes[:, None],
+            mid_home[mid_nodes] * mid_count + mid_nodes[:, None],
             own_homes[:, None] * leaf_slots + jnp.arange(leaf_slots, dtype=jnp.int32)[None, :],
         ],
         1,
@@ -392,7 +421,7 @@
         [jnp.transpose(new_keys[:, :, 0], (1, 2, 0)), jnp.transpose(new_values[:, :, 0], (1, 2, 0))], 1
     )
     query_rows = jnp.transpose(queries[:, :, 0], (1, 2, 0, 3)).reshape(local_reqs, -1, HD)
-    attended = paged_attention(tbl, meta, query_rows, fresh_pack, shared_store, leaf_store)
+    attended = paged_attention(tbl, meta, query_rows, fresh_pack, root_store, mid_store, leaf_store)
     attended = (
         jnp.transpose(attended.reshape(local_reqs, group_size, new_rows, HD), (2, 0, 1, 3))
         .reshape(new_rows * local_reqs, -1)

time: 316 us -> 342 us (1.082)
  waiting for transfers between devices: 180 us -> 192 us
  other arithmetic: 25 us -> 30.4 us
  local copies, waits for them, and re-layouts: 26.3 us -> 31.4 us
    all_gather x1 -> x2, waiting for transfers between devices: 19.4 us -> 40 us  [the longest x1 39.9 us: shards(): lax.all_gather(jnp.take(shared_pages, mid_local, axis=0), 'seq', axis=0,...]
    all_to_all x1, waiting for transfers between devices: 64.3 us -> 53.1 us  [shards(): lax.all_to_all(outgoing, 'seq', split_axis=0, concat_axis=0, tiled=True)]
    gather x2 -> x6, local copies, waits for them, and re-layouts: 1.12 us -> 7.45 us  [the longest x1 2.61 us: shards(): jnp.take(shared_pages, mid_local, axis=0)]
    pallas_call x2 -> x3, Pallas kernels: 34.4 us -> 36.5 us  [part_call(): pl.pallas_call(kernel, grid_spec=grid_spec, out_shape=out_shapes, compile...]
  transfers between devices with their start and end apart: 5 -> 6, of which waited for: 5 -> 5; matrix products, arithmetic and copies ran while one was open for 15% -> 16% of each run, Pallas kernels for 3% -> 8%
where the time goes in v11:
time: 342 us; the launch traced here: 341 us
  waiting for transfers between devices  192 us (56%)
  Pallas kernels  36.5 us (11%)
  local copies, waits for them, and re-layouts  31.4 us (9%)
  other arithmetic  30.4 us (9%)
  matrix products  28.1 us (8%)
  between operations  13.5 us (4%)
  starting transfers between devices  8.74 us (3%)
    all_to_all x1, waiting for transfers between devices, shards(): lax.all_to_all(outgoing, 'seq', split_axis=0, concat_axis=0, tiled=True)  53.1 us
    all_gather x1, waiting for transfers between devices, shards(): lax.all_gather(jnp.take(shared_pages, mid_local, axis=0), 'seq', axis=0,...  39.9 us
    reduce_scatter x1, waiting for transfers between devices, shards(): lax.psum_scatter(jnp.dot(attended, w_out, preferred_element_type=jnp.floa...  38.6 us
    pallas_call x3, Pallas kernels, part_call(): pl.pallas_call(kernel, grid_spec=grid_spec, out_shape=out_shapes, compile...  36.5 us
    reduce_scatter x1, waiting for transfers between devices, shards(): lax.psum_scatter(jnp.dot(activated, w_down, preferred_element_type=jnp.fl...  35.3 us
    all_gather x1, waiting for transfers between devices, shards(): normed_ffn = lax.all_gather(normed_own, 'tp', axis=0, tiled=True)  24.8 us
    dot_general x1, matrix products, shards(): jnp.dot(activated, w_down, preferred_element_type=jnp.float32)  11.7 us
    all_to_all x1, starting transfers between devices, shards(): lax.all_to_all(outgoing, 'seq', split_axis=0, concat_axis=0, tiled=True)  8.35 us
  transfers between devices with their start and end apart: 6, of which 5 were waited for; matrix products, arithmetic and copies ran while one was open for 16% of the time, Pallas kernels for 8%

profile of v11, /device:TPU:0, one launch (start us, length us, event | category | flops | bytes accessed | tf_op | source)
XLA Modules:
  0.0 340.6 jit_solution(2862967185791029492)
XLA Ops:
  6.5 1.4 iota_reduce_fusion.2
  8.0 1.3 gather_fusion.15
  9.4 1.7 gather_fusion.12
  16.4 2.6 gather_fusion.13
  19.0 2.0 bitcast_select_fusion
  23.0 3.6 %gather_fusion.11 = bf16[128,2,80,128]{3,2,1,0:T(8,128)(2,1)} fusion(bf16[32,2,80,128]{3,2,1,0:T(8,128)(2,1)S(1)} %bitcast.103, s32[1024]{0:T(1024)S(1)} %pad_clamp_fusion.2), kind=kCustom, calls=%fused_computation.11 | custom fusion | bytes 10486272 | tf_op jit(solution)/shard_map/jit(_take)/gather | solution.py:404
  26.6 5.4 %select_select_fusion = bf16[16,8,1,2,80,128]{5,4,3,1,2,0:T(8,128)(2,1)} fusion(bf16[16,8,1,2,80,128]{5,4,3,1,2,0:T(8,128)(2,1)} %bitcast.102, pred[16]{0:T(512)(128)(4,1)S(1)} %reduce_or.9, pred[16,8]{1,0:T(8,128)(4,1)S(1)} %get-tuple-element.27), kind=kLoop, calls=%fused_computation.22 | loop fusion | flops 5242880 | bytes 10485904 | tf_op jit(solution)/shard_map/jit(_where)/select_n | solution.py:403
  32.0 8.3 %all-to-all-start = ((bf16[16,8,1,2,80,128]{5,4,3,1,2,0:T(8,128)(2,1)}), bf16[16,8,1,2,80,128]{5,4,3,1,2,0:T(8,128)(2,1)}, u32[]{:S(2)}, u32[]{:S(2)}) async-start(bf16[16,8,1,2,80,128]{5,4,3,1,2,0:T(8,128)(2,1)} %select_select_fusion), calls=%async_computation | async-start | bytes 10485760 | tf_op jit(solution)/shard_map/all_to_all | solution.py:406
  45.2 3.3 fusion
  48.9 1.5 fusion.45
  50.4 1.1 fusion.3
  52.7 4.7 %fusion.2 = bf16[128,4,2560]{2,1,0:T(4,128)(2,1)} fusion(bf16[128,4,2560]{2,1,0:T(4,128)(2,1)} %param.21, f32[2560]{0:T(1024)S(1)} %convert_element_type.51, f32[128,4]{1,0:T(8,128)S(1)} %add_rsqrt_fusion), kind=kLoop, calls=%fused_computation.21 | loop fusion | flops 5242880 | bytes 5255168 | tf_op jit(solution)/shard_map/convert_element_type | solution.py:21
  57.4 5.4 %reshape.408 = bf16[512,2560]{1,0:T(8,128)(2,1)} reshape(bf16[128,4,2560]{2,1,0:T(4,128)(2,1)} %fusion.2) | data formatting | bytes 5242880 | tf_op jit(solution)/shard_map/reshape | solution.py:375
  62.8 2.7 convolution_convert_fusion.2
  67.9 2.8 fusion.7
  73.6 53.1 %all-to-all-done = bf16[16,8,1,2,80,128]{5,4,3,1,2,0:T(8,128)(2,1)} async-done(((bf16[16,8,1,2,80,128]{5,4,3,1,2,0:T(8,128)(2,1)}), bf16[16,8,1,2,80,128]{5,4,3,1,2,0:T(8,128)(2,1)}, u32[]{:S(2)}, u32[]{:S(2)}) %all-to-all-start) | async-done | bytes 5242912 | tf_op jit(solution)/shard_map/all_to_all | solution.py:406
  126.7 10.3 %shard_map.199 = (f32[4,512,80]{2,1,0:T(8,128)}, f32[4,512,128]{2,1,0:T(8,128)}, f32[4,512,128]{2,1,0:T(8,128)}) custom-call(s32[4,8]{1,0:T(4,128)} %iota_add_fusion.tbl, s32[4,4]{1,0:T(4,128)} %pad_add_fusion.meta, bf16[4,512,80]{2,1,0:T(8,128)(2,1)} %bitcast.105, bf16[4,2,80,128]{3,2,1,0:T(8,128)(2,1)} %pad_maximum_fusion.fresh_ref, ...), custom_call_target="tpu_custom_call" | custom-call | flops 671088640 | bytes 1310720 | tf_op jit(solution)/shard_map/pallas_call | solution.py:285
  137.1 16.5 %shard_map.200 = (f32[4,512,80]{2,1,0:T(8,128)}, f32[4,512,128]{2,1,0:T(8,128)}, f32[4,512,128]{2,1,0:T(8,128)}) custom-call(s32[4,16]{1,0:T(4,128)} %multiply_add_fusion.tbl, s32[4,4]{1,0:T(4,128)} %pad_add_fusion.meta, bf16[4,512,80]{2,1,0:T(8,128)(2,1)} %bitcast.106, f32[4,512,80]{2,1,0:T(8,128)} %get-tuple-element.15.acc_in, ...), custom_call_target="tpu_custom_call" | custom-call | flops 1342177280 | bytes 2621440 | tf_op jit(solution)/shard_map/pallas_call | solution.py:285
  153.6 39.9 %all-gather.6.cloned.1.call-done = bf16[256,1,2,80,128]{4,3,2,1,0:T(8,128)(2,1)} async-done(((bf16[16,1,2,80,128]{4,3,2,1,0:T(8,128)(2,1)}), bf16[256,1,2,80,128]{4,3,2,1,0:T(8,128)(2,1)}) %all-gather.6.cloned.1.call-update) | async-done | bytes 10485776 | tf_op jit(solution)/shard_map/all_gather | solution.py:372
  193.5 9.7 %shard_map.201 = bf16[4,512,80]{2,1,0:T(8,128)(2,1)} custom-call(s32[4,16]{1,0:T(4,128)} %multiply_add_fusion.1.tbl, s32[4,4]{1,0:T(4,128)} %pad_add_fusion.meta, bf16[4,512,80]{2,1,0:T(8,128)(2,1)} %bitcast.107, f32[4,512,80]{2,1,0:T(8,128)} %get-tuple-element.19.acc_in, f32[4,512,128]{2,1,0:T(8,128)} %get-tuple-element.20.top_in, ...), custom_call_target="tpu_custom_call" | custom-call | flops 1342177280 | bytes 2621440 | tf_op jit(solution)/shard_map/pallas_call | solution.py:285
  203.2 1.5 copy.108
  205.0 3.0 convolution_convert_fusion.1
  208.8 38.6 %reduce-scatter.3.cloned.1.call-done = bf16[64,2560]{1,0:T(8,128)(2,1)} async-done(((bf16[512,2560]{1,0:T(8,128)(2,1)}), bf16[64,2560]{1,0:T(8,128)(2,1)}) %reduce-scatter.3.cloned.1.call-update) | async-done | bytes 327696 | tf_op jit(solution)/shard_map/reduce_scatter | solution.py:432
  247.3 1.2 reshape.425
  248.5 1.3 multiply_reduce_fusion
  249.8 1.2 multiply_convert_fusion.1
  252.1 24.8 %all-gather.8.cloned.1.call-done = bf16[512,2560]{1,0:T(8,128)(2,1)} async-done(((bf16[64,2560]{1,0:T(8,128)(2,1)}), bf16[512,2560]{1,0:T(8,128)(2,1)}) %all-gather.8.cloned.1.call-update) | async-done | bytes 2621456 | tf_op jit(solution)/shard_map/all_gather | solution.py:444
  277.0 6.8 %fusion.34 = f32[512,864]{0,1:T(8,128)} fusion(bf16[512,2560]{1,0:T(8,128)(2,1)} %all-gather.8.cloned.1.call-done, bf16[2560,864]{0,1:T(8,128)(2,1)} %param.28), kind=kOutput, calls=%fused_computation.133 | convolution fusion | flops 2264924160 | bytes 8814592 | tf_op jit(solution)/shard_map/dot_general | solution.py:445
  283.8 11.7 %convolution_convert_fusion = bf16[512,2560]{1,0:T(8,128)(2,1)} fusion(bf16[864,2560]{1,0:T(8,128)(2,1)} %param.30, f32[512,864]{0,1:T(8,128)} %fusion.34, bf16[512,2560]{1,0:T(8,128)(2,1)} %all-gather.8.cloned.1.call-done, bf16[2560,864]{0,1:T(8,128)(2,1)} %param.29), kind=kOutput, calls=%fused_computation.23 | convolution fusion | flops 4533813248 | bytes 15859712 | tf_op jit(solution)/shard_map/dot_general | solution.py:450
  295.5 35.3 %reduce-scatter.5.cloned.1.call-done = bf16[64,2560]{1,0:T(8,128)(2,1)} async-done(((bf16[512,2560]{1,0:T(8,128)(2,1)}), bf16[64,2560]{1,0:T(8,128)(2,1)}) %reduce-scatter.5.cloned.1.call-update) | async-done | bytes 327696 | tf_op jit(solution)/shard_map/reduce_scatter | solution.py:449
  330.8 1.2 reshape.427
  332.0 2.0 fusion.21
  (129 shorter events, 20.9 us)
Async XLA Ops:
  6.5 198.5 %copy-start = (bf16[320,2560]{1,0:T(8,128)(2,1)S(1)}, bf16[320,2560]{1,0:T(8,128)(2,1)}, u32[]{:S(2)}) copy-start(bf16[320,2560]{1,0:T(8,128)(2,1)} %param.26) | copy-start | bytes 4915204
  6.5 130.5 %all-gather.4.cloned.1.call-start = ((), (), s32[]{:S(2)}) async-start(), calls=%async_computation.3 | async-start | bytes 2785280 | tf_op jit(solution)/shard_map/all_gather | solution.py:371
  11.9 181.6 %all-gather.6.cloned.1.call-start = ((), (), s32[]{:S(2)}) async-start(), calls=%async_computation.4 | async-start | bytes 11141120 | tf_op jit(solution)/shard_map/all_gather | solution.py:372
  13.5 1.6 copy-start.8
  14.3 6.8 %copy-start.1 = (s32[64]{0:T(128)S(1)}, s32[64]{0:T(128)}, u32[]{:S(2)}) copy-start(s32[64]{0:T(128)} %param.41) | copy-start | bytes 772
  14.3 6.9 %copy-start.14 = (s32[64,8]{0,1:T(8,128)S(1)}, s32[64,8]{0,1:T(8,128)}, u32[]{:S(2)}) copy-start(s32[64,8]{0,1:T(8,128)} %param.35) | copy-start | bytes 6148
  14.3 8.7 %copy-start.10 = (bf16[32,1,2,80,128]{4,3,2,1,0:T(8,128)(2,1)S(1)}, bf16[32,1,2,80,128]{4,3,2,1,0:T(8,128)(2,1)}, u32[]{:S(2)}) copy-start(bf16[32,1,2,80,128]{4,3,2,1,0:T(8,128)(2,1)} %param.32) | copy-start | bytes 3932164
  32.0 9.8 %copy-start.2 = (s32[64]{0:T(128)S(1)}, s32[64]{0:T(128)}, u32[]{:S(2)}) copy-start(s32[64]{0:T(128)} %param.40) | copy-start | bytes 772
  32.0 10.4 %copy-start.3 = (s32[16]{0:T(128)S(1)}, s32[16]{0:T(128)}, u32[]{:S(2)}) copy-start(s32[16]{0:T(128)} %param.39) | copy-start | bytes 196
  32.0 11.1 %copy-start.4 = (s32[16]{0:T(128)S(1)}, s32[16]{0:T(128)}, u32[]{:S(2)}) copy-start(s32[16]{0:T(128)} %param.37) | copy-start | bytes 196
  32.0 94.7 %all-to-all-start = ((bf16[16,8,1,2,80,128]{5,4,3,1,2,0:T(8,128)(2,1)}), bf16[16,8,1,2,80,128]{5,4,3,1,2,0:T(8,128)(2,1)}, u32[]{:S(2)}, u32[]{:S(2)}) async-start(bf16[16,8,1,2,80,128]{5,4,3,1,2,0:T(8,128)(2,1)} %select_select_fusion), calls=%async_computation | async-start | bytes 10485760 | tf_op jit(solution)/shard_map/all_to_all | solution.py:406
  40.4 3.4 copy-start.5
  40.4 4.0 %copy-start.12 = (bf16[2560]{0:T(1024)(128)(2,1)S(1)}, bf16[2560]{0:T(1024)(128)(2,1)}, u32[]{:S(2)}) copy-start(bf16[2560]{0:T(1024)(128)(2,1)} %param.22) | copy-start | bytes 15364
  40.4 4.0 %copy-start.6 = (s32[4]{0:T(128)S(1)}, s32[4]{0:T(128)}, u32[]{:S(2)}) copy-start(s32[4]{0:T(128)} %param.36) | copy-start | bytes 52
  40.4 206.9 %reduce-scatter.3.cloned.1.call-start = ((), (), s32[]{:S(2)}) async-start(), calls=%async_computation.5 | async-start | bytes 2949120 | tf_op jit(solution)/shard_map/reduce_scatter | solution.py:432
  45.1 3.8 %copy-start.9 = (bf16[128,4,2560]{2,1,0:T(4,128)(2,1)S(1)}, bf16[128,4,2560]{2,1,0:T(4,128)(2,1)}, u32[]{:S(2)}) copy-start(bf16[128,4,2560]{2,1,0:T(4,128)(2,1)} %param.21) | copy-start | bytes 7864324
  48.9 1.5 copy-start.15
  57.4 5.4 %copy-start.11 = (bf16[2560,80]{0,1:T(8,128)(2,1)S(1)}, bf16[2560,80]{0,1:T(8,128)(2,1)}, u32[]{:S(2)}) copy-start(bf16[2560,80]{0,1:T(8,128)(2,1)} %param.25) | copy-start | bytes 1228804
  62.8 3.2 copy-start.7
  62.8 5.1 %copy-start.16 = (bf16[2560,80]{0,1:T(8,128)(2,1)S(1)}, bf16[2560,80]{0,1:T(8,128)(2,1)}, u32[]{:S(2)}) copy-start(bf16[2560,80]{0,1:T(8,128)(2,1)} %param.24) | copy-start | bytes 1228804
  208.1 0.7 copy-start.13
  208.1 68.9 %all-gather.8.cloned.1.call-start = ((), (), s32[]{:S(2)}) async-start(), calls=%async_computation.6 | async-start | bytes 2949120 | tf_op jit(solution)/shard_map/all_gather | solution.py:444
  251.9 79.0 %reduce-scatter.5.cloned.1.call-start = ((), (), s32[]{:S(2)}) async-start(), calls=%async_computation.7 | async-start | bytes 2949120 | tf_op jit(solution)/shard_map/reduce_scatter | solution.py:449
Sparse Core Ops, SparseCore 0:
  12.0 97.6 all-gather.3
  111.9 81.5 all-gather.5
  208.2 39.0 reduce-scatter.2
  252.0 24.9 all-gather.7
  295.6 35.1 reduce-scatter.4

commit v12 on v8

--- a/solution.py
+++ b/solution.py
@@ -1,3 +1,5 @@
+import functools
+
 import jax
 import jax.numpy as jnp
 from jax import lax
@@ -193,7 +195,7 @@
     lax.fori_loop(0, chunks, sum_body, 0)
 
 
-def leaf_kernel(tbl, meta, q_ref, fresh_ref, store_hbm, acc_out, top_out, mass_out, kv, sc, fresh_sc, top, mass, acc, sem):
+def leaf_kernel(chunk0, tbl, meta, q_ref, fresh_ref, store_hbm, acc_out, top_out, mass_out, kv, sc, fresh_sc, top, mass, acc, sem):
     def begin(q, query_pos, masked, scale):
         width = fresh_sc.shape[-1]
         fresh_lanes = lax.broadcasted_iota(jnp.int32, (1, width), 1)
@@ -214,7 +216,7 @@
         )
 
     part_body(
-        (ROOT_PAGES + MID_PAGES) // CHUNK_PAGES, True, tbl, meta, q_ref, store_hbm, kv, sc, top, mass, acc, sem,
+        chunk0, True, tbl, meta, q_ref, store_hbm, kv, sc, top, mass, acc, sem,
         begin, finish,
     )
     acc_out[0] = acc[...]
@@ -222,7 +224,7 @@
     mass_out[0] = mass[...]
 
 
-def shared_kernel(tbl, meta, q_ref, acc_in, top_in, mass_in, store_hbm, out_ref, kv, sc, top, mass, acc, sem):
+def shared_kernel(chunk0, tbl, meta, q_ref, acc_in, top_in, mass_in, store_hbm, out_ref, kv, sc, top, mass, acc, sem):
     def begin(q, query_pos, masked, scale):
         top[...] = top_in[0]
 
@@ -231,7 +233,7 @@
         mass[...] = mass_in[0] * factor
         acc[...] = acc_in[0] * factor[:, :1]
 
-    part_body(0, False, tbl, meta, q_ref, store_hbm, kv, sc, top, mass, acc, sem, begin, finish)
+    part_body(chunk0, False, tbl, meta, q_ref, store_hbm, kv, sc, top, mass, acc, sem, begin, finish)
     totals = jnp.sum(mass[...], -1, keepdims=True)
     out_ref[0] = (acc[...] / totals).astype(out_ref.dtype)
 
@@ -249,7 +251,7 @@
         pltpu.VMEM((2, pages) + page_shape, store.dtype),
         pltpu.VMEM((pages // CHUNK_PAGES, rows, CHUNK_PAGES * width), jnp.float32),
     ]
-    if kernel is leaf_kernel:
+    if kernel.func is leaf_kernel:
         scratch.append(pltpu.VMEM((rows, width), jnp.float32))
     scratch += [
         pltpu.VMEM((rows, width), jnp.float32),
@@ -283,7 +285,7 @@
     width = shared_store.shape[-1]
     shared_count = ROOT_PAGES + MID_PAGES
     state = part_call(
-        leaf_kernel, tbl[:, shared_count:], meta, [queries, fresh], None, leaf_store,
+        functools.partial(leaf_kernel, 0), tbl[:, :shared_count], meta, [queries, fresh], None, shared_store,
         [
             jax.ShapeDtypeStruct((reqs, rows, head), jnp.float32),
             jax.ShapeDtypeStruct((reqs, rows, width), jnp.float32),
@@ -291,7 +293,8 @@
         ],
     )
     (out,) = part_call(
-        shared_kernel, tbl[:, :shared_count], meta, [queries] + list(state), None, shared_store,
+        functools.partial(shared_kernel, shared_count // CHUNK_PAGES), tbl[:, shared_count:], meta,
+        [queries] + list(state), None, leaf_store,
         [jax.ShapeDtypeStruct((reqs, rows, head), jnp.bfloat16)],
     )
     return out
@@ -375,6 +378,7 @@
     outgoing = jnp.where(
         sender_have[:, None, None, None, None, None], jnp.take(leaf_pages, page_ids, axis=0), 0
     )
+    outgoing, page_store = lax.optimization_barrier((outgoing, page_store))
     arrived = lax.all_to_all(outgoing, "seq", split_axis=0, concat_axis=0, tiled=True)
     page_shape = arrived.shape[-3:]
     leaf_store = arrived.reshape((-1,) + page_shape)

time: 316 us -> 333 us (1.054)
  waiting for transfers between devices: 180 us -> 197 us
    all_gather x1, waiting for transfers between devices: 19.4 us -> 74.1 us  [shards(): page_store = lax.all_gather(shared_pages, 'seq', axis=0, tiled=True)]
    all_to_all x1, waiting for transfers between devices: 64.3 us -> 27.8 us  [shards(): lax.all_to_all(outgoing, 'seq', split_axis=0, concat_axis=0, tiled=True)]
  transfers between devices with their start and end apart: 5 -> 5, of which waited for: 5 -> 5; matrix products, arithmetic and copies ran while one was open for 15% -> 15% of each run, Pallas kernels for 3% -> 7%
where the time goes in v12:
time: 333 us; the launch traced here: 331 us
  waiting for transfers between devices  197 us (59%)
  Pallas kernels  33.4 us (10%)
  matrix products  28 us (8%)
  local copies, waits for them, and re-layouts  27.4 us (8%)
  other arithmetic  26.1 us (8%)
  between operations  13.4 us (4%)
  starting transfers between devices  5.89 us (2%)
    all_gather x1, waiting for transfers between devices, shards(): page_store = lax.all_gather(shared_pages, 'seq', axis=0, tiled=True)  74.1 us
    reduce_scatter x1, waiting for transfers between devices, shards(): lax.psum_scatter(jnp.dot(activated, w_down, preferred_element_type=jnp.fl...  35.3 us
    reduce_scatter x1, waiting for transfers between devices, shards(): lax.psum_scatter(jnp.dot(attended, w_out, preferred_element_type=jnp.floa...  34.3 us
    pallas_call x2, Pallas kernels, part_call(): pl.pallas_call(kernel, grid_spec=grid_spec, out_shape=out_shapes, compile...  33.4 us
    all_to_all x1, waiting for transfers between devices, shards(): lax.all_to_all(outgoing, 'seq', split_axis=0, concat_axis=0, tiled=True)  27.8 us
    all_gather x1, waiting for transfers between devices, shards(): normed_ffn = lax.all_gather(normed_own, 'tp', axis=0, tiled=True)  25.1 us
    dot_general x1, matrix products, shards(): jnp.dot(activated, w_down, preferred_element_type=jnp.float32)  11.7 us
    convert_element_type x3, other arithmetic, rms_norm(): (values * inverse_rms * gain_vector.astype(jnp.float32)).astype(jnp.bfloa...  9.3 us
  transfers between devices with their start and end apart: 5, of which 5 were waited for; matrix products, arithmetic and copies ran while one was open for 15% of the time, Pallas kernels for 7%

profile of v12, /device:TPU:0, one launch (start us, length us, event | category | flops | bytes accessed | tf_op | source)
XLA Modules:
  0.0 331.5 jit_solution(7555183638199827792)
XLA Ops:
  8.8 1.3 gather_fusion
  10.1 1.3 gather_fusion.6
  11.4 1.3 gather_fusion.2
  14.2 0.8 gather_fusion.9
  18.2 3.5 %gather_fusion.11 = bf16[128,2,80,128]{3,2,1,0:T(8,128)(2,1)} fusion(bf16[32,2,80,128]{3,2,1,0:T(8,128)(2,1)S(1)} %bitcast.85, s32[1024]{0:T(1024)S(1)} %pad_clamp_fusion), kind=kCustom, calls=%fused_computation.11 | custom fusion | bytes 10486272 | tf_op jit(solution)/shard_map/jit(_take)/gather | solution.py:379
  21.7 3.4 %fusion = f32[128,4]{1,0:T(8,128)S(1)} fusion(bf16[128,4,2560]{2,1,0:T(4,128)(2,1)} %param.21), kind=kLoop, calls=%fused_computation.15 | loop fusion | flops 3931648 | bytes 2623488 | tf_op jit(solution)/shard_map/reduce_sum | solution.py:22
  25.2 5.5 %select_select_fusion = bf16[16,8,1,2,80,128]{5,4,3,1,2,0:T(8,128)(2,1)} fusion(bf16[16,8,1,2,80,128]{5,4,3,1,2,0:T(8,128)(2,1)} %bitcast.84, pred[16]{0:T(512)(128)(4,1)S(1)} %reduce_or.9, pred[16,8]{1,0:T(8,128)(4,1)S(1)} %get-tuple-element.17), kind=kLoop, calls=%fused_computation.18 | loop fusion | flops 5242880 | bytes 10485904 | tf_op jit(solution)/shard_map/jit(_where)/select_n | solution.py:378
  30.7 74.1 %all-gather.3.cloned.1.call-done = bf16[320,1,2,80,128]{4,3,2,1,0:T(8,128)(2,1)} async-done(((bf16[20,1,2,80,128]{4,3,2,1,0:T(8,128)(2,1)}), bf16[320,1,2,80,128]{4,3,2,1,0:T(8,128)(2,1)}) %all-gather.3.cloned.1.call-update) | async-done | bytes 13107216 | tf_op jit(solution)/shard_map/all_gather | solution.py:347
  104.7 5.3 %all-to-all-start = ((bf16[16,8,1,2,80,128]{5,4,3,1,2,0:T(8,128)(2,1)}), bf16[16,8,1,2,80,128]{5,4,3,1,2,0:T(8,128)(2,1)}, u32[]{:S(2)}, u32[]{:S(2)}) async-start(bf16[16,8,1,2,80,128]{5,4,3,1,2,0:T(8,128)(2,1)} %select_select_fusion), calls=%async_computation | async-start | bytes 10485760 | tf_op jit(solution)/shard_map/all_to_all | solution.py:382
  111.6 3.3 %fusion.39 = bf16[128,4,2560,1]{2,1,0,3:T(4,128)(2,1)S(1)} fusion(f32[2560]{0:T(1024)S(1)} %convert_element_type.51, f32[128,4]{1,0:T(8,128)S(1)} %add_rsqrt_fusion, bf16[128,4,2560]{2,1,0:T(4,128)(2,1)} %param.21), kind=kLoop, calls=%fused_computation.99 | loop fusion | flops 5242880 | bytes 5255168 | tf_op jit(solution)/shard_map/convert_element_type | solution.py:23
  115.0 1.1 fusion.3
  116.2 1.0 copy.91
  118.4 4.7 %fusion.2 = bf16[128,4,2560]{2,1,0:T(4,128)(2,1)} fusion(bf16[128,4,2560]{2,1,0:T(4,128)(2,1)} %param.21, f32[2560]{0:T(1024)S(1)} %convert_element_type.51, f32[128,4]{1,0:T(8,128)S(1)} %add_rsqrt_fusion), kind=kLoop, calls=%fused_computation.17 | loop fusion | flops 5242880 | bytes 5255168 | tf_op jit(solution)/shard_map/convert_element_type | solution.py:23
  123.1 5.3 %reshape.333 = bf16[512,2560]{1,0:T(8,128)(2,1)} reshape(bf16[128,4,2560]{2,1,0:T(4,128)(2,1)} %fusion.2) | data formatting | bytes 5242880 | tf_op jit(solution)/shard_map/reshape | solution.py:350
  128.5 2.7 convolution_convert_fusion.2
  132.8 2.7 fusion.7
  137.1 23.3 %shard_map.199 = (f32[4,512,80]{2,1,0:T(8,128)}, f32[4,512,128]{2,1,0:T(8,128)}, f32[4,512,128]{2,1,0:T(8,128)}) custom-call(s32[4,32]{1,0:T(4,128)} %pad_add_fusion.1.tbl, s32[4,4]{1,0:T(4,128)} %pad_add_fusion.meta, bf16[4,512,80]{2,1,0:T(8,128)(2,1)} %bitcast.87, bf16[4,2,80,128]{3,2,1,0:T(8,128)(2,1)} %pad_maximum_fusion.fresh_ref, ...), custom_call_target="tpu_custom_call" | custom-call | flops 2684354560 | bytes 5242880 | tf_op jit(solution)/shard_map/pallas_call | solution.py:270
  160.4 27.8 %all-to-all-done = bf16[16,8,1,2,80,128]{5,4,3,1,2,0:T(8,128)(2,1)} async-done(((bf16[16,8,1,2,80,128]{5,4,3,1,2,0:T(8,128)(2,1)}), bf16[16,8,1,2,80,128]{5,4,3,1,2,0:T(8,128)(2,1)}, u32[]{:S(2)}, u32[]{:S(2)}) %all-to-all-start) | async-done | bytes 5242912 | tf_op jit(solution)/shard_map/all_to_all | solution.py:382
  188.3 10.2 %shard_map.200 = bf16[4,512,80]{2,1,0:T(8,128)(2,1)} custom-call(s32[4,8]{1,0:T(4,128)} %iota_add_fusion.tbl, s32[4,4]{1,0:T(4,128)} %pad_add_fusion.meta, bf16[4,512,80]{2,1,0:T(8,128)(2,1)} %bitcast.88, f32[4,512,80]{2,1,0:T(8,128)} %get-tuple-element.13.acc_in, f32[4,512,128]{2,1,0:T(8,128)} %get-tuple-element.14.top_in, ...), custom_call_target="tpu_custom_call" | custom-call | flops 671088640 | bytes 1310720 | tf_op jit(solution)/shard_map/pallas_call | solution.py:270
  198.4 1.4 copy.110
  200.2 3.0 convolution_convert_fusion.1
  204.0 34.3 %reduce-scatter.3.cloned.1.call-done = bf16[64,2560]{1,0:T(8,128)(2,1)} async-done(((bf16[512,2560]{1,0:T(8,128)(2,1)}), bf16[64,2560]{1,0:T(8,128)(2,1)}) %reduce-scatter.3.cloned.1.call-update) | async-done | bytes 327696 | tf_op jit(solution)/shard_map/reduce_scatter | solution.py:407
  238.2 1.2 reshape.347
  239.4 1.3 multiply_reduce_fusion
  240.7 1.2 multiply_convert_fusion.1
  241.9 0.8 reshape.343
  242.8 25.1 %all-gather.5.cloned.1.call-done = bf16[512,2560]{1,0:T(8,128)(2,1)} async-done(((bf16[64,2560]{1,0:T(8,128)(2,1)}), bf16[512,2560]{1,0:T(8,128)(2,1)}) %all-gather.5.cloned.1.call-update) | async-done | bytes 2621456 | tf_op jit(solution)/shard_map/all_gather | solution.py:419
  267.9 6.8 %fusion.28 = f32[512,864]{0,1:T(8,128)} fusion(bf16[512,2560]{1,0:T(8,128)(2,1)} %all-gather.5.cloned.1.call-done, bf16[2560,864]{0,1:T(8,128)(2,1)} %param.28), kind=kOutput, calls=%fused_computation.98 | convolution fusion | flops 2264924160 | bytes 8814592 | tf_op jit(solution)/shard_map/dot_general | solution.py:420
  274.7 11.7 %convolution_convert_fusion = bf16[512,2560]{1,0:T(8,128)(2,1)} fusion(bf16[864,2560]{1,0:T(8,128)(2,1)} %param.30, f32[512,864]{0,1:T(8,128)} %fusion.28, bf16[512,2560]{1,0:T(8,128)(2,1)} %all-gather.5.cloned.1.call-done, bf16[2560,864]{0,1:T(8,128)(2,1)} %param.29), kind=kOutput, calls=%fused_computation.19 | convolution fusion | flops 4533813248 | bytes 15859712 | tf_op jit(solution)/shard_map/dot_general | solution.py:425
  286.4 35.3 %reduce-scatter.5.cloned.1.call-done = bf16[64,2560]{1,0:T(8,128)(2,1)} async-done(((bf16[512,2560]{1,0:T(8,128)(2,1)}), bf16[64,2560]{1,0:T(8,128)(2,1)}) %reduce-scatter.5.cloned.1.call-update) | async-done | bytes 327696 | tf_op jit(solution)/shard_map/reduce_scatter | solution.py:424
  321.7 1.2 reshape.349
  322.9 2.0 fusion.21
  (97 shorter events, 14.1 us)
Async XLA Ops:
  6.5 193.7 %copy-start = (bf16[320,2560]{1,0:T(8,128)(2,1)S(1)}, bf16[320,2560]{1,0:T(8,128)(2,1)}, u32[]{:S(2)}) copy-start(bf16[320,2560]{1,0:T(8,128)(2,1)} %param.26) | copy-start | bytes 4915204
  6.5 6.2 %copy-start.1 = (s32[16]{0:T(128)S(1)}, s32[16]{0:T(128)}, u32[]{:S(2)}) copy-start(s32[16]{0:T(128)} %param.39) | copy-start | bytes 196
  6.5 6.8 %copy-start.2 = (s32[16]{0:T(128)S(1)}, s32[16]{0:T(128)}, u32[]{:S(2)}) copy-start(s32[16]{0:T(128)} %param.37) | copy-start | bytes 196
  6.5 7.6 %copy-start.10 = (s32[64,8]{0,1:T(8,128)S(1)}, s32[64,8]{0,1:T(8,128)}, u32[]{:S(2)}) copy-start(s32[64,8]{0,1:T(8,128)} %param.35) | copy-start | bytes 6148
  6.5 98.2 %all-gather.3.cloned.1.call-start = ((), (), s32[]{:S(2)}) async-start(), calls=%async_computation.3 | async-start | bytes 13926400 | tf_op jit(solution)/shard_map/all_gather | solution.py:347
  14.2 3.3 copy-start.3
  14.2 4.0 %copy-start.4 = (bf16[32,1,2,80,128]{4,3,2,1,0:T(8,128)(2,1)S(1)}, bf16[32,1,2,80,128]{4,3,2,1,0:T(8,128)(2,1)}, u32[]{:S(2)}) copy-start(bf16[32,1,2,80,128]{4,3,2,1,0:T(8,128)(2,1)} %param.32) | copy-start | bytes 3932164
  30.7 80.6 %copy-start.8 = (bf16[2560]{0:T(1024)(128)(2,1)S(1)}, bf16[2560]{0:T(1024)(128)(2,1)}, u32[]{:S(2)}) copy-start(bf16[2560]{0:T(1024)(128)(2,1)} %param.22) | copy-start | bytes 15364
  104.7 83.5 %all-to-all-start = ((bf16[16,8,1,2,80,128]{5,4,3,1,2,0:T(8,128)(2,1)}), bf16[16,8,1,2,80,128]{5,4,3,1,2,0:T(8,128)(2,1)}, u32[]{:S(2)}, u32[]{:S(2)}) async-start(bf16[16,8,1,2,80,128]{5,4,3,1,2,0:T(8,128)(2,1)} %select_select_fusion), calls=%async_computation | async-start | bytes 10485760 | tf_op jit(solution)/shard_map/all_to_all | solution.py:382
  110.1 128.2 %reduce-scatter.3.cloned.1.call-start = ((), (), s32[]{:S(2)}) async-start(), calls=%async_computation.4 | async-start | bytes 2949120 | tf_op jit(solution)/shard_map/reduce_scatter | solution.py:407
  111.6 3.3 %copy-start.11 = (bf16[2560,320]{0,1:T(8,128)(2,1)S(1)}, bf16[2560,320]{0,1:T(8,128)(2,1)}, u32[]{:S(2)}) copy-start(bf16[2560,320]{0,1:T(8,128)(2,1)} %param.23) | copy-start | bytes 4915204
  116.0 1.2 copy-start.7
  116.1 1.7 copy-start.6
  123.1 5.4 %copy-start.5 = (bf16[2560,80]{0,1:T(8,128)(2,1)S(1)}, bf16[2560,80]{0,1:T(8,128)(2,1)}, u32[]{:S(2)}) copy-start(bf16[2560,80]{0,1:T(8,128)(2,1)} %param.25) | copy-start | bytes 1228804
  128.5 4.3 %copy-start.12 = (bf16[2560,80]{0,1:T(8,128)(2,1)S(1)}, bf16[2560,80]{0,1:T(8,128)(2,1)}, u32[]{:S(2)}) copy-start(bf16[2560,80]{0,1:T(8,128)(2,1)} %param.24) | copy-start | bytes 1228804
  203.3 0.7 copy-start.9
  203.3 64.6 %all-gather.5.cloned.1.call-start = ((), (), s32[]{:S(2)}) async-start(), calls=%async_computation.5 | async-start | bytes 2949120 | tf_op jit(solution)/shard_map/all_gather | solution.py:419
  242.8 79.0 %reduce-scatter.5.cloned.1.call-start = ((), (), s32[]{:S(2)}) async-start(), calls=%async_computation.6 | async-start | bytes 2949120 | tf_op jit(solution)/shard_map/reduce_scatter | solution.py:424
Sparse Core Ops, SparseCore 0:
  9.5 95.1 all-gather.2
  203.4 34.7 reduce-scatter.2
  242.9 24.9 all-gather.4
  286.5 35.1 reduce-scatter.4

commit v13 on v8

--- a/solution.py
+++ b/solution.py
@@ -76,7 +76,7 @@
 ROOT_PAGES = 16
 MID_PAGES = 16
 LEAF_SLOTS = 8
-CHUNK_PAGES = 4
+CHUNK_PAGES = 8
 
 
 def part_body(chunk0, with_fresh, tbl, meta, q_ref, store_hbm, kv, sc, top, mass, acc, sem, begin, finish):

time: 316 us -> 317 us (level)
  waiting for transfers between devices: 180 us -> 184 us
    reduce_scatter x1, waiting for transfers between devices: 35.2 us -> 39 us  [shards(): lax.psum_scatter(jnp.dot(attended, w_out, preferred_element_type=jnp.floa...]
where the time goes in v13:
time: 317 us
  waiting for transfers between devices  184 us (58%)
  Pallas kernels  32.1 us (10%)
  matrix products  28 us (9%)
  local copies, waits for them, and re-layouts  26.3 us (8%)
  other arithmetic  25 us (8%)
  between operations  13.5 us (4%)
  starting transfers between devices  8.67 us (3%)
    all_to_all x1, waiting for transfers between devices, shards(): lax.all_to_all(outgoing, 'seq', split_axis=0, concat_axis=0, tiled=True)  64.3 us
    reduce_scatter x1, waiting for transfers between devices, shards(): lax.psum_scatter(jnp.dot(attended, w_out, preferred_element_type=jnp.floa...  39 us
    reduce_scatter x1, waiting for transfers between devices, shards(): lax.psum_scatter(jnp.dot(activated, w_down, preferred_element_type=jnp.fl...  35.3 us
    pallas_call x2, Pallas kernels, part_call(): pl.pallas_call(kernel, grid_spec=grid_spec, out_shape=out_shapes, compile...  32.1 us
    all_gather x1, waiting for transfers between devices, shards(): normed_ffn = lax.all_gather(normed_own, 'tp', axis=0, tiled=True)  24.8 us
    all_gather x1, waiting for transfers between devices, shards(): page_store = lax.all_gather(shared_pages, 'seq', axis=0, tiled=True)  19.4 us
    dot_general x1, matrix products, shards(): jnp.dot(activated, w_down, preferred_element_type=jnp.float32)  11.7 us
    all_to_all x1, starting transfers between devices, shards(): lax.all_to_all(outgoing, 'seq', split_axis=0, concat_axis=0, tiled=True)  8.32 us
  transfers between devices with their start and end apart: 5, of which 5 were waited for; matrix products, arithmetic and copies ran while one was open for 15% of the time, Pallas kernels for 3%

profile of v13, /device:TPU:0, one launch (start us, length us, event | category | flops | bytes accessed | tf_op | source)
XLA Modules:
  0.0 317.0 jit_solution(16389279813815532637)
XLA Ops:
  7.3 0.7 reshape.334
  8.0 0.7 reshape.335
  8.8 0.8 copy.95
  10.3 0.8 gather_fusion.9
  13.6 3.5 %gather_fusion.11 = bf16[128,2,80,128]{3,2,1,0:T(8,128)(2,1)} fusion(bf16[32,2,80,128]{3,2,1,0:T(8,128)(2,1)S(1)} %bitcast.85, s32[1024]{0:T(1024)S(1)} %pad_clamp_fusion), kind=kCustom, calls=%fused_computation.11 | custom fusion | bytes 10486272 | tf_op jit(solution)/shard_map/jit(_take)/gather | solution.py:376
  17.1 5.5 %select_select_fusion = bf16[16,8,1,2,80,128]{5,4,3,1,2,0:T(8,128)(2,1)} fusion(bf16[16,8,1,2,80,128]{5,4,3,1,2,0:T(8,128)(2,1)} %bitcast.84, pred[16]{0:T(512)(128)(4,1)S(1)} %reduce_or.9, pred[16,8]{1,0:T(8,128)(4,1)S(1)} %get-tuple-element.13), kind=kLoop, calls=%fused_computation.18 | loop fusion | flops 5242880 | bytes 10485904 | tf_op jit(solution)/shard_map/jit(_where)/select_n | solution.py:375
  22.6 8.3 %all-to-all-start = ((bf16[16,8,1,2,80,128]{5,4,3,1,2,0:T(8,128)(2,1)}), bf16[16,8,1,2,80,128]{5,4,3,1,2,0:T(8,128)(2,1)}, u32[]{:S(2)}, u32[]{:S(2)}) async-start(bf16[16,8,1,2,80,128]{5,4,3,1,2,0:T(8,128)(2,1)} %select_select_fusion), calls=%async_computation | async-start | bytes 10485760 | tf_op jit(solution)/shard_map/all_to_all | solution.py:378
  35.7 3.3 %fusion = f32[128,4]{1,0:T(8,128)S(1)} fusion(bf16[128,4,2560]{2,1,0:T(4,128)(2,1)} %param.21), kind=kLoop, calls=%fused_computation.15 | loop fusion | flops 3931648 | bytes 2623488 | tf_op jit(solution)/shard_map/reduce_sum | solution.py:20
  39.5 1.5 fusion.39
  41.0 1.1 fusion.3
  42.2 1.0 copy.91
  43.2 4.8 %fusion.2 = bf16[128,4,2560]{2,1,0:T(4,128)(2,1)} fusion(bf16[128,4,2560]{2,1,0:T(4,128)(2,1)} %param.21, f32[2560]{0:T(1024)S(1)} %convert_element_type.51, f32[128,4]{1,0:T(8,128)S(1)} %add_rsqrt_fusion), kind=kLoop, calls=%fused_computation.17 | loop fusion | flops 5242880 | bytes 5255168 | tf_op jit(solution)/shard_map/convert_element_type | solution.py:21
  48.0 5.4 %reshape.333 = bf16[512,2560]{1,0:T(8,128)(2,1)} reshape(bf16[128,4,2560]{2,1,0:T(4,128)(2,1)} %fusion.2) | data formatting | bytes 5242880 | tf_op jit(solution)/shard_map/reshape | solution.py:347
  53.4 2.7 convolution_convert_fusion.2
  59.1 2.7 fusion.7
  63.5 64.3 %all-to-all-done = bf16[16,8,1,2,80,128]{5,4,3,1,2,0:T(8,128)(2,1)} async-done(((bf16[16,8,1,2,80,128]{5,4,3,1,2,0:T(8,128)(2,1)}), bf16[16,8,1,2,80,128]{5,4,3,1,2,0:T(8,128)(2,1)}, u32[]{:S(2)}, u32[]{:S(2)}) %all-to-all-start) | async-done | bytes 5242912 | tf_op jit(solution)/shard_map/all_to_all | solution.py:378
  127.9 10.9 %shard_map.199 = (f32[4,512,80]{2,1,0:T(8,128)}, f32[4,512,128]{2,1,0:T(8,128)}, f32[4,512,128]{2,1,0:T(8,128)}) custom-call(s32[4,8]{1,0:T(4,128)} %iota_add_fusion.tbl, s32[4,4]{1,0:T(4,128)} %pad_add_fusion.1.meta, bf16[4,512,80]{2,1,0:T(8,128)(2,1)} %bitcast.87, bf16[4,2,80,128]{3,2,1,0:T(8,128)(2,1)} %pad_maximum_fusion.fresh_ref, ...), custom_call_target="tpu_custom_call" | custom-call | flops 671088640 | bytes 1310720 | tf_op jit(solution)/shard_map/pallas_call | solution.py:268
  138.8 19.4 %all-gather.3.cloned.1.call-done = bf16[320,1,2,80,128]{4,3,2,1,0:T(8,128)(2,1)} async-done(((bf16[20,1,2,80,128]{4,3,2,1,0:T(8,128)(2,1)}), bf16[320,1,2,80,128]{4,3,2,1,0:T(8,128)(2,1)}) %all-gather.3.cloned.1.call-update) | async-done | bytes 13107216 | tf_op jit(solution)/shard_map/all_gather | solution.py:344
  158.2 21.2 %shard_map.200 = bf16[4,512,80]{2,1,0:T(8,128)(2,1)} custom-call(s32[4,32]{1,0:T(4,128)} %pad_add_fusion.tbl, s32[4,4]{1,0:T(4,128)} %pad_add_fusion.1.meta, bf16[4,512,80]{2,1,0:T(8,128)(2,1)} %bitcast.88, f32[4,512,80]{2,1,0:T(8,128)} %get-tuple-element.10.acc_in, f32[4,512,128]{2,1,0:T(8,128)} %get-tuple-element.11.top_in, ...), custom_call_target="tpu_custom_call" | custom-call | flops 2684354560 | bytes 5242880 | tf_op jit(solution)/shard_map/pallas_call | solution.py:268
  179.4 1.4 copy.110
  181.2 3.0 convolution_convert_fusion.1
  184.9 39.0 %reduce-scatter.3.cloned.1.call-done = bf16[64,2560]{1,0:T(8,128)(2,1)} async-done(((bf16[512,2560]{1,0:T(8,128)(2,1)}), bf16[64,2560]{1,0:T(8,128)(2,1)}) %reduce-scatter.3.cloned.1.call-update) | async-done | bytes 327696 | tf_op jit(solution)/shard_map/reduce_scatter | solution.py:403
  223.9 1.2 reshape.347
  225.1 1.3 multiply_reduce_fusion
  226.3 1.2 multiply_convert_fusion.1
  227.6 0.8 reshape.343
  228.7 24.8 %all-gather.5.cloned.1.call-done = bf16[512,2560]{1,0:T(8,128)(2,1)} async-done(((bf16[64,2560]{1,0:T(8,128)(2,1)}), bf16[512,2560]{1,0:T(8,128)(2,1)}) %all-gather.5.cloned.1.call-update) | async-done | bytes 2621456 | tf_op jit(solution)/shard_map/all_gather | solution.py:415
  253.5 6.8 %fusion.28 = f32[512,864]{0,1:T(8,128)} fusion(bf16[512,2560]{1,0:T(8,128)(2,1)} %all-gather.5.cloned.1.call-done, bf16[2560,864]{0,1:T(8,128)(2,1)} %param.28), kind=kOutput, calls=%fused_computation.98 | convolution fusion | flops 2264924160 | bytes 8814592 | tf_op jit(solution)/shard_map/dot_general | solution.py:416
  260.2 11.7 %convolution_convert_fusion = bf16[512,2560]{1,0:T(8,128)(2,1)} fusion(bf16[864,2560]{1,0:T(8,128)(2,1)} %param.30, f32[512,864]{0,1:T(8,128)} %fusion.28, bf16[512,2560]{1,0:T(8,128)(2,1)} %all-gather.5.cloned.1.call-done, bf16[2560,864]{0,1:T(8,128)(2,1)} %param.29), kind=kOutput, calls=%fused_computation.19 | convolution fusion | flops 4533813248 | bytes 15859712 | tf_op jit(solution)/shard_map/dot_general | solution.py:421
  272.0 35.3 %reduce-scatter.5.cloned.1.call-done = bf16[64,2560]{1,0:T(8,128)(2,1)} async-done(((bf16[512,2560]{1,0:T(8,128)(2,1)}), bf16[64,2560]{1,0:T(8,128)(2,1)}) %reduce-scatter.5.cloned.1.call-update) | async-done | bytes 327696 | tf_op jit(solution)/shard_map/reduce_scatter | solution.py:420
  307.3 1.2 reshape.349
  308.5 2.0 fusion.21
  (103 shorter events, 15.2 us)
Async XLA Ops:
  6.5 174.6 %copy-start = (bf16[320,2560]{1,0:T(8,128)(2,1)S(1)}, bf16[320,2560]{1,0:T(8,128)(2,1)}, u32[]{:S(2)}) copy-start(bf16[320,2560]{1,0:T(8,128)(2,1)} %param.26) | copy-start | bytes 4915204
  6.5 151.6 %all-gather.3.cloned.1.call-start = ((), (), s32[]{:S(2)}) async-start(), calls=%async_computation.3 | async-start | bytes 13926400 | tf_op jit(solution)/shard_map/all_gather | solution.py:344
  10.3 3.3 %copy-start.8 = (bf16[32,1,2,80,128]{4,3,2,1,0:T(8,128)(2,1)S(1)}, bf16[32,1,2,80,128]{4,3,2,1,0:T(8,128)(2,1)}, u32[]{:S(2)}) copy-start(bf16[32,1,2,80,128]{4,3,2,1,0:T(8,128)(2,1)} %param.32) | copy-start | bytes 3932164
  22.6 8.5 %copy-start.1 = (s32[64]{0:T(128)S(1)}, s32[64]{0:T(128)}, u32[]{:S(2)}) copy-start(s32[64]{0:T(128)} %param.41) | copy-start | bytes 772
  22.6 9.8 %copy-start.2 = (s32[64]{0:T(128)S(1)}, s32[64]{0:T(128)}, u32[]{:S(2)}) copy-start(s32[64]{0:T(128)} %param.40) | copy-start | bytes 772
  22.6 10.4 %copy-start.3 = (s32[16]{0:T(128)S(1)}, s32[16]{0:T(128)}, u32[]{:S(2)}) copy-start(s32[16]{0:T(128)} %param.39) | copy-start | bytes 196
  22.6 11.1 %copy-start.4 = (s32[16]{0:T(128)S(1)}, s32[16]{0:T(128)}, u32[]{:S(2)}) copy-start(s32[16]{0:T(128)} %param.37) | copy-start | bytes 196
  22.6 105.3 %all-to-all-start = ((bf16[16,8,1,2,80,128]{5,4,3,1,2,0:T(8,128)(2,1)}), bf16[16,8,1,2,80,128]{5,4,3,1,2,0:T(8,128)(2,1)}, u32[]{:S(2)}, u32[]{:S(2)}) async-start(bf16[16,8,1,2,80,128]{5,4,3,1,2,0:T(8,128)(2,1)} %select_select_fusion), calls=%async_computation | async-start | bytes 10485760 | tf_op jit(solution)/shard_map/all_to_all | solution.py:378
  30.9 3.4 %copy-start.5 = (s32[64]{0:T(128)S(1)}, s32[64]{0:T(128)}, u32[]{:S(2)}) copy-start(s32[64]{0:T(128)} %param.38) | copy-start | bytes 772
  30.9 4.0 %copy-start.12 = (bf16[2560]{0:T(1024)(128)(2,1)S(1)}, bf16[2560]{0:T(1024)(128)(2,1)}, u32[]{:S(2)}) copy-start(bf16[2560]{0:T(1024)(128)(2,1)} %param.22) | copy-start | bytes 15364
  31.0 4.0 %copy-start.6 = (s32[4]{0:T(128)S(1)}, s32[4]{0:T(128)}, u32[]{:S(2)}) copy-start(s32[4]{0:T(128)} %param.36) | copy-start | bytes 52
  31.0 192.9 %reduce-scatter.3.cloned.1.call-start = ((), (), s32[]{:S(2)}) async-start(), calls=%async_computation.4 | async-start | bytes 2949120 | tf_op jit(solution)/shard_map/reduce_scatter | solution.py:403
  35.6 3.8 %copy-start.7 = (bf16[128,4,2560]{2,1,0:T(4,128)(2,1)S(1)}, bf16[128,4,2560]{2,1,0:T(4,128)(2,1)}, u32[]{:S(2)}) copy-start(bf16[128,4,2560]{2,1,0:T(4,128)(2,1)} %param.21) | copy-start | bytes 7864324
  39.5 1.5 copy-start.14
  48.0 5.4 %copy-start.9 = (bf16[2560,80]{0,1:T(8,128)(2,1)S(1)}, bf16[2560,80]{0,1:T(8,128)(2,1)}, u32[]{:S(2)}) copy-start(bf16[2560,80]{0,1:T(8,128)(2,1)} %param.25) | copy-start | bytes 1228804
  53.4 3.3 %copy-start.10 = (s32[4,16]{1,0:T(4,128)S(1)}, s32[4,16]{1,0:T(4,128)}, u32[]{:S(2)}) copy-start(s32[4,16]{1,0:T(4,128)} %param.33) | copy-start | bytes 772
  53.4 3.8 %copy-start.11 = (s32[16,16]{1,0:T(8,128)S(1)}, s32[16,16]{1,0:T(8,128)}, u32[]{:S(2)}) copy-start(s32[16,16]{1,0:T(8,128)} %param.34) | copy-start | bytes 3076
  53.4 5.7 %copy-start.15 = (bf16[2560,80]{0,1:T(8,128)(2,1)S(1)}, bf16[2560,80]{0,1:T(8,128)(2,1)}, u32[]{:S(2)}) copy-start(bf16[2560,80]{0,1:T(8,128)(2,1)} %param.24) | copy-start | bytes 1228804
  184.2 0.7 copy-start.13
  184.2 69.2 %all-gather.5.cloned.1.call-start = ((), (), s32[]{:S(2)}) async-start(), calls=%async_computation.5 | async-start | bytes 2949120 | tf_op jit(solution)/shard_map/all_gather | solution.py:415
  228.4 78.9 %reduce-scatter.5.cloned.1.call-start = ((), (), s32[]{:S(2)}) async-start(), calls=%async_computation.6 | async-start | bytes 2949120 | tf_op jit(solution)/shard_map/reduce_scatter | solution.py:420
Sparse Core Ops, SparseCore 0:
  9.5 148.6 all-gather.2
  184.4 39.4 reduce-scatter.2
  228.5 24.9 all-gather.4
  272.1 35.1 reduce-scatter.4

commit v14 on v13

--- a/solution.py
+++ b/solution.py
@@ -79,14 +79,13 @@
 CHUNK_PAGES = 8
 
 
-def part_body(chunk0, with_fresh, tbl, meta, q_ref, store_hbm, kv, sc, top, mass, acc, sem, begin, finish):
+def part_body(chunk0, group, tbl, meta, q_ref, store_hbm, kv, sc, top, mass, acc, sem, begin, finish):
     b = pl.program_id(0)
     requests = pl.num_programs(0)
     slot = b % 2
     shared_count = ROOT_PAGES + MID_PAGES
     page_count = kv.shape[1]
     width = kv.shape[-1]
-    group = CHUNK_PAGES
     span = group * width
 
     def start_request(j, into):
@@ -214,8 +213,8 @@
         )
 
     part_body(
-        (ROOT_PAGES + MID_PAGES) // CHUNK_PAGES, True, tbl, meta, q_ref, store_hbm, kv, sc, top, mass, acc, sem,
-        begin, finish,
+        (ROOT_PAGES + MID_PAGES) // LEAF_SLOTS, LEAF_SLOTS, tbl, meta, q_ref, store_hbm, kv, sc, top, mass, acc,
+        sem, begin, finish,
     )
     acc_out[0] = acc[...]
     top_out[0] = top[...]
@@ -231,12 +230,12 @@
         mass[...] = mass_in[0] * factor
         acc[...] = acc_in[0] * factor[:, :1]
 
-    part_body(0, False, tbl, meta, q_ref, store_hbm, kv, sc, top, mass, acc, sem, begin, finish)
+    part_body(0, ROOT_PAGES, tbl, meta, q_ref, store_hbm, kv, sc, top, mass, acc, sem, begin, finish)
     totals = jnp.sum(mass[...], -1, keepdims=True)
     out_ref[0] = (acc[...] / totals).astype(out_ref.dtype)
 
 
-def part_call(kernel, tbl, meta, inputs, in_blocks, store, out_shapes):
+def part_call(kernel, tbl, meta, inputs, chunk, store, out_shapes):
     reqs, rows, head = inputs[0].shape
     page_shape = store.shape[1:]
     width = page_shape[-1]
@@ -247,7 +246,7 @@
 
     scratch = [
         pltpu.VMEM((2, pages) + page_shape, store.dtype),
-        pltpu.VMEM((pages // CHUNK_PAGES, rows, CHUNK_PAGES * width), jnp.float32),
+        pltpu.VMEM((pages // chunk, rows, chunk * width), jnp.float32),
     ]
     if kernel is leaf_kernel:
         scratch.append(pltpu.VMEM((rows, width), jnp.float32))
@@ -283,7 +282,7 @@
     width = shared_store.shape[-1]
     shared_count = ROOT_PAGES + MID_PAGES
     state = part_call(
-        leaf_kernel, tbl[:, shared_count:], meta, [queries, fresh], None, leaf_store,
+        leaf_kernel, tbl[:, shared_count:], meta, [queries, fresh], LEAF_SLOTS, leaf_store,
         [
             jax.ShapeDtypeStruct((reqs, rows, head), jnp.float32),
             jax.ShapeDtypeStruct((reqs, rows, width), jnp.float32),
@@ -291,7 +290,7 @@
         ],
     )
     (out,) = part_call(
-        shared_kernel, tbl[:, :shared_count], meta, [queries] + list(state), None, shared_store,
+        shared_kernel, tbl[:, :shared_count], meta, [queries] + list(state), ROOT_PAGES, shared_store,
         [jax.ShapeDtypeStruct((reqs, rows, head), jnp.bfloat16)],
     )
     return out

time: 317 us -> 318 us (level)
  no operation moved by 1% of the time
where the time goes in v14:
time: 318 us; the launch traced here: 317 us
  waiting for transfers between devices  181 us (57%)
  Pallas kernels  34.8 us (11%)
  matrix products  28 us (9%)
  local copies, waits for them, and re-layouts  26.3 us (8%)
  other arithmetic  25 us (8%)
  between operations  13.5 us (4%)
  starting transfers between devices  8.67 us (3%)
    all_to_all x1, waiting for transfers between devices, shards(): lax.all_to_all(outgoing, 'seq', split_axis=0, concat_axis=0, tiled=True)  64.4 us
    reduce_scatter x1, waiting for transfers between devices, shards(): lax.psum_scatter(jnp.dot(attended, w_out, preferred_element_type=jnp.floa...  36.1 us
    reduce_scatter x1, waiting for transfers between devices, shards(): lax.psum_scatter(jnp.dot(activated, w_down, preferred_element_type=jnp.fl...  35.3 us
    pallas_call x2, Pallas kernels, part_call(): pl.pallas_call(kernel, grid_spec=grid_spec, out_shape=out_shapes, compile...  34.8 us
    all_gather x1, waiting for transfers between devices, shards(): normed_ffn = lax.all_gather(normed_own, 'tp', axis=0, tiled=True)  24.7 us
    all_gather x1, waiting for transfers between devices, shards(): page_store = lax.all_gather(shared_pages, 'seq', axis=0, tiled=True)  19.4 us
    dot_general x1, matrix products, shards(): jnp.dot(activated, w_down, preferred_element_type=jnp.float32)  11.7 us
    all_to_all x1, starting transfers between devices, shards(): lax.all_to_all(outgoing, 'seq', split_axis=0, concat_axis=0, tiled=True)  8.32 us
  transfers between devices with their start and end apart: 5, of which 5 were waited for; matrix products, arithmetic and copies ran while one was open for 15% of the time, Pallas kernels for 3%

profile of v14, /device:TPU:0, one launch (start us, length us, event | category | flops | bytes accessed | tf_op | source)
XLA Modules:
  0.0 316.8 jit_solution(1040826075836237684)
XLA Ops:
  7.3 0.7 reshape.334
  8.0 0.7 reshape.335
  8.8 0.8 copy.95
  10.3 0.8 gather_fusion.9
  13.6 3.5 %gather_fusion.11 = bf16[128,2,80,128]{3,2,1,0:T(8,128)(2,1)} fusion(bf16[32,2,80,128]{3,2,1,0:T(8,128)(2,1)S(1)} %bitcast.85, s32[1024]{0:T(1024)S(1)} %pad_clamp_fusion), kind=kCustom, calls=%fused_computation.11 | custom fusion | bytes 10486272 | tf_op jit(solution)/shard_map/jit(_take)/gather | solution.py:375
  17.1 5.5 %select_select_fusion = bf16[16,8,1,2,80,128]{5,4,3,1,2,0:T(8,128)(2,1)} fusion(bf16[16,8,1,2,80,128]{5,4,3,1,2,0:T(8,128)(2,1)} %bitcast.84, pred[16]{0:T(512)(128)(4,1)S(1)} %reduce_or.9, pred[16,8]{1,0:T(8,128)(4,1)S(1)} %get-tuple-element.13), kind=kLoop, calls=%fused_computation.18 | loop fusion | flops 5242880 | bytes 10485904 | tf_op jit(solution)/shard_map/jit(_where)/select_n | solution.py:374
  22.6 8.3 %all-to-all-start = ((bf16[16,8,1,2,80,128]{5,4,3,1,2,0:T(8,128)(2,1)}), bf16[16,8,1,2,80,128]{5,4,3,1,2,0:T(8,128)(2,1)}, u32[]{:S(2)}, u32[]{:S(2)}) async-start(bf16[16,8,1,2,80,128]{5,4,3,1,2,0:T(8,128)(2,1)} %select_select_fusion), calls=%async_computation | async-start | bytes 10485760 | tf_op jit(solution)/shard_map/all_to_all | solution.py:377
  35.7 3.3 %fusion = f32[128,4]{1,0:T(8,128)S(1)} fusion(bf16[128,4,2560]{2,1,0:T(4,128)(2,1)} %param.21), kind=kLoop, calls=%fused_computation.15 | loop fusion | flops 3931648 | bytes 2623488 | tf_op jit(solution)/shard_map/reduce_sum | solution.py:20
  39.5 1.5 fusion.39
  41.0 1.1 fusion.3
  42.2 1.0 copy.91
  43.2 4.8 %fusion.2 = bf16[128,4,2560]{2,1,0:T(4,128)(2,1)} fusion(bf16[128,4,2560]{2,1,0:T(4,128)(2,1)} %param.21, f32[2560]{0:T(1024)S(1)} %convert_element_type.51, f32[128,4]{1,0:T(8,128)S(1)} %add_rsqrt_fusion), kind=kLoop, calls=%fused_computation.17 | loop fusion | flops 5242880 | bytes 5255168 | tf_op jit(solution)/shard_map/convert_element_type | solution.py:21
  48.0 5.4 %reshape.333 = bf16[512,2560]{1,0:T(8,128)(2,1)} reshape(bf16[128,4,2560]{2,1,0:T(4,128)(2,1)} %fusion.2) | data formatting | bytes 5242880 | tf_op jit(solution)/shard_map/reshape | solution.py:346
  53.4 2.7 convolution_convert_fusion.2
  59.1 2.7 fusion.7
  63.5 64.4 %all-to-all-done = bf16[16,8,1,2,80,128]{5,4,3,1,2,0:T(8,128)(2,1)} async-done(((bf16[16,8,1,2,80,128]{5,4,3,1,2,0:T(8,128)(2,1)}), bf16[16,8,1,2,80,128]{5,4,3,1,2,0:T(8,128)(2,1)}, u32[]{:S(2)}, u32[]{:S(2)}) %all-to-all-start) | async-done | bytes 5242912 | tf_op jit(solution)/shard_map/all_to_all | solution.py:377
  127.9 10.9 %shard_map.199 = (f32[4,512,80]{2,1,0:T(8,128)}, f32[4,512,128]{2,1,0:T(8,128)}, f32[4,512,128]{2,1,0:T(8,128)}) custom-call(s32[4,8]{1,0:T(4,128)} %iota_add_fusion.tbl, s32[4,4]{1,0:T(4,128)} %pad_add_fusion.1.meta, bf16[4,512,80]{2,1,0:T(8,128)(2,1)} %bitcast.87, bf16[4,2,80,128]{3,2,1,0:T(8,128)(2,1)} %pad_maximum_fusion.fresh_ref, ...), custom_call_target="tpu_custom_call" | custom-call | flops 671088640 | bytes 1310720 | tf_op jit(solution)/shard_map/pallas_call | solution.py:267
  138.8 19.4 %all-gather.3.cloned.1.call-done = bf16[320,1,2,80,128]{4,3,2,1,0:T(8,128)(2,1)} async-done(((bf16[20,1,2,80,128]{4,3,2,1,0:T(8,128)(2,1)}), bf16[320,1,2,80,128]{4,3,2,1,0:T(8,128)(2,1)}) %all-gather.3.cloned.1.call-update) | async-done | bytes 13107216 | tf_op jit(solution)/shard_map/all_gather | solution.py:343
  158.2 23.9 %shard_map.200 = bf16[4,512,80]{2,1,0:T(8,128)(2,1)} custom-call(s32[4,32]{1,0:T(4,128)} %pad_add_fusion.tbl, s32[4,4]{1,0:T(4,128)} %pad_add_fusion.1.meta, bf16[4,512,80]{2,1,0:T(8,128)(2,1)} %bitcast.88, f32[4,512,80]{2,1,0:T(8,128)} %get-tuple-element.10.acc_in, f32[4,512,128]{2,1,0:T(8,128)} %get-tuple-element.11.top_in, ...), custom_call_target="tpu_custom_call" | custom-call | flops 2684354560 | bytes 5242880 | tf_op jit(solution)/shard_map/pallas_call | solution.py:267
  182.1 1.4 copy.110
  183.9 3.0 convolution_convert_fusion.1
  187.6 36.1 %reduce-scatter.3.cloned.1.call-done = bf16[64,2560]{1,0:T(8,128)(2,1)} async-done(((bf16[512,2560]{1,0:T(8,128)(2,1)}), bf16[64,2560]{1,0:T(8,128)(2,1)}) %reduce-scatter.3.cloned.1.call-update) | async-done | bytes 327696 | tf_op jit(solution)/shard_map/reduce_scatter | solution.py:402
  223.7 1.2 reshape.347
  224.9 1.3 multiply_reduce_fusion
  226.2 1.2 multiply_convert_fusion.1
  227.4 0.8 reshape.343
  228.5 24.7 %all-gather.5.cloned.1.call-done = bf16[512,2560]{1,0:T(8,128)(2,1)} async-done(((bf16[64,2560]{1,0:T(8,128)(2,1)}), bf16[512,2560]{1,0:T(8,128)(2,1)}) %all-gather.5.cloned.1.call-update) | async-done | bytes 2621456 | tf_op jit(solution)/shard_map/all_gather | solution.py:414
  253.3 6.8 %fusion.28 = f32[512,864]{0,1:T(8,128)} fusion(bf16[512,2560]{1,0:T(8,128)(2,1)} %all-gather.5.cloned.1.call-done, bf16[2560,864]{0,1:T(8,128)(2,1)} %param.28), kind=kOutput, calls=%fused_computation.98 | convolution fusion | flops 2264924160 | bytes 8814592 | tf_op jit(solution)/shard_map/dot_general | solution.py:415
  260.0 11.7 %convolution_convert_fusion = bf16[512,2560]{1,0:T(8,128)(2,1)} fusion(bf16[864,2560]{1,0:T(8,128)(2,1)} %param.30, f32[512,864]{0,1:T(8,128)} %fusion.28, bf16[512,2560]{1,0:T(8,128)(2,1)} %all-gather.5.cloned.1.call-done, bf16[2560,864]{0,1:T(8,128)(2,1)} %param.29), kind=kOutput, calls=%fused_computation.19 | convolution fusion | flops 4533813248 | bytes 15859712 | tf_op jit(solution)/shard_map/dot_general | solution.py:420
  271.8 35.3 %reduce-scatter.5.cloned.1.call-done = bf16[64,2560]{1,0:T(8,128)(2,1)} async-done(((bf16[512,2560]{1,0:T(8,128)(2,1)}), bf16[64,2560]{1,0:T(8,128)(2,1)}) %reduce-scatter.5.cloned.1.call-update) | async-done | bytes 327696 | tf_op jit(solution)/shard_map/reduce_scatter | solution.py:419
  307.1 1.2 reshape.349
  308.3 2.0 fusion.21
  (103 shorter events, 15.2 us)
Async XLA Ops:
  6.5 177.3 %copy-start = (bf16[320,2560]{1,0:T(8,128)(2,1)S(1)}, bf16[320,2560]{1,0:T(8,128)(2,1)}, u32[]{:S(2)}) copy-start(bf16[320,2560]{1,0:T(8,128)(2,1)} %param.26) | copy-start | bytes 4915204
  6.5 151.6 %all-gather.3.cloned.1.call-start = ((), (), s32[]{:S(2)}) async-start(), calls=%async_computation.3 | async-start | bytes 13926400 | tf_op jit(solution)/shard_map/all_gather | solution.py:343
  10.3 3.3 %copy-start.8 = (bf16[32,1,2,80,128]{4,3,2,1,0:T(8,128)(2,1)S(1)}, bf16[32,1,2,80,128]{4,3,2,1,0:T(8,128)(2,1)}, u32[]{:S(2)}) copy-start(bf16[32,1,2,80,128]{4,3,2,1,0:T(8,128)(2,1)} %param.32) | copy-start | bytes 3932164
  22.6 8.5 %copy-start.1 = (s32[64]{0:T(128)S(1)}, s32[64]{0:T(128)}, u32[]{:S(2)}) copy-start(s32[64]{0:T(128)} %param.41) | copy-start | bytes 772
  22.6 9.8 %copy-start.2 = (s32[64]{0:T(128)S(1)}, s32[64]{0:T(128)}, u32[]{:S(2)}) copy-start(s32[64]{0:T(128)} %param.40) | copy-start | bytes 772
  22.6 10.4 %copy-start.3 = (s32[16]{0:T(128)S(1)}, s32[16]{0:T(128)}, u32[]{:S(2)}) copy-start(s32[16]{0:T(128)} %param.39) | copy-start | bytes 196
  22.6 11.1 %copy-start.4 = (s32[16]{0:T(128)S(1)}, s32[16]{0:T(128)}, u32[]{:S(2)}) copy-start(s32[16]{0:T(128)} %param.37) | copy-start | bytes 196
  22.6 105.3 %all-to-all-start = ((bf16[16,8,1,2,80,128]{5,4,3,1,2,0:T(8,128)(2,1)}), bf16[16,8,1,2,80,128]{5,4,3,1,2,0:T(8,128)(2,1)}, u32[]{:S(2)}, u32[]{:S(2)}) async-start(bf16[16,8,1,2,80,128]{5,4,3,1,2,0:T(8,128)(2,1)} %select_select_fusion), calls=%async_computation | async-start | bytes 10485760 | tf_op jit(solution)/shard_map/all_to_all | solution.py:377
  30.9 3.4 %copy-start.5 = (s32[64]{0:T(128)S(1)}, s32[64]{0:T(128)}, u32[]{:S(2)}) copy-start(s32[64]{0:T(128)} %param.38) | copy-start | bytes 772
  30.9 4.0 %copy-start.12 = (bf16[2560]{0:T(1024)(128)(2,1)S(1)}, bf16[2560]{0:T(1024)(128)(2,1)}, u32[]{:S(2)}) copy-start(bf16[2560]{0:T(1024)(128)(2,1)} %param.22) | copy-start | bytes 15364
  31.0 4.0 %copy-start.6 = (s32[4]{0:T(128)S(1)}, s32[4]{0:T(128)}, u32[]{:S(2)}) copy-start(s32[4]{0:T(128)} %param.36) | copy-start | bytes 52
  31.0 192.8 %reduce-scatter.3.cloned.1.call-start = ((), (), s32[]{:S(2)}) async-start(), calls=%async_computation.4 | async-start | bytes 2949120 | tf_op jit(solution)/shard_map/reduce_scatter | solution.py:402
  35.6 3.8 %copy-start.7 = (bf16[128,4,2560]{2,1,0:T(4,128)(2,1)S(1)}, bf16[128,4,2560]{2,1,0:T(4,128)(2,1)}, u32[]{:S(2)}) copy-start(bf16[128,4,2560]{2,1,0:T(4,128)(2,1)} %param.21) | copy-start | bytes 7864324
  39.5 1.5 copy-start.14
  48.0 5.4 %copy-start.9 = (bf16[2560,80]{0,1:T(8,128)(2,1)S(1)}, bf16[2560,80]{0,1:T(8,128)(2,1)}, u32[]{:S(2)}) copy-start(bf16[2560,80]{0,1:T(8,128)(2,1)} %param.25) | copy-start | bytes 1228804
  53.4 3.3 %copy-start.10 = (s32[4,16]{1,0:T(4,128)S(1)}, s32[4,16]{1,0:T(4,128)}, u32[]{:S(2)}) copy-start(s32[4,16]{1,0:T(4,128)} %param.33) | copy-start | bytes 772
  53.4 3.8 %copy-start.11 = (s32[16,16]{1,0:T(8,128)S(1)}, s32[16,16]{1,0:T(8,128)}, u32[]{:S(2)}) copy-start(s32[16,16]{1,0:T(8,128)} %param.34) | copy-start | bytes 3076
  53.4 5.7 %copy-start.15 = (bf16[2560,80]{0,1:T(8,128)(2,1)S(1)}, bf16[2560,80]{0,1:T(8,128)(2,1)}, u32[]{:S(2)}) copy-start(bf16[2560,80]{0,1:T(8,128)(2,1)} %param.24) | copy-start | bytes 1228804
  186.9 0.7 copy-start.13
  186.9 66.3 %all-gather.5.cloned.1.call-start = ((), (), s32[]{:S(2)}) async-start(), calls=%async_computation.5 | async-start | bytes 2949120 | tf_op jit(solution)/shard_map/all_gather | solution.py:414
  228.3 78.8 %reduce-scatter.5.cloned.1.call-start = ((), (), s32[]{:S(2)}) async-start(), calls=%async_computation.6 | async-start | bytes 2949120 | tf_op jit(solution)/shard_map/reduce_scatter | solution.py:419
Sparse Core Ops, SparseCore 0:
  9.5 148.6 all-gather.2
  187.1 36.6 reduce-scatter.2
  228.4 24.8 all-gather.4
  271.9 35.1 reduce-scatter.4

commit v15 on v9

--- a/solution.py
+++ b/solution.py
@@ -76,7 +76,7 @@
 ROOT_PAGES = 16
 MID_PAGES = 16
 LEAF_SLOTS = 8
-CHUNK_PAGES = 4
+CHUNK_PAGES = 8
 
 
 def part_body(chunk0, with_fresh, tbl, meta, q_ref, store_hbm, kv, sc, top, mass, acc, sem, begin, finish):

time: 325 us -> 323 us (level)
  no operation moved by 1% of the time
where the time goes in v15:
time: 323 us; the launch traced here: 322 us
  waiting for transfers between devices  145 us (45%)
  blocking collectives  36.8 us (11%)
  Pallas kernels  32.7 us (10%)
  other arithmetic  28.3 us (9%)
  matrix products  28 us (9%)
  local copies, waits for them, and re-layouts  24.8 us (8%)
  between operations  13.8 us (4%)
  starting transfers between devices  12.9 us (4%)
    all_to_all x1, waiting for transfers between devices, shards(): lax.all_to_all(outgoing, 'seq', split_axis=0, concat_axis=0, tiled=True)  64.4 us
    all_to_all x1, blocking collectives, tp_row_sum(): arrived = lax.all_to_all(blocks, 'tp', 0, 0, tiled=True)  36.8 us
    all_to_all x1, waiting for transfers between devices, tp_row_sum(): arrived = lax.all_to_all(blocks, 'tp', 0, 0, tiled=True)  32.7 us
    pallas_call x2, Pallas kernels, part_call(): pl.pallas_call(kernel, grid_spec=grid_spec, out_shape=out_shapes, compile...  32.7 us
    all_gather x1, waiting for transfers between devices, shards(): normed_ffn = lax.all_gather(normed_own, 'tp', axis=0, tiled=True)  27.2 us
    all_gather x1, waiting for transfers between devices, shards(): page_store = lax.all_gather(shared_pages, 'seq', axis=0, tiled=True)  19.7 us
    dot_general x1, matrix products, shards(): jnp.dot(activated, w_down, preferred_element_type=jnp.float32)  11.7 us
    all_to_all x1, starting transfers between devices, shards(): lax.all_to_all(outgoing, 'seq', split_axis=0, concat_axis=0, tiled=True)  8.33 us
  transfers between devices with their start and end apart: 4, of which 4 were waited for; matrix products, arithmetic and copies ran while one was open for 15% of the time, Pallas kernels for 3%

profile of v15, /device:TPU:0, one launch (start us, length us, event | category | flops | bytes accessed | tf_op | source)
XLA Modules:
  0.0 322.0 jit_solution(13254866159796928234)
XLA Ops:
  8.8 0.8 copy.95
  10.3 0.8 gather_fusion.9
  13.6 3.5 %gather_fusion.11 = bf16[128,2,80,128]{3,2,1,0:T(8,128)(2,1)} fusion(bf16[32,2,80,128]{3,2,1,0:T(8,128)(2,1)S(1)} %bitcast.87, s32[1024]{0:T(1024)S(1)} %pad_clamp_fusion), kind=kCustom, calls=%fused_computation.11 | custom fusion | bytes 10486272 | tf_op jit(solution)/shard_map/jit(_take)/gather | solution.py:383
  17.1 5.5 %select_select_fusion = bf16[16,8,1,2,80,128]{5,4,3,1,2,0:T(8,128)(2,1)} fusion(bf16[16,8,1,2,80,128]{5,4,3,1,2,0:T(8,128)(2,1)} %bitcast.86, pred[16]{0:T(512)(128)(4,1)S(1)} %reduce_or.9, pred[16,8]{1,0:T(8,128)(4,1)S(1)} %get-tuple-element.13), kind=kLoop, calls=%fused_computation.20 | loop fusion | flops 5242880 | bytes 10485904 | tf_op jit(solution)/shard_map/jit(_where)/select_n | solution.py:382
  22.6 8.3 %all-to-all-start = ((bf16[16,8,1,2,80,128]{5,4,3,1,2,0:T(8,128)(2,1)}), bf16[16,8,1,2,80,128]{5,4,3,1,2,0:T(8,128)(2,1)}, u32[]{:S(2)}, u32[]{:S(2)}) async-start(bf16[16,8,1,2,80,128]{5,4,3,1,2,0:T(8,128)(2,1)} %select_select_fusion), calls=%async_computation | async-start | bytes 10485760 | tf_op jit(solution)/shard_map/all_to_all | solution.py:385
  35.7 3.3 %fusion = f32[128,4]{1,0:T(8,128)S(1)} fusion(bf16[128,4,2560]{2,1,0:T(4,128)(2,1)} %param.21), kind=kLoop, calls=%fused_computation.15 | loop fusion | flops 3931648 | bytes 2623488 | tf_op jit(solution)/shard_map/reduce_sum | solution.py:20
  39.4 1.5 fusion.39
  40.9 1.1 fusion.3
  42.2 1.0 copy.91
  43.2 4.8 %fusion.2 = bf16[128,4,2560]{2,1,0:T(4,128)(2,1)} fusion(bf16[128,4,2560]{2,1,0:T(4,128)(2,1)} %param.21, f32[2560]{0:T(1024)S(1)} %convert_element_type.55, f32[128,4]{1,0:T(8,128)S(1)} %add_rsqrt_fusion), kind=kLoop, calls=%fused_computation.17 | loop fusion | flops 5242880 | bytes 5255168 | tf_op jit(solution)/shard_map/convert_element_type | solution.py:21
  48.0 5.3 %reshape.333 = bf16[512,2560]{1,0:T(8,128)(2,1)} reshape(bf16[128,4,2560]{2,1,0:T(4,128)(2,1)} %fusion.2) | data formatting | bytes 5242880 | tf_op jit(solution)/shard_map/reshape | solution.py:354
  53.3 2.7 convolution_convert_fusion.2
  59.0 2.7 fusion.7
  63.5 64.4 %all-to-all-done = bf16[16,8,1,2,80,128]{5,4,3,1,2,0:T(8,128)(2,1)} async-done(((bf16[16,8,1,2,80,128]{5,4,3,1,2,0:T(8,128)(2,1)}), bf16[16,8,1,2,80,128]{5,4,3,1,2,0:T(8,128)(2,1)}, u32[]{:S(2)}, u32[]{:S(2)}) %all-to-all-start) | async-done | bytes 5242912 | tf_op jit(solution)/shard_map/all_to_all | solution.py:385
  127.9 10.6 %shard_map.199 = (f32[4,512,80]{2,1,0:T(8,128)}, f32[4,512,128]{2,1,0:T(8,128)}, f32[4,512,128]{2,1,0:T(8,128)}) custom-call(s32[4,8]{1,0:T(4,128)} %iota_add_fusion.tbl, s32[4,4]{1,0:T(4,128)} %pad_add_fusion.1.meta, bf16[4,512,80]{2,1,0:T(8,128)(2,1)} %bitcast.89, bf16[4,2,80,128]{3,2,1,0:T(8,128)(2,1)} %pad_maximum_fusion.fresh_ref, ...), custom_call_target="tpu_custom_call" | custom-call | flops 671088640 | bytes 1310720 | tf_op jit(solution)/shard_map/pallas_call | solution.py:268
  138.5 19.7 %all-gather.3.cloned.1.call-done = bf16[320,1,2,80,128]{4,3,2,1,0:T(8,128)(2,1)} async-done(((bf16[20,1,2,80,128]{4,3,2,1,0:T(8,128)(2,1)}), bf16[320,1,2,80,128]{4,3,2,1,0:T(8,128)(2,1)}) %all-gather.3.cloned.1.call-update) | async-done | bytes 13107216 | tf_op jit(solution)/shard_map/all_gather | solution.py:351
  158.2 22.1 %shard_map.200 = bf16[4,512,80]{2,1,0:T(8,128)(2,1)} custom-call(s32[4,32]{1,0:T(4,128)} %pad_add_fusion.tbl, s32[4,4]{1,0:T(4,128)} %pad_add_fusion.1.meta, bf16[4,512,80]{2,1,0:T(8,128)(2,1)} %bitcast.90, f32[4,512,80]{2,1,0:T(8,128)} %get-tuple-element.10.acc_in, f32[4,512,128]{2,1,0:T(8,128)} %get-tuple-element.11.top_in, ...), custom_call_target="tpu_custom_call" | custom-call | flops 2684354560 | bytes 5242880 | tf_op jit(solution)/shard_map/pallas_call | solution.py:268
  180.3 1.4 copy.110
  182.1 3.0 convolution_convert_fusion.1
  185.2 4.5 %all-to-all-start.1 = ((bf16[8,64,2560]{2,1,0:T(8,128)(2,1)}), bf16[8,64,2560]{2,1,0:T(8,128)(2,1)}, u32[]{:S(2)}, u32[]{:S(2)}) async-start(bf16[8,64,2560]{2,1,0:T(8,128)(2,1)} %bitcast.91), calls=%async_computation.1 | async-start | bytes 5242880 | tf_op jit(solution)/shard_map/all_to_all | solution.py:303
  189.8 32.7 %all-to-all-done.1 = bf16[8,64,2560]{2,1,0:T(8,128)(2,1)} async-done(((bf16[8,64,2560]{2,1,0:T(8,128)(2,1)}), bf16[8,64,2560]{2,1,0:T(8,128)(2,1)}, u32[]{:S(2)}, u32[]{:S(2)}) %all-to-all-start.1) | async-done | bytes 2621472 | tf_op jit(solution)/shard_map/all_to_all | solution.py:303
  222.5 2.2 convert_reduce_fusion.1
  224.9 1.3 multiply_reduce_fusion
  226.2 1.2 multiply_convert_fusion.1
  227.4 0.8 reshape.343
  228.2 27.2 %all-gather.5.cloned.1.call-done = bf16[512,2560]{1,0:T(8,128)(2,1)} async-done(((bf16[64,2560]{1,0:T(8,128)(2,1)}), bf16[512,2560]{1,0:T(8,128)(2,1)}) %all-gather.5.cloned.1.call-update) | async-done | bytes 2621456 | tf_op jit(solution)/shard_map/all_gather | solution.py:415
  255.4 6.8 %fusion.28 = f32[512,864]{0,1:T(8,128)} fusion(bf16[512,2560]{1,0:T(8,128)(2,1)} %all-gather.5.cloned.1.call-done, bf16[2560,864]{0,1:T(8,128)(2,1)} %param.28), kind=kOutput, calls=%fused_computation.100 | convolution fusion | flops 2264924160 | bytes 8814592 | tf_op jit(solution)/shard_map/dot_general | solution.py:416
  262.2 11.7 %convolution_convert_fusion = bf16[512,2560]{1,0:T(8,128)(2,1)} fusion(bf16[864,2560]{1,0:T(8,128)(2,1)} %param.30, f32[512,864]{0,1:T(8,128)} %fusion.28, bf16[512,2560]{1,0:T(8,128)(2,1)} %all-gather.5.cloned.1.call-done, bf16[2560,864]{0,1:T(8,128)(2,1)} %param.29), kind=kOutput, calls=%fused_computation.21 | convolution fusion | flops 4533813248 | bytes 15859712 | tf_op jit(solution)/shard_map/dot_general | solution.py:419
  273.9 36.8 %all_to_all.15 = bf16[8,64,2560]{2,1,0:T(8,128)(2,1)S(1)} all-to-all(bf16[8,64,2560]{2,1,0:T(8,128)(2,1)} %bitcast.92), channel_id=1, replica_groups=mesh['seq'=16,'tp'=8] {'tp'}, dimensions={0} | all-to-all | bytes 5242880 | tf_op jit(solution)/shard_map/all_to_all | solution.py:303
  310.7 1.2 convert_reduce_fusion
  311.8 1.3 reshape.345
  313.1 2.0 fusion.21
  (104 shorter events, 16.0 us)
Async XLA Ops:
  6.5 175.6 %copy-start = (bf16[320,2560]{1,0:T(8,128)(2,1)S(1)}, bf16[320,2560]{1,0:T(8,128)(2,1)}, u32[]{:S(2)}) copy-start(bf16[320,2560]{1,0:T(8,128)(2,1)} %param.26) | copy-start | bytes 4915204
  6.5 151.6 %all-gather.3.cloned.1.call-start = ((), (), s32[]{:S(2)}) async-start(), calls=%async_computation.3 | async-start | bytes 13926400 | tf_op jit(solution)/shard_map/all_gather | solution.py:351
  10.3 3.3 %copy-start.9 = (bf16[32,1,2,80,128]{4,3,2,1,0:T(8,128)(2,1)S(1)}, bf16[32,1,2,80,128]{4,3,2,1,0:T(8,128)(2,1)}, u32[]{:S(2)}) copy-start(bf16[32,1,2,80,128]{4,3,2,1,0:T(8,128)(2,1)} %param.32) | copy-start | bytes 3932164
  22.6 8.4 %copy-start.2 = (s32[64]{0:T(128)S(1)}, s32[64]{0:T(128)}, u32[]{:S(2)}) copy-start(s32[64]{0:T(128)} %param.41) | copy-start | bytes 772
  22.6 9.7 %copy-start.3 = (s32[64]{0:T(128)S(1)}, s32[64]{0:T(128)}, u32[]{:S(2)}) copy-start(s32[64]{0:T(128)} %param.40) | copy-start | bytes 772
  22.6 10.4 %copy-start.4 = (s32[16]{0:T(128)S(1)}, s32[16]{0:T(128)}, u32[]{:S(2)}) copy-start(s32[16]{0:T(128)} %param.39) | copy-start | bytes 196
  22.6 11.0 %copy-start.5 = (s32[16]{0:T(128)S(1)}, s32[16]{0:T(128)}, u32[]{:S(2)}) copy-start(s32[16]{0:T(128)} %param.37) | copy-start | bytes 196
  22.6 105.3 %all-to-all-start = ((bf16[16,8,1,2,80,128]{5,4,3,1,2,0:T(8,128)(2,1)}), bf16[16,8,1,2,80,128]{5,4,3,1,2,0:T(8,128)(2,1)}, u32[]{:S(2)}, u32[]{:S(2)}) async-start(bf16[16,8,1,2,80,128]{5,4,3,1,2,0:T(8,128)(2,1)} %select_select_fusion), calls=%async_computation | async-start | bytes 10485760 | tf_op jit(solution)/shard_map/all_to_all | solution.py:385
  30.9 3.3 %copy-start.6 = (s32[64]{0:T(128)S(1)}, s32[64]{0:T(128)}, u32[]{:S(2)}) copy-start(s32[64]{0:T(128)} %param.38) | copy-start | bytes 772
  31.0 4.0 %copy-start.13 = (bf16[2560]{0:T(1024)(128)(2,1)S(1)}, bf16[2560]{0:T(1024)(128)(2,1)}, u32[]{:S(2)}) copy-start(bf16[2560]{0:T(1024)(128)(2,1)} %param.22) | copy-start | bytes 15364
  31.0 4.0 %copy-start.7 = (s32[4]{0:T(128)S(1)}, s32[4]{0:T(128)}, u32[]{:S(2)}) copy-start(s32[4]{0:T(128)} %param.36) | copy-start | bytes 52
  35.6 3.8 %copy-start.8 = (bf16[128,4,2560]{2,1,0:T(4,128)(2,1)S(1)}, bf16[128,4,2560]{2,1,0:T(4,128)(2,1)}, u32[]{:S(2)}) copy-start(bf16[128,4,2560]{2,1,0:T(4,128)(2,1)} %param.21) | copy-start | bytes 7864324
  39.4 1.5 copy-start.15
  48.0 5.4 %copy-start.10 = (bf16[2560,80]{0,1:T(8,128)(2,1)S(1)}, bf16[2560,80]{0,1:T(8,128)(2,1)}, u32[]{:S(2)}) copy-start(bf16[2560,80]{0,1:T(8,128)(2,1)} %param.25) | copy-start | bytes 1228804
  53.3 3.3 %copy-start.11 = (s32[4,16]{1,0:T(4,128)S(1)}, s32[4,16]{1,0:T(4,128)}, u32[]{:S(2)}) copy-start(s32[4,16]{1,0:T(4,128)} %param.33) | copy-start | bytes 772
  53.3 3.8 %copy-start.12 = (s32[16,16]{1,0:T(8,128)S(1)}, s32[16,16]{1,0:T(8,128)}, u32[]{:S(2)}) copy-start(s32[16,16]{1,0:T(8,128)} %param.34) | copy-start | bytes 3076
  53.3 5.7 %copy-start.16 = (bf16[2560,80]{0,1:T(8,128)(2,1)S(1)}, bf16[2560,80]{0,1:T(8,128)(2,1)}, u32[]{:S(2)}) copy-start(bf16[2560,80]{0,1:T(8,128)(2,1)} %param.24) | copy-start | bytes 1228804
  185.2 4.6 %copy-start.14 = (bf16[2560]{0:T(1024)(128)(2,1)S(1)}, bf16[2560]{0:T(1024)(128)(2,1)}, u32[]{:S(2)}) copy-start(bf16[2560]{0:T(1024)(128)(2,1)} %param.27) | copy-start | bytes 15364
  185.2 37.4 %all-to-all-start.1 = ((bf16[8,64,2560]{2,1,0:T(8,128)(2,1)}), bf16[8,64,2560]{2,1,0:T(8,128)(2,1)}, u32[]{:S(2)}, u32[]{:S(2)}) async-start(bf16[8,64,2560]{2,1,0:T(8,128)(2,1)} %bitcast.91), calls=%async_computation.1 | async-start | bytes 5242880 | tf_op jit(solution)/shard_map/all_to_all | solution.py:303
  189.7 65.7 %all-gather.5.cloned.1.call-start = ((), (), s32[]{:S(2)}) async-start(), calls=%async_computation.4 | async-start | bytes 2949120 | tf_op jit(solution)/shard_map/all_gather | solution.py:415
  310.6 4.5 %copy-start.1 = (bf16[320,2560]{1,0:T(8,128)(2,1)S(1)}, bf16[320,2560]{1,0:T(8,128)(2,1)}, u32[]{:S(2)}) copy-start(bf16[320,2560]{1,0:T(8,128)(2,1)} %param.26) | copy-start | bytes 4915204
Sparse Core Ops, SparseCore 0:
  9.5 148.6 all-gather.2
  228.4 27.0 all-gather.4
